TPU v7x, 128 devices: a whole 4x4x4 slice. The times are simulated.
128 devices in a mesh: sta: 32 (over y, x, z_hi), tm: 4 (over z_lo, core).
Axes of the slice: x: 4, y: 4, z: 4 (z_hi: 2, z_lo: 2; z = z_hi * 2 + z_lo), core: 2. Of those that a mesh axis runs over, the one named last changes fastest.
Arguments:
- spectra: bfloat16 [8, 4096, 2, 4096], P('tm', None, None, 'sta')
- src_ids: int32 [3, 8], replicated, may hold values from 0 to 4095, as said below
Outputs:
- correlations: float32 [3, 256, 8, 4096], P(None, 'tm', None, 'sta')
Inputs may be any that keep to these rules, and one draw needn't show every extreme that they name: `src_ids`: the 8 ids of a round are distinct and all lie in one block of 128 consecutive stations that starts at a multiple of 128.
All inputs are finite; a program needn't handle non-finite values.
Results may differ from a plain program's by a relative error of at most 0.0056.
Values may be sent and summed in bfloat16 or wider, within the bound.
No kernel may reach another device: no remote copies, remote signals or barrier semaphores. Data moves between devices by JAX's collectives and lax.ppermute only.
A program may use at most 128 MiB of HBM per device.

v0:
```python
import math

import jax
import jax.numpy as jnp
from jax import lax
from jax.experimental import pallas as pl
from jax.experimental.pallas import tpu as pltpu
from jax.sharding import PartitionSpec as P

BINS = 4096
BLOCK = 64
LAGS = 256
NSRC = 8
ROUNDS = 3

CHUNK = 256
ROWS = 16

EPSILON = 1e-05


def block_sums(spec):
    values = spec.astype(jnp.float32)
    magnitude = jnp.sqrt(
        values[..., 0, :] * values[..., 0, :] + values[..., 1, :] * values[..., 1, :]
    )
    full_shape = magnitude.shape
    return magnitude.reshape(full_shape[:-1] + (full_shape[-1] // BLOCK, BLOCK)).sum(axis=-1)


def level_divide(spec, padded):
    block_num = padded.shape[-1] - 2
    level_mean = (padded[..., :-2] + padded[..., 1:-1] + padded[..., 2:]) / (3.0 * BLOCK)
    full_shape = spec.shape
    grid_view = spec.astype(jnp.float32).reshape(full_shape[:-1] + (block_num, BLOCK))
    whitened = grid_view / (level_mean[..., None, :, None] + EPSILON)
    return whitened.reshape(full_shape).astype(jnp.bfloat16)


def make_table(total_hours):
    lag_index = lax.iota(jnp.int32, LAGS) - LAGS // 2
    freq_index = lax.iota(jnp.int32, BINS)
    phase_int = jnp.remainder(lag_index[:, None] * freq_index[None, :], 2 * BINS)
    angle_rad = 2.0 * math.pi / (2 * BINS) * phase_int.astype(jnp.float32)
    norm_scale = 1.0 / math.sqrt(BINS * total_hours)
    return jnp.concatenate(
        [jnp.cos(angle_rad) * norm_scale, -jnp.sin(angle_rad) * norm_scale], axis=1
    ).astype(jnp.bfloat16)


def cross_project_kernel(x_ref, y_ref, tre_ref, tim_ref, out_ref, yb_ref, cre_ref, cim_ref):
    step = pl.program_id(0)
    hours = x_ref.shape[0]
    stations = x_ref.shape[2]
    count_src = y_ref.shape[2]
    width = x_ref.shape[3]

    @pl.when(step == 0)
    def _():
        out_ref[...] = jnp.zeros_like(out_ref)

    for h in range(hours):
        for p in range(2):
            for k in range(count_src):
                row = y_ref[h, p, pl.ds(k, 1), :].astype(jnp.float32)
                yb_ref[h, p, k] = jnp.broadcast_to(row, (ROWS, width))

    def body(r, carry):
        first = pl.multiple_of(r * ROWS, ROWS)
        xs = [
            [x_ref[h, p, pl.ds(first, ROWS), :].astype(jnp.float32) for p in range(2)]
            for h in range(hours)
        ]
        for k in range(count_src):
            real = None
            imag = None
            for h in range(hours):
                y0 = yb_ref[h, 0, k]
                y1 = yb_ref[h, 1, k]
                x0, x1 = xs[h]
                re_h = y0 * x0 + y1 * x1
                im_h = y1 * x0 - y0 * x1
                real = re_h if real is None else real + re_h
                imag = im_h if imag is None else imag + im_h
            dest = pl.ds(k * stations + first, ROWS)
            cre_ref[dest, :] = real.astype(jnp.bfloat16)
            cim_ref[dest, :] = imag.astype(jnp.bfloat16)
        return carry

    lax.fori_loop(0, stations // ROWS, body, 0)
    dims = (((1,), (1,)), ((), ()))
    out_ref[...] += lax.dot_general(
        tre_ref[...], cre_ref[...], dims, preferred_element_type=jnp.float32
    ) + lax.dot_general(tim_ref[...], cim_ref[...], dims, preferred_element_type=jnp.float32)


def cross_project(receivers, sources, transform):
    hours, _, stations, bins = receivers.shape
    count_src = sources.shape[2]
    lags = transform.shape[0]
    steps = bins // CHUNK
    return pl.pallas_call(
        cross_project_kernel,
        grid=(steps,),
        in_specs=[
            pl.BlockSpec((hours, 2, stations, CHUNK), lambda j: (0, 0, 0, j)),
            pl.BlockSpec((hours, 2, count_src, CHUNK), lambda j: (0, 0, 0, j)),
            pl.BlockSpec((lags, CHUNK), lambda j: (0, j)),
            pl.BlockSpec((lags, CHUNK), lambda j: (0, j + steps)),
        ],
        out_specs=pl.BlockSpec((lags, count_src * stations), lambda j: (0, 0)),
        out_shape=jax.ShapeDtypeStruct((lags, count_src * stations), jnp.float32),
        scratch_shapes=[
            pltpu.VMEM((hours, 2, count_src, ROWS, CHUNK), jnp.float32),
            pltpu.VMEM((count_src * stations, CHUNK), jnp.bfloat16),
            pltpu.VMEM((count_src * stations, CHUNK), jnp.bfloat16),
        ],
        compiler_params=pltpu.CompilerParams(dimension_semantics=("arbitrary",)),
    )(receivers, sources, transform, transform)


def local(spectra, src_ids):
    flat_ids = src_ids.reshape(-1)
    src_raw = jnp.take(spectra, flat_ids, axis=1)
    src_all = lax.all_gather(src_raw, "sta", axis=3, tiled=True)
    arrived = lax.all_to_all(spectra, "sta", split_axis=1, concat_axis=3, tiled=True)
    stations_dev = arrived.shape[1]
    joined = jnp.concatenate([arrived, src_all], axis=1)
    totals = block_sums(joined)
    white = level_divide(joined, jnp.pad(totals, ((0, 0), (0, 0), (1, 1))))
    white = jnp.transpose(white, (0, 2, 1, 3))
    by_station = white[:, :, :stations_dev]
    src_white = white[:, :, stations_dev:]
    hours_dev = by_station.shape[0]
    transform = make_table(hours_dev * lax.axis_size("tm"))
    row_count = transform.shape[0] // lax.axis_size("tm")
    results = []
    for step_no in range(ROUNDS):
        sources = src_white[:, :, step_no * NSRC:(step_no + 1) * NSRC]
        projected = cross_project(by_station, sources, transform)
        stacked = lax.psum_scatter(projected, "tm", scatter_dimension=0, tiled=True)
        results.append(stacked.reshape(row_count, NSRC, stations_dev))
    return jnp.stack(results)


def solution(mesh):
    return jax.shard_map(
        local,
        mesh=mesh,
        in_specs=(P("tm", None, None, "sta"), P()),
        out_specs=P(None, "tm", None, "sta"),
        check_vma=False,
    )
```

profile of v0, /device:TPU:1, one launch (start us, length us, event | category | flops | bytes accessed | tf_op | source)
XLA Modules:
  0.0 340.2 jit_solution(1783392149644888150)
XLA Ops:
  6.5 7.7 %copy.6 = bf16[2,4096,2,128]{3,2,0,1:T(2,128)(2,1)} copy(bf16[2,4096,2,128]{3,2,1,0:T(2,128)(2,1)} %param.2) | data formatting | bytes 8388608 | tf_op args[0]
  14.3 11.4 %all-to-all-start = ((bf16[2,4096,2,128]{3,2,0,1:T(2,128)(2,1)}), bf16[2,4096,2,128]{3,2,0,1:T(2,128)(2,1)}, u32[]{:S(2)}, u32[]{:S(2)}) async-start(bf16[2,4096,2,128]{3,2,0,1:T(2,128)(2,1)} %copy.6), calls=%async_computation | async-start | bytes 8388608 | tf_op jit(solution)/shard_map/all_to_all | solution.py:126
  25.7 0.0 reduce-scatter.4.cloned.1.call-start
  25.8 0.1 reshape.63
  25.9 0.1 reshape.62
  26.0 2.8 gather_fusion
  28.8 0.1 fusion.9
  28.9 125.6 %all_gather.3 = bf16[2,24,2,4096]{3,1,2,0:T(8,128)(2,1)S(1)} all-gather(bf16[2,24,2,128]{3,1,2,0:T(8,128)(2,1)S(1)} %fusion.9), channel_id=1, replica_groups=mesh['sta'=32,'tm'=4] {'sta'}, dimensions={3}, use_global_device_ids=true | all-gather | bytes 811008 | tf_op jit(solution)/shard_map/all_gather | solution.py:125
  154.5 18.2 %multiply_convert_fusion.1 = (bf16[256,4096]{1,0:T(8,128)(2,1)S(1)}, bf16[256,4096]{1,0:T(8,128)(2,1)S(1)}) fusion(s32[256]{0:T(256)S(1)} %iota_add_fusion), kind=kLoop, calls=%fused_computation.17 | loop fusion | flops 19922944 | bytes 4195328 | tf_op jit(solution)/shard_map/convert
  172.6 2.4 pad_maximum_fusion.tre_ref.tim_ref
  175.0 6.9 %copy.16 = bf16[2,32,128,2,128]{4,1,2,3,0:T(8,128)(2,1)} copy(bf16[2,32,128,2,128]{4,3,0,2,1:T(2,128)(2,1)} %bitcast) | data formatting | bytes 8388608 | tf_op jit(solution)/shard_map/all_to_all | solution.py:126
  181.9 7.3 %concatenate.11 = bf16[2,128,2,4096]{3,1,2,0:T(8,128)(2,1)} reshape(bf16[2,128,2,32,128]{4,3,1,2,0:T(8,128)(2,1)} %bitcast.29) | data formatting | bytes 8388608 | tf_op jit(solution)/shard_map/concatenate | solution.py:128
  189.2 3.5 %maximum_convert_fusion = f32[2,152,2,4096]{3,1,2,0:T(8,128)S(1)} fusion(bf16[2,24,2,4096]{3,1,2,0:T(8,128)(2,1)S(1)} %all_gather.3, bf16[2,128,2,4096]{3,1,2,0:T(8,128)(2,1)} %concatenate.11), kind=kLoop, calls=%fused_computation.9 | loop fusion | flops 9961472 | bytes 14942208 | tf_op jit(solution)/shard_map/convert_element_type | solution.py:35
  192.7 3.9 %fusion.1 = f32[2,152,1,4096]{3,1,2,0:T(8,128)} fusion(f32[2,152,2,4096]{3,1,2,0:T(8,128)S(1)} %maximum_convert_fusion), kind=kLoop, calls=%fused_computation.7 | loop fusion | flops 3735552 | bytes 14942208 | tf_op jit(solution)/shard_map/sqrt | solution.py:24
  196.6 8.7 %sqrt.12 = f32[2,152,64,64]{3,2,1,0:T(8,128)} reshape(f32[2,152,1,4096]{3,1,2,0:T(8,128)} %fusion.1) | data formatting | bytes 9961472 | tf_op jit(solution)/shard_map/sqrt | solution.py:24
  205.4 6.5 %reduce_sum.9 = f32[2,152,64]{2,1,0:T(8,128)S(1)} reduce(f32[2,152,64,64]{3,2,1,0:T(8,128)} %sqrt.12, f32[]{:T(128)} %constant.38.clone.1), dimensions={3}, to_apply=%region_0.1 | reduce | flops 1225728 | bytes 5058564 | tf_op jit(solution)/shard_map/reduce_sum | solution.py:28
  211.9 0.2 multiply_add_fusion
  212.0 6.0 %div.21 = f32[2,152,64,64]{3,2,1,0:T(8,128)} broadcast(f32[2,152,64]{2,1,0:T(8,128)S(1)} %multiply_add_fusion), dimensions={0,1,2} | broadcast | bytes 5058560 | tf_op jit(solution)/shard_map/div | solution.py:36
  218.0 9.2 %div.22 = f32[2,152,4096]{2,1,0:T(8,128)} reshape(f32[2,152,64,64]{3,2,1,0:T(8,128)} %div.21) | data formatting | bytes 9961472 | tf_op jit(solution)/shard_map/div | solution.py:36
  227.2 4.6 %fusion.2 = bf16[2,2,152,4096]{3,2,1,0:T(8,128)(2,1)S(1)} fusion(f32[2,152,4096]{2,1,0:T(8,128)} %div.22, bf16[2,24,2,4096]{3,1,2,0:T(8,128)(2,1)S(1)} %all_gather.3, bf16[2,128,2,4096]{3,1,2,0:T(8,128)(2,1)} %concatenate.11), kind=kLoop, calls=%fused_computation.10 | loop fusion | flops 14942208 | bytes 14942208 | tf_op jit(solution)/shard_map/transpose | solution.py:131
  231.8 2.2 slice.43.x_ref
  234.0 0.9 fusion.11
  234.9 19.9 %shard_map.28 = f32[256,1024]{1,0:T(8,128)} custom-call(bf16[2,2,128,4096]{3,2,1,0:T(8,128)(2,1)} %slice.43.x_ref, bf16[2,2,8,4096]{3,2,1,0:T(8,128)(2,1)} %get-tuple-element.5.y_ref, bf16[256,8192]{1,0:T(8,128)(2,1)} %pad_maximum_fusion.tre_ref.tim_ref, bf16[256,8192]{1,0:T(8,128)(2,1)} %pad_maximum_fusion.tre_ref.tim_ref), custom_call_target="tpu_custom_call" | custom-call | tf_op jit(solution)/shard_map/pallas_call | solution.py:102
  254.8 19.9 %shard_map.29 = f32[256,1024]{1,0:T(8,128)} custom-call(bf16[2,2,128,4096]{3,2,1,0:T(8,128)(2,1)} %slice.43.x_ref, bf16[2,2,8,4096]{3,2,1,0:T(8,128)(2,1)} %get-tuple-element.7.y_ref, bf16[256,8192]{1,0:T(8,128)(2,1)} %pad_maximum_fusion.tre_ref.tim_ref, bf16[256,8192]{1,0:T(8,128)(2,1)} %pad_maximum_fusion.tre_ref.tim_ref), custom_call_target="tpu_custom_call" | custom-call | tf_op jit(solution)/shard_map/pallas_call | solution.py:102
  274.8 0.0 reduce-scatter.8.cloned.1.call-start
  274.8 19.9 %shard_map.30 = f32[256,1024]{1,0:T(8,128)} custom-call(bf16[2,2,128,4096]{3,2,1,0:T(8,128)(2,1)} %slice.43.x_ref, bf16[2,2,8,4096]{3,2,1,0:T(8,128)(2,1)} %get-tuple-element.6.y_ref, bf16[256,8192]{1,0:T(8,128)(2,1)} %pad_maximum_fusion.tre_ref.tim_ref, bf16[256,8192]{1,0:T(8,128)(2,1)} %pad_maximum_fusion.tre_ref.tim_ref), custom_call_target="tpu_custom_call" | custom-call | tf_op jit(solution)/shard_map/pallas_call | solution.py:102
  294.8 1.0 copy.9
  295.8 12.2 %reduce-scatter.6.cloned.1.call-done = f32[64,1024]{1,0:T(8,128)} async-done(((f32[256,1024]{1,0:T(8,128)}), f32[64,1024]{1,0:T(8,128)}) %reduce-scatter.6.cloned.1.call-update) | async-done | bytes 262160 | tf_op jit(solution)/shard_map/reduce_scatter | solution.py:141
  308.0 1.0 copy.10
  309.0 22.8 %reduce-scatter.8.cloned.1.call-done = f32[64,1024]{1,0:T(8,128)} async-done(((f32[256,1024]{1,0:T(8,128)}), f32[64,1024]{1,0:T(8,128)}) %reduce-scatter.8.cloned.1.call-update) | async-done | bytes 262160 | tf_op jit(solution)/shard_map/reduce_scatter | solution.py:141
  331.8 1.0 copy.11
  332.8 1.0 pad_maximum_fusion.1
  (12 shorter events, 0.1 us)
Async XLA Ops:
  14.3 11.5 %copy-start = (s32[3,8]{1,0:T(4,128)S(1)}, s32[3,8]{1,0:T(4,128)}, u32[]{:S(2)}) copy-start(s32[3,8]{1,0:T(4,128)} %param.3) | copy-start | bytes 292
  14.3 160.8 %all-to-all-start = ((bf16[2,4096,2,128]{3,2,0,1:T(2,128)(2,1)}), bf16[2,4096,2,128]{3,2,0,1:T(2,128)(2,1)}, u32[]{:S(2)}, u32[]{:S(2)}) async-start(bf16[2,4096,2,128]{3,2,0,1:T(2,128)(2,1)} %copy.6), calls=%async_computation | async-start | bytes 8388608 | tf_op jit(solution)/shard_map/all_to_all | solution.py:126
  25.7 269.1 %reduce-scatter.4.cloned.1.call-start = ((), (), s32[]{:S(2)}) async-start(), calls=%async_computation.4 | async-start | bytes 1310720 | tf_op jit(solution)/shard_map/reduce_scatter | solution.py:141
  254.8 53.2 %reduce-scatter.6.cloned.1.call-start = ((), (), s32[]{:S(2)}) async-start(), calls=%async_computation.5 | async-start | bytes 1310720 | tf_op jit(solution)/shard_map/reduce_scatter | solution.py:141
  274.8 57.0 %reduce-scatter.8.cloned.1.call-start = ((), (), s32[]{:S(2)}) async-start(), calls=%async_computation.6 | async-start | bytes 1310720 | tf_op jit(solution)/shard_map/reduce_scatter | solution.py:141
Sparse Core Ops, SparseCore 0:
  254.9 29.2 reduce-scatter.3
  286.6 21.3 reduce-scatter.5
  310.4 21.3 reduce-scatter.7
where the time goes:
time: 342 us; the launch traced here: 340 us
  blocking collectives  126 us (37%)
  Pallas kernels  59.7 us (17%)
  local copies, waits for them, and re-layouts  54.9 us (16%)
  other arithmetic  40.3 us (12%)
  waiting for transfers between devices  35 us (10%)
  between operations  13.2 us (4%)
  starting transfers between devices  11.6 us (3%)
    all_gather x1, blocking collectives, local(): src_all = lax.all_gather(src_raw, 'sta', axis=3, tiled=True)  126 us
    pallas_call x3, Pallas kernels, cross_project(): pl.pallas_call(cross_project_kernel, grid=(steps,), in_specs=[pl.BlockSpe...  59.7 us
    reduce_scatter x3, waiting for transfers between devices, local(): stacked = lax.psum_scatter(projected, 'tm', scatter_dimension=0, tiled=True)  35 us
    another operation x1, other arithmetic  18.2 us
    div x2, local copies, waits for them, and re-layouts, level_divide(): whitened = grid_view / (level_mean[..., None, :, None] + EPSILON)  15.1 us
    all_to_all x1, starting transfers between devices, local(): lax.all_to_all(spectra, 'sta', split_axis=1, concat_axis=3, tiled=True)  11.4 us
    unnamed x6, local copies, waits for them, and re-layouts  10.7 us
    sqrt x1, local copies, waits for them, and re-layouts, block_sums(): jnp.sqrt(values[..., 0, :] * values[..., 0, :] + values[..., 1, :] * valu...  8.74 us
  transfers between devices with their start and end apart: 4, of which 2 were waited for; matrix products, arithmetic and copies ran while one was open for 8% of the time, Pallas kernels for 12%

commit v1 on v0

--- a/solution.py
+++ b/solution.py
@@ -94,8 +94,8 @@
     ) + lax.dot_general(tim_ref[...], cim_ref[...], dims, preferred_element_type=jnp.float32)
 
 
-def cross_project(receivers, sources, transform):
-    hours, _, stations, bins = receivers.shape
+def cross_project(receivers, sources, transform, stations):
+    hours, _, _, bins = receivers.shape
     count_src = sources.shape[2]
     lags = transform.shape[0]
     steps = bins // CHUNK
@@ -120,24 +120,38 @@
 
 
 def local(spectra, src_ids):
+    hours_dev, stations, _, bins_dev = spectra.shape
+    shards = lax.axis_size("sta")
+    stations_dev = stations // shards
     flat_ids = src_ids.reshape(-1)
-    src_raw = jnp.take(spectra, flat_ids, axis=1)
-    src_all = lax.all_gather(src_raw, "sta", axis=3, tiled=True)
-    arrived = lax.all_to_all(spectra, "sta", split_axis=1, concat_axis=3, tiled=True)
-    stations_dev = arrived.shape[1]
-    joined = jnp.concatenate([arrived, src_all], axis=1)
-    totals = block_sums(joined)
-    white = level_divide(joined, jnp.pad(totals, ((0, 0), (0, 0), (1, 1))))
-    white = jnp.transpose(white, (0, 2, 1, 3))
-    by_station = white[:, :, :stations_dev]
-    src_white = white[:, :, stations_dev:]
-    hours_dev = by_station.shape[0]
+    count_all = flat_ids.shape[0]
+    by_part = jnp.transpose(spectra, (0, 2, 1, 3))
+    src_raw = jnp.take(by_part, flat_ids, axis=2)
+    chunks = by_part.reshape(hours_dev, 2, shards, stations_dev, bins_dev)
+    src_copies = jnp.broadcast_to(
+        src_raw[:, :, None], (hours_dev, 2, shards, count_all, bins_dev)
+    )
+    send = jnp.concatenate([chunks, src_copies], axis=3).reshape(
+        hours_dev, 2, shards * (stations_dev + count_all), bins_dev
+    )
+    joined = lax.all_to_all(send, "sta", split_axis=2, concat_axis=3, tiled=True)
+    values = joined.astype(jnp.float32)
+    magnitude = jnp.sqrt(values[:, 0] * values[:, 0] + values[:, 1] * values[:, 1])
+    rows = magnitude.shape[1]
+    block_num = BINS // BLOCK
+    totals = magnitude.reshape(hours_dev, rows, block_num, BLOCK).sum(axis=-1)
+    padded = jnp.pad(totals, ((0, 0), (0, 0), (1, 1)))
+    level_mean = (padded[..., :-2] + padded[..., 1:-1] + padded[..., 2:]) / (3.0 * BLOCK)
+    grid_view = values.reshape(hours_dev, 2, rows, block_num, BLOCK)
+    white = (grid_view / (level_mean[:, None, :, :, None] + EPSILON)).reshape(values.shape)
+    white = white.astype(jnp.bfloat16)
     transform = make_table(hours_dev * lax.axis_size("tm"))
     row_count = transform.shape[0] // lax.axis_size("tm")
     results = []
     for step_no in range(ROUNDS):
-        sources = src_white[:, :, step_no * NSRC:(step_no + 1) * NSRC]
-        projected = cross_project(by_station, sources, transform)
+        first = stations_dev + step_no * NSRC
+        sources = white[:, :, first:first + NSRC]
+        projected = cross_project(white, sources, transform, stations_dev)
         stacked = lax.psum_scatter(projected, "tm", scatter_dimension=0, tiled=True)
         results.append(stacked.reshape(row_count, NSRC, stations_dev))
     return jnp.stack(results)

time: 342 us -> 258 us (0.75)
  blocking collectives: 126 us -> 0 us
  waiting for transfers between devices: 35 us -> 80 us
  local copies, waits for them, and re-layouts: 54.9 us -> 38.8 us
  other arithmetic: 40.3 us -> 53.2 us
    all_gather x1 -> x0, blocking collectives: 126 us -> none  [local(): src_all = lax.all_gather(src_raw, 'sta', axis=3, tiled=True)]
    all_to_all x1, waiting for transfers between devices: 0.01 us -> 51.2 us  [local(): lax.all_to_all(send, 'sta', split_axis=2, concat_axis=3, tiled=True)]
    concatenate x0 -> x1, other arithmetic: none -> 14.5 us  [local(): jnp.concatenate([chunks, src_copies], axis=3)]
    concatenate x1 -> x0, local copies, waits for them, and re-layouts: 7.3 us -> none  [local(): joined = jnp.concatenate([arrived, src_all], axis=1)]
    reduce_scatter x3, waiting for transfers between devices: 35 us -> 28.8 us  [local(): stacked = lax.psum_scatter(projected, 'tm', scatter_dimension=0, tiled=True)]
    transpose x1 -> x0, other arithmetic: 4.6 us -> none  [local(): white = jnp.transpose(white, (0, 2, 1, 3))]
    unnamed x6 -> x7, local copies, waits for them, and re-layouts: 10.7 us -> 6.21 us
    all_to_all x1, local copies, waits for them, and re-layouts: 6.86 us -> 3.05 us  [local(): lax.all_to_all(send, 'sta', split_axis=2, concat_axis=3, tiled=True)]
  transfers between devices with their start and end apart: 4 -> 4, of which waited for: 2 -> 3; matrix products, arithmetic and copies ran while one was open for 8% -> 9% of each run, Pallas kernels for 12% -> 16%
where the time goes in v1:
time: 258 us; the launch traced here: 257 us
  waiting for transfers between devices  80 us (31%)
  Pallas kernels  60 us (23%)
  other arithmetic  53.2 us (21%)
  local copies, waits for them, and re-layouts  38.8 us (15%)
  between operations  13.2 us (5%)
  starting transfers between devices  11.6 us (4%)
    pallas_call x3, Pallas kernels, cross_project(): pl.pallas_call(cross_project_kernel, grid=(steps,), in_specs=[pl.BlockSpe...  60 us
    all_to_all x1, waiting for transfers between devices, local(): lax.all_to_all(send, 'sta', split_axis=2, concat_axis=3, tiled=True)  51.2 us
    reduce_scatter x3, waiting for transfers between devices, local(): stacked = lax.psum_scatter(projected, 'tm', scatter_dimension=0, tiled=True)  28.8 us
    another operation x1, other arithmetic  18.2 us
    div x2, local copies, waits for them, and re-layouts, local(): grid_view / (level_mean[:, None, :, :, None] + EPSILON)  15.2 us
    concatenate x1, other arithmetic, local(): jnp.concatenate([chunks, src_copies], axis=3)  14.5 us
    all_to_all x1, starting transfers between devices, local(): lax.all_to_all(send, 'sta', split_axis=2, concat_axis=3, tiled=True)  11.3 us
    sqrt x1, local copies, waits for them, and re-layouts, local(): jnp.sqrt(values[:, 0] * values[:, 0] + values[:, 1] * values[:, 1])  8.74 us
  transfers between devices with their start and end apart: 4, of which 3 were waited for; matrix products, arithmetic and copies ran while one was open for 9% of the time, Pallas kernels for 16%

profile of v1, /device:TPU:1, one launch (start us, length us, event | category | flops | bytes accessed | tf_op | source)
XLA Modules:
  0.0 256.8 jit_solution(529513376300035412)
XLA Ops:
  6.5 0.8 reshape.72
  7.3 0.8 reshape.71
  8.1 2.8 %gather_fusion = bf16[24,2,2,128]{3,2,1,0:T(2,128)(2,1)S(1)} fusion(bf16[2,2,4096,128]{3,1,2,0:T(2,128)(2,1)} %bitcast.35, s32[1024]{0:T(1024)S(1)} %pad_clamp_fusion), kind=kCustom, calls=%fused_computation | custom fusion | bytes 49248 | tf_op jit(solution)/shard_map/jit(_take)/gather | solution.py:129
  10.9 0.1 fusion.8
  11.0 0.4 broadcast_in_dim.21
  11.4 14.5 %pad_maximum_fusion = bf16[2,2,32,152,128]{4,1,0,3,2:T(2,128)(2,1)} fusion(bf16[2,2,32,24,128]{4,1,0,3,2:T(2,128)(2,1)S(1)} %broadcast_in_dim.21, bf16[2,2,32,128,128]{4,1,3,2,0:T(2,128)(2,1)} %bitcast.36), kind=kLoop, calls=%fused_computation.11 | loop fusion | flops 9961472 | bytes 9961472 | tf_op jit(solution)/shard_map/concatenate | solution.py:134
  25.9 11.3 %all-to-all-start = ((bf16[2,2,4864,128]{3,1,0,2:T(2,128)(2,1)}), bf16[2,2,4864,128]{3,1,0,2:T(2,128)(2,1)}, u32[]{:S(2)}, u32[]{:S(2)}) async-start(bf16[2,2,4864,128]{3,1,0,2:T(2,128)(2,1)} %bitcast.34), calls=%async_computation | async-start | bytes 9961472 | tf_op jit(solution)/shard_map/all_to_all | solution.py:137
  37.2 0.2 reduce-scatter.4.cloned.1.call-start
  37.4 18.2 %multiply_convert_fusion.1 = (bf16[256,4096]{1,0:T(8,128)(2,1)S(1)}, bf16[256,4096]{1,0:T(8,128)(2,1)S(1)}) fusion(s32[256]{0:T(256)S(1)} %iota_add_fusion), kind=kLoop, calls=%fused_computation.17 | loop fusion | flops 19922944 | bytes 4195328 | tf_op jit(solution)/shard_map/convert.3
  55.7 2.4 pad_maximum_fusion.1.tre_ref.tim_ref
  58.1 51.2 %all-to-all-done = bf16[2,2,4864,128]{3,1,0,2:T(2,128)(2,1)} async-done(((bf16[2,2,4864,128]{3,1,0,2:T(2,128)(2,1)}), bf16[2,2,4864,128]{3,1,0,2:T(2,128)(2,1)}, u32[]{:S(2)}, u32[]{:S(2)}) %all-to-all-start) | async-done | bytes 4980768 | tf_op jit(solution)/shard_map/all_to_all | solution.py:137
  109.2 3.1 %copy.8 = bf16[2,2,4864,128]{3,2,1,0:T(8,128)(2,1)S(1)} copy(bf16[2,2,4864,128]{3,1,0,2:T(2,128)(2,1)} %all-to-all-done) | data formatting | bytes 9961472 | tf_op jit(solution)/shard_map/all_to_all | solution.py:137
  112.3 1.3 copy_bitcast_fusion
  113.6 1.0 copy-done.1
  114.6 3.9 %fusion.1 = f32[2,1,152,4096]{3,2,1,0:T(8,128)} fusion(f32[2,2,152,4096]{3,2,1,0:T(8,128)S(1)} %copy_bitcast_fusion), kind=kLoop, calls=%fused_computation.9 | loop fusion | flops 3735552 | bytes 14942208 | tf_op jit(solution)/shard_map/sqrt | solution.py:139
  118.5 8.7 %sqrt.12 = f32[2,152,64,64]{3,2,1,0:T(8,128)} reshape(f32[2,1,152,4096]{3,2,1,0:T(8,128)} %fusion.1) | data formatting | bytes 9961472 | tf_op jit(solution)/shard_map/sqrt | solution.py:139
  127.2 6.5 %reduce_sum.9 = f32[2,152,64]{2,1,0:T(8,128)S(1)} reduce(f32[2,152,64,64]{3,2,1,0:T(8,128)} %sqrt.12, f32[]{:T(128)} %constant.38.clone.1), dimensions={3}, to_apply=%region_0.1 | reduce | flops 1225728 | bytes 5058564 | tf_op jit(solution)/shard_map/reduce_sum | solution.py:142
  133.7 0.2 multiply_add_fusion
  133.9 6.0 %div.21 = f32[2,152,64,64]{3,2,1,0:T(8,128)} broadcast(f32[2,152,64]{2,1,0:T(8,128)S(1)} %multiply_add_fusion), dimensions={0,1,2} | broadcast | bytes 5058560 | tf_op jit(solution)/shard_map/div | solution.py:146
  139.9 9.2 %div.22 = f32[2,152,4096]{2,1,0:T(8,128)} reshape(f32[2,152,64,64]{3,2,1,0:T(8,128)} %div.21) | data formatting | bytes 9961472 | tf_op jit(solution)/shard_map/div | solution.py:146
  149.0 5.2 %divide_convert_fusion.x_ref = bf16[2,2,152,4096]{3,2,1,0:T(8,128)(2,1)S(1)} fusion(f32[2,152,4096]{2,1,0:T(8,128)} %div.22, bf16[2,2,32,152,128]{4,3,2,1,0:T(8,128)(2,1)} %bitcast.33), kind=kLoop, calls=%fused_computation.3 | loop fusion | flops 7471104 | bytes 14942208 | tf_op jit(solution)/shard_map/convert_element_type | solution.py:147
  154.2 2.2 copy-done
  156.4 0.9 fusion.10
  157.3 20.0 %shard_map.28 = f32[256,1024]{1,0:T(8,128)} custom-call(bf16[2,2,152,4096]{3,2,1,0:T(8,128)(2,1)} %copy-done, bf16[2,2,8,4096]{3,2,1,0:T(8,128)(2,1)} %get-tuple-element.5.y_ref, bf16[256,8192]{1,0:T(8,128)(2,1)} %pad_maximum_fusion.1.tre_ref.tim_ref, bf16[256,8192]{1,0:T(8,128)(2,1)} %pad_maximum_fusion.1.tre_ref.tim_ref), custom_call_target="tpu_custom_call" | custom-call | tf_op jit(solution)/shard_map/pallas_call | solution.py:102
  177.4 20.0 %shard_map.29 = f32[256,1024]{1,0:T(8,128)} custom-call(bf16[2,2,152,4096]{3,2,1,0:T(8,128)(2,1)} %copy-done, bf16[2,2,8,4096]{3,2,1,0:T(8,128)(2,1)} %get-tuple-element.7.y_ref, bf16[256,8192]{1,0:T(8,128)(2,1)} %pad_maximum_fusion.1.tre_ref.tim_ref, bf16[256,8192]{1,0:T(8,128)(2,1)} %pad_maximum_fusion.1.tre_ref.tim_ref), custom_call_target="tpu_custom_call" | custom-call | tf_op jit(solution)/shard_map/pallas_call | solution.py:102
  197.5 20.0 %shard_map.30 = f32[256,1024]{1,0:T(8,128)} custom-call(bf16[2,2,152,4096]{3,2,1,0:T(8,128)(2,1)} %copy-done, bf16[2,2,8,4096]{3,2,1,0:T(8,128)(2,1)} %get-tuple-element.6.y_ref, bf16[256,8192]{1,0:T(8,128)(2,1)} %pad_maximum_fusion.1.tre_ref.tim_ref, bf16[256,8192]{1,0:T(8,128)(2,1)} %pad_maximum_fusion.1.tre_ref.tim_ref), custom_call_target="tpu_custom_call" | custom-call | tf_op jit(solution)/shard_map/pallas_call | solution.py:102
  217.6 1.0 copy.11
  218.6 6.0 %reduce-scatter.6.cloned.1.call-done = f32[64,1024]{1,0:T(8,128)} async-done(((f32[256,1024]{1,0:T(8,128)}), f32[64,1024]{1,0:T(8,128)}) %reduce-scatter.6.cloned.1.call-update) | async-done | bytes 262160 | tf_op jit(solution)/shard_map/reduce_scatter | solution.py:155
  224.5 1.0 copy.12
  225.5 22.8 %reduce-scatter.8.cloned.1.call-done = f32[64,1024]{1,0:T(8,128)} async-done(((f32[256,1024]{1,0:T(8,128)}), f32[64,1024]{1,0:T(8,128)}) %reduce-scatter.8.cloned.1.call-update) | async-done | bytes 262160 | tf_op jit(solution)/shard_map/reduce_scatter | solution.py:155
  248.3 1.0 copy.13
  249.3 1.0 pad_maximum_fusion.2
  (12 shorter events, 0.2 us)
Async XLA Ops:
  25.9 83.3 %all-to-all-start = ((bf16[2,2,4864,128]{3,1,0,2:T(2,128)(2,1)}), bf16[2,2,4864,128]{3,1,0,2:T(2,128)(2,1)}, u32[]{:S(2)}, u32[]{:S(2)}) async-start(bf16[2,2,4864,128]{3,1,0,2:T(2,128)(2,1)} %bitcast.34), calls=%async_computation | async-start | bytes 9961472 | tf_op jit(solution)/shard_map/all_to_all | solution.py:137
  37.2 180.4 %reduce-scatter.4.cloned.1.call-start = ((), (), s32[]{:S(2)}) async-start(), calls=%async_computation.4 | async-start | bytes 1310720 | tf_op jit(solution)/shard_map/reduce_scatter | solution.py:155
  112.3 2.3 copy-start.1
  154.2 2.2 copy-start
  177.4 47.2 %reduce-scatter.6.cloned.1.call-start = ((), (), s32[]{:S(2)}) async-start(), calls=%async_computation.5 | async-start | bytes 1310720 | tf_op jit(solution)/shard_map/reduce_scatter | solution.py:155
  197.5 50.8 %reduce-scatter.8.cloned.1.call-start = ((), (), s32[]{:S(2)}) async-start(), calls=%async_computation.6 | async-start | bytes 1310720 | tf_op jit(solution)/shard_map/reduce_scatter | solution.py:155
Sparse Core Ops, SparseCore 0:
  177.5 23.2 reduce-scatter.3
  203.2 21.3 reduce-scatter.5
  227.0 21.3 reduce-scatter.7

commit v2 on v1

--- a/solution.py
+++ b/solution.py
@@ -137,14 +137,20 @@
     joined = lax.all_to_all(send, "sta", split_axis=2, concat_axis=3, tiled=True)
     values = joined.astype(jnp.float32)
     magnitude = jnp.sqrt(values[:, 0] * values[:, 0] + values[:, 1] * values[:, 1])
-    rows = magnitude.shape[1]
     block_num = BINS // BLOCK
-    totals = magnitude.reshape(hours_dev, rows, block_num, BLOCK).sum(axis=-1)
+    indicator = (
+        lax.broadcasted_iota(jnp.int32, (BINS, block_num), 0) // BLOCK
+        == lax.broadcasted_iota(jnp.int32, (BINS, block_num), 1)
+    ).astype(jnp.float32)
+    totals = jnp.einsum(
+        "hrf,fb->hrb", magnitude, indicator, precision=lax.Precision.HIGHEST
+    )
     padded = jnp.pad(totals, ((0, 0), (0, 0), (1, 1)))
     level_mean = (padded[..., :-2] + padded[..., 1:-1] + padded[..., 2:]) / (3.0 * BLOCK)
-    grid_view = values.reshape(hours_dev, 2, rows, block_num, BLOCK)
-    white = (grid_view / (level_mean[:, None, :, :, None] + EPSILON)).reshape(values.shape)
-    white = white.astype(jnp.bfloat16)
+    denom = jnp.einsum(
+        "hrb,fb->hrf", level_mean + EPSILON, indicator, precision=lax.Precision.HIGHEST
+    )
+    white = (values / denom[:, None]).astype(jnp.bfloat16)
     transform = make_table(hours_dev * lax.axis_size("tm"))
     row_count = transform.shape[0] // lax.axis_size("tm")
     results = []

time: 258 us -> 230 us (0.89)
  local copies, waits for them, and re-layouts: 38.8 us -> 13.9 us
  other arithmetic: 53.2 us -> 41.3 us
  matrix products: 0 us -> 8.79 us
    div x2 -> x0, local copies, waits for them, and re-layouts: 15.2 us -> none  [local(): grid_view / (level_mean[:, None, :, :, None] + EPSILON)]
    dot_general x0 -> x2, matrix products: none -> 8.79 us  [the longest x1 4.42 us: local(): jnp.einsum('hrf,fb->hrb', magnitude, indicator, precision=lax.Precision.H...]
    sqrt x1 -> x0, local copies, waits for them, and re-layouts: 8.74 us -> none  [local(): jnp.sqrt(values[:, 0] * values[:, 0] + values[:, 1] * values[:, 1])]
    reduce_sum x1 -> x0, other arithmetic: 6.47 us -> none  [local(): totals = magnitude.reshape(hours_dev, rows, block_num, BLOCK).sum(axis=-1)]
    sqrt x1 -> x0, other arithmetic: 3.89 us -> none  [local(): jnp.sqrt(values[:, 0] * values[:, 0] + values[:, 1] * values[:, 1])]
    unnamed x7 -> x5, local copies, waits for them, and re-layouts: 6.21 us -> 5.2 us
  transfers between devices with their start and end apart: 4 -> 4, of which waited for: 3 -> 3; matrix products, arithmetic and copies ran while one was open for 9% -> 10% of each run, Pallas kernels for 16% -> 18%
where the time goes in v2:
time: 230 us; the launch traced here: 229 us
  waiting for transfers between devices  79.8 us (35%)
  Pallas kernels  60 us (26%)
  other arithmetic  41.3 us (18%)
  local copies, waits for them, and re-layouts  13.9 us (6%)
  between operations  13.2 us (6%)
  starting transfers between devices  11.6 us (5%)
  matrix products  8.79 us (4%)
    pallas_call x3, Pallas kernels, cross_project(): pl.pallas_call(cross_project_kernel, grid=(steps,), in_specs=[pl.BlockSpe...  60 us
    all_to_all x1, waiting for transfers between devices, local(): lax.all_to_all(send, 'sta', split_axis=2, concat_axis=3, tiled=True)  51 us
    reduce_scatter x3, waiting for transfers between devices, local(): stacked = lax.psum_scatter(projected, 'tm', scatter_dimension=0, tiled=True)  28.8 us
    another operation x1, other arithmetic  18.2 us
    concatenate x1, other arithmetic, local(): jnp.concatenate([chunks, src_copies], axis=3)  14.4 us
    all_to_all x1, starting transfers between devices, local(): lax.all_to_all(send, 'sta', split_axis=2, concat_axis=3, tiled=True)  11.3 us
    unnamed x5, local copies, waits for them, and re-layouts  5.2 us
  transfers between devices with their start and end apart: 4, of which 3 were waited for; matrix products, arithmetic and copies ran while one was open for 10% of the time, Pallas kernels for 18%

profile of v2, /device:TPU:1, one launch (start us, length us, event | category | flops | bytes accessed | tf_op | source)
XLA Modules:
  0.0 228.7 jit_solution(18063502961188566393)
XLA Ops:
  6.5 0.8 reshape.63
  7.3 0.8 reshape.62
  8.1 2.8 %gather_fusion = bf16[24,2,2,128]{3,2,1,0:T(2,128)(2,1)S(1)} fusion(bf16[2,2,4096,128]{3,1,2,0:T(2,128)(2,1)} %bitcast.38, s32[1024]{0:T(1024)S(1)} %pad_clamp_fusion), kind=kCustom, calls=%fused_computation | custom fusion | bytes 49248 | tf_op jit(solution)/shard_map/jit(_take)/gather | solution.py:129
  10.9 0.1 fusion.28
  11.0 0.4 broadcast_in_dim.21
  11.4 14.4 %pad_maximum_fusion = bf16[2,2,32,152,128]{4,1,0,3,2:T(2,128)(2,1)} fusion(bf16[2,2,32,24,128]{4,1,0,3,2:T(2,128)(2,1)S(1)} %broadcast_in_dim.21, bf16[2,2,32,128,128]{4,1,3,2,0:T(2,128)(2,1)} %bitcast.39), kind=kLoop, calls=%fused_computation.13 | loop fusion | flops 9961472 | bytes 9961472 | tf_op jit(solution)/shard_map/concatenate | solution.py:134
  25.9 11.3 %all-to-all-start = ((bf16[2,2,4864,128]{3,1,0,2:T(2,128)(2,1)}), bf16[2,2,4864,128]{3,1,0,2:T(2,128)(2,1)}, u32[]{:S(2)}, u32[]{:S(2)}) async-start(bf16[2,2,4864,128]{3,1,0,2:T(2,128)(2,1)} %bitcast.37), calls=%async_computation | async-start | bytes 9961472 | tf_op jit(solution)/shard_map/all_to_all | solution.py:137
  37.2 0.2 reduce-scatter.4.cloned.1.call-start
  37.4 18.2 %multiply_convert_fusion.1 = (bf16[256,4096]{1,0:T(8,128)(2,1)S(1)}, bf16[256,4096]{1,0:T(8,128)(2,1)S(1)}) fusion(s32[256]{0:T(256)S(1)} %iota_add_fusion), kind=kLoop, calls=%fused_computation.19 | loop fusion | flops 19922944 | bytes 4195328 | tf_op jit(solution)/shard_map/convert.3
  55.7 2.5 %pad_maximum_fusion.1.tre_ref.tim_ref = bf16[256,8192]{1,0:T(8,128)(2,1)} fusion(bf16[256,4096]{1,0:T(8,128)(2,1)S(1)} %get-tuple-element.9, bf16[256,4096]{1,0:T(8,128)(2,1)S(1)} %get-tuple-element.8), kind=kLoop, calls=%fused_computation.17 | loop fusion | flops 8388608 | bytes 8388608 | tf_op jit(solution)/shard_map/concatenate | solution.py:46
  58.2 51.0 %all-to-all-done = bf16[2,2,4864,128]{3,1,0,2:T(2,128)(2,1)} async-done(((bf16[2,2,4864,128]{3,1,0,2:T(2,128)(2,1)}), bf16[2,2,4864,128]{3,1,0,2:T(2,128)(2,1)}, u32[]{:S(2)}, u32[]{:S(2)}) %all-to-all-start) | async-done | bytes 4980768 | tf_op jit(solution)/shard_map/all_to_all | solution.py:137
  109.2 3.1 %copy.8 = bf16[2,2,4864,128]{3,2,1,0:T(8,128)(2,1)S(1)} copy(bf16[2,2,4864,128]{3,1,0,2:T(2,128)(2,1)} %all-to-all-done) | data formatting | bytes 9961472 | tf_op jit(solution)/shard_map/all_to_all | solution.py:137
  112.3 1.3 copy_bitcast_fusion
  113.5 4.4 %fusion.3 = f32[2,152,64]{1,2,0:T(8,128)S(1)} fusion(f32[2,2,152,4096]{3,2,1,0:T(8,128)S(1)} %copy_bitcast_fusion, s32[4096]{0:T(1024)S(1)} %iota_shift-right-logical_fusion, s32[4096]{0:T(1024)S(1)} %broadcast_add_fusion, pred[4096]{0:T(1024)(128)(4,1)S(1)} %fusion.31), kind=kOutput, calls=%fused_computation.11 | convolution fusion | flops 960561152 | bytes 10076160 | tf_op jit(solution)/shard_map/hrf,fb->hrb/dot_general | solution.py:145
  118.0 4.4 %fusion.12 = f32[2,152,4096]{2,1,0:T(8,128)} fusion(s32[4096]{0:T(1024)S(1)} %iota_shift-right-logical_fusion, s32[4096]{0:T(1024)S(1)} %broadcast_add_fusion, pred[4096]{0:T(1024)(128)(4,1)S(1)} %fusion.31, f32[2,152,64]{1,2,0:T(8,128)S(1)} %fusion.3), kind=kOutput, calls=%fused_computation.26 | convolution fusion | flops 956903424 | bytes 5095424 | tf_op jit(solution)/shard_map/hrb,fb->hrf/dot_general | solution.py:150
  122.3 3.7 %divide_convert_fusion.x_ref = bf16[2,2,152,4096]{3,2,1,0:T(8,128)(2,1)S(1)} fusion(f32[2,152,4096]{2,1,0:T(8,128)} %fusion.12, bf16[2,2,32,152,128]{4,3,2,1,0:T(8,128)(2,1)S(1)} %bitcast.36), kind=kLoop, calls=%fused_computation.3 | loop fusion | flops 7471104 | bytes 14942208 | tf_op jit(solution)/shard_map/convert_element_type | solution.py:153
  126.1 2.2 copy-done
  128.3 0.9 fusion.36
  129.2 20.0 %shard_map.28 = f32[256,1024]{1,0:T(8,128)} custom-call(bf16[2,2,152,4096]{3,2,1,0:T(8,128)(2,1)} %copy-done, bf16[2,2,8,4096]{3,2,1,0:T(8,128)(2,1)} %get-tuple-element.5.y_ref, bf16[256,8192]{1,0:T(8,128)(2,1)} %pad_maximum_fusion.1.tre_ref.tim_ref, bf16[256,8192]{1,0:T(8,128)(2,1)} %pad_maximum_fusion.1.tre_ref.tim_ref), custom_call_target="tpu_custom_call" | custom-call | tf_op jit(solution)/shard_map/pallas_call | solution.py:102
  149.2 0.0 reduce-scatter.4.cloned.1.call-update
  149.2 0.0 reduce-scatter.6.cloned.1.call-start
  149.3 20.0 %shard_map.29 = f32[256,1024]{1,0:T(8,128)} custom-call(bf16[2,2,152,4096]{3,2,1,0:T(8,128)(2,1)} %copy-done, bf16[2,2,8,4096]{3,2,1,0:T(8,128)(2,1)} %get-tuple-element.7.y_ref, bf16[256,8192]{1,0:T(8,128)(2,1)} %pad_maximum_fusion.1.tre_ref.tim_ref, bf16[256,8192]{1,0:T(8,128)(2,1)} %pad_maximum_fusion.1.tre_ref.tim_ref), custom_call_target="tpu_custom_call" | custom-call | tf_op jit(solution)/shard_map/pallas_call | solution.py:102
  169.3 0.0 reduce-scatter.6.cloned.1.call-update
  169.3 0.0 reduce-scatter.8.cloned.1.call-start
  169.4 20.0 %shard_map.30 = f32[256,1024]{1,0:T(8,128)} custom-call(bf16[2,2,152,4096]{3,2,1,0:T(8,128)(2,1)} %copy-done, bf16[2,2,8,4096]{3,2,1,0:T(8,128)(2,1)} %get-tuple-element.6.y_ref, bf16[256,8192]{1,0:T(8,128)(2,1)} %pad_maximum_fusion.1.tre_ref.tim_ref, bf16[256,8192]{1,0:T(8,128)(2,1)} %pad_maximum_fusion.1.tre_ref.tim_ref), custom_call_target="tpu_custom_call" | custom-call | tf_op jit(solution)/shard_map/pallas_call | solution.py:102
  189.4 0.0 reduce-scatter.4.cloned.1.call-done
  189.4 1.0 copy.11
  190.4 6.0 %reduce-scatter.6.cloned.1.call-done = f32[64,1024]{1,0:T(8,128)} async-done(((f32[256,1024]{1,0:T(8,128)}), f32[64,1024]{1,0:T(8,128)}) %reduce-scatter.6.cloned.1.call-update) | async-done | bytes 262160 | tf_op jit(solution)/shard_map/reduce_scatter | solution.py:161
  196.4 1.0 copy.12
  197.4 22.8 %reduce-scatter.8.cloned.1.call-done = f32[64,1024]{1,0:T(8,128)} async-done(((f32[256,1024]{1,0:T(8,128)}), f32[64,1024]{1,0:T(8,128)}) %reduce-scatter.8.cloned.1.call-update) | async-done | bytes 262160 | tf_op jit(solution)/shard_map/reduce_scatter | solution.py:161
  220.2 1.0 copy.13
  221.2 1.0 pad_maximum_fusion.2
  (9 shorter events, 0.1 us)
Async XLA Ops:
  25.9 83.3 %all-to-all-start = ((bf16[2,2,4864,128]{3,1,0,2:T(2,128)(2,1)}), bf16[2,2,4864,128]{3,1,0,2:T(2,128)(2,1)}, u32[]{:S(2)}, u32[]{:S(2)}) async-start(bf16[2,2,4864,128]{3,1,0,2:T(2,128)(2,1)} %bitcast.37), calls=%async_computation | async-start | bytes 9961472 | tf_op jit(solution)/shard_map/all_to_all | solution.py:137
  37.2 152.3 %reduce-scatter.4.cloned.1.call-start = ((), (), s32[]{:S(2)}) async-start(), calls=%async_computation.4 | async-start | bytes 1310720 | tf_op jit(solution)/shard_map/reduce_scatter | solution.py:161
  126.1 2.2 copy-start
  149.2 47.2 %reduce-scatter.6.cloned.1.call-start = ((), (), s32[]{:S(2)}) async-start(), calls=%async_computation.5 | async-start | bytes 1310720 | tf_op jit(solution)/shard_map/reduce_scatter | solution.py:161
  169.3 50.9 %reduce-scatter.8.cloned.1.call-start = ((), (), s32[]{:S(2)}) async-start(), calls=%async_computation.6 | async-start | bytes 1310720 | tf_op jit(solution)/shard_map/reduce_scatter | solution.py:161
Sparse Core Ops, SparseCore 0:
  149.4 23.2 reduce-scatter.3
  175.1 21.3 reduce-scatter.5
  198.8 21.3 reduce-scatter.7

commit v3 on v2

--- a/solution.py
+++ b/solution.py
@@ -119,6 +119,20 @@
     )(receivers, sources, transform, transform)
 
 
+def reduce_lags(projected):
+    index = lax.axis_index("tm")
+    core = index % 2
+    z_lo = index // 2
+    lags, width = projected.shape
+    blocks = projected.reshape(2, 2, lags // 4, width)
+    keep = lax.dynamic_index_in_dim(blocks, core, axis=1, keepdims=False)
+    send = lax.dynamic_index_in_dim(blocks, 1 - core, axis=1, keepdims=False)
+    half = keep + lax.ppermute(send, "tm", perm=[(0, 1), (1, 0), (2, 3), (3, 2)])
+    keep = lax.dynamic_index_in_dim(half, z_lo, axis=0, keepdims=False)
+    send = lax.dynamic_index_in_dim(half, 1 - z_lo, axis=0, keepdims=False)
+    return keep + lax.ppermute(send, "tm", perm=[(0, 2), (2, 0), (1, 3), (3, 1)])
+
+
 def local(spectra, src_ids):
     hours_dev, stations, _, bins_dev = spectra.shape
     shards = lax.axis_size("sta")
@@ -158,7 +172,7 @@
         first = stations_dev + step_no * NSRC
         sources = white[:, :, first:first + NSRC]
         projected = cross_project(white, sources, transform, stations_dev)
-        stacked = lax.psum_scatter(projected, "tm", scatter_dimension=0, tiled=True)
+        stacked = reduce_lags(projected)
         results.append(stacked.reshape(row_count, NSRC, stations_dev))
     return jnp.stack(results)
 

time: 230 us -> 212 us (0.922)
  between operations: 13.2 us -> 0.22 us
  waiting for transfers between devices: 79.8 us -> 67.4 us
  starting transfers between devices: 11.6 us -> 16.3 us
    reduce_scatter x3 -> x0, waiting for transfers between devices: 28.8 us -> none  [local(): stacked = lax.psum_scatter(projected, 'tm', scatter_dimension=0, tiled=True)]
    ppermute x0 -> x6, waiting for transfers between devices: none -> 16.3 us  [the longest x3 16.3 us: reduce_lags(): lax.ppermute(send, 'tm', perm=[(0, 2), (2, 0), (1, 3), (3, 1)])]
    squeeze x0 -> x6, local copies, waits for them, and re-layouts: none -> 5.08 us  [the longest x3 5 us: reduce_lags(): send = lax.dynamic_index_in_dim(blocks, 1 - core, axis=1, keepdims=False)]
    ppermute x0 -> x6, starting transfers between devices: none -> 4.79 us  [the longest x3 2.43 us: reduce_lags(): lax.ppermute(send, 'tm', perm=[(0, 2), (2, 0), (1, 3), (3, 1)])]
    unnamed x5 -> x11, local copies, waits for them, and re-layouts: 5.2 us -> 2.38 us
  transfers between devices with their start and end apart: 4 -> 7, of which waited for: 3 -> 4; matrix products, arithmetic and copies ran while one was open for 10% -> 12% of each run, Pallas kernels for 18% -> 19%
where the time goes in v3:
time: 212 us; the launch traced here: 211 us
  waiting for transfers between devices  67.4 us (32%)
  Pallas kernels  60.2 us (28%)
  other arithmetic  41.5 us (20%)
  starting transfers between devices  16.3 us (8%)
  local copies, waits for them, and re-layouts  16.2 us (8%)
  matrix products  8.8 us (4%)
    pallas_call x3, Pallas kernels, cross_project(): pl.pallas_call(cross_project_kernel, grid=(steps,), in_specs=[pl.BlockSpe...  60.2 us
    all_to_all x1, waiting for transfers between devices, local(): lax.all_to_all(send, 'sta', split_axis=2, concat_axis=3, tiled=True)  51.1 us
    another operation x1, other arithmetic  18.2 us
    ppermute x3, waiting for transfers between devices, reduce_lags(): lax.ppermute(send, 'tm', perm=[(0, 2), (2, 0), (1, 3), (3, 1)])  16.3 us
    concatenate x1, other arithmetic, local(): jnp.concatenate([chunks, src_copies], axis=3)  14.4 us
    all_to_all x1, starting transfers between devices, local(): lax.all_to_all(send, 'sta', split_axis=2, concat_axis=3, tiled=True)  11.5 us
    squeeze x3, local copies, waits for them, and re-layouts, reduce_lags(): send = lax.dynamic_index_in_dim(blocks, 1 - core, axis=1, keepdims=False)  5 us
    dot_general x1, matrix products, local(): jnp.einsum('hrf,fb->hrb', magnitude, indicator, precision=lax.Precision.H...  4.42 us
  transfers between devices with their start and end apart: 7, of which 4 were waited for; matrix products, arithmetic and copies ran while one was open for 12% of the time, Pallas kernels for 19%

profile of v3, /device:TPU:1, one launch (start us, length us, event | category | flops | bytes accessed | tf_op | source)
XLA Modules:
  0.0 210.6 jit_solution(16860987716037705097)
XLA Ops:
  0.0 0.8 reshape.72
  0.8 0.8 reshape.71
  1.6 2.8 %gather_fusion = bf16[24,2,2,128]{3,2,1,0:T(2,128)(2,1)S(1)} fusion(bf16[2,2,4096,128]{3,1,2,0:T(2,128)(2,1)} %bitcast.74, s32[1024]{0:T(1024)S(1)} %pad_clamp_fusion), kind=kCustom, calls=%fused_computation | custom fusion | bytes 49248 | tf_op jit(solution)/shard_map/jit(_take)/gather | solution.py:143
  4.4 0.1 fusion.31
  4.5 0.4 broadcast_in_dim.21
  4.9 14.4 %pad_maximum_fusion = bf16[2,2,32,152,128]{4,1,0,3,2:T(2,128)(2,1)} fusion(bf16[2,2,32,24,128]{4,1,0,3,2:T(2,128)(2,1)S(1)} %broadcast_in_dim.21, bf16[2,2,32,128,128]{4,1,3,2,0:T(2,128)(2,1)} %bitcast.75), kind=kLoop, calls=%fused_computation.13 | loop fusion | flops 9961472 | bytes 9961472 | tf_op jit(solution)/shard_map/concatenate | solution.py:148
  19.3 11.5 %all-to-all-start = ((bf16[2,2,4864,128]{3,1,0,2:T(2,128)(2,1)}), bf16[2,2,4864,128]{3,1,0,2:T(2,128)(2,1)}, u32[]{:S(2)}, u32[]{:S(2)}) async-start(bf16[2,2,4864,128]{3,1,0,2:T(2,128)(2,1)} %bitcast.73), calls=%async_computation | async-start | bytes 9961472 | tf_op jit(solution)/shard_map/all_to_all | solution.py:151
  30.8 18.2 %multiply_convert_fusion.1 = (bf16[256,4096]{1,0:T(8,128)(2,1)S(1)}, bf16[256,4096]{1,0:T(8,128)(2,1)S(1)}) fusion(s32[256]{0:T(256)S(1)} %iota_add_fusion), kind=kLoop, calls=%fused_computation.19 | loop fusion | flops 19922944 | bytes 4195328 | tf_op jit(solution)/shard_map/convert.3
  49.1 2.5 %pad_maximum_fusion.1.tre_ref.tim_ref = bf16[256,8192]{1,0:T(8,128)(2,1)} fusion(bf16[256,4096]{1,0:T(8,128)(2,1)S(1)} %get-tuple-element.9, bf16[256,4096]{1,0:T(8,128)(2,1)S(1)} %get-tuple-element.8), kind=kLoop, calls=%fused_computation.17 | loop fusion | flops 8388608 | bytes 8388608 | tf_op jit(solution)/shard_map/concatenate | solution.py:46
  51.6 51.1 %all-to-all-done = bf16[2,2,4864,128]{3,1,0,2:T(2,128)(2,1)} async-done(((bf16[2,2,4864,128]{3,1,0,2:T(2,128)(2,1)}), bf16[2,2,4864,128]{3,1,0,2:T(2,128)(2,1)}, u32[]{:S(2)}, u32[]{:S(2)}) %all-to-all-start) | async-done | bytes 4980768 | tf_op jit(solution)/shard_map/all_to_all | solution.py:151
  102.7 3.1 %copy.8 = bf16[2,2,4864,128]{3,2,1,0:T(8,128)(2,1)S(1)} copy(bf16[2,2,4864,128]{3,1,0,2:T(2,128)(2,1)} %all-to-all-done) | data formatting | bytes 9961472 | tf_op jit(solution)/shard_map/all_to_all | solution.py:151
  105.8 1.3 copy_bitcast_fusion
  107.1 4.4 %fusion.3 = f32[2,152,64]{1,2,0:T(8,128)S(1)} fusion(f32[2,2,152,4096]{3,2,1,0:T(8,128)S(1)} %copy_bitcast_fusion, s32[4096]{0:T(1024)S(1)} %iota_shift-right-logical_fusion, s32[4096]{0:T(1024)S(1)} %broadcast_add_fusion, pred[4096]{0:T(1024)(128)(4,1)S(1)} %fusion.34), kind=kOutput, calls=%fused_computation.11 | convolution fusion | flops 960561152 | bytes 10076160 | tf_op jit(solution)/shard_map/hrf,fb->hrb/dot_general | solution.py:159
  111.5 4.4 %fusion.12 = f32[2,152,4096]{2,1,0:T(8,128)} fusion(s32[4096]{0:T(1024)S(1)} %iota_shift-right-logical_fusion, s32[4096]{0:T(1024)S(1)} %broadcast_add_fusion, pred[4096]{0:T(1024)(128)(4,1)S(1)} %fusion.34, f32[2,152,64]{1,2,0:T(8,128)S(1)} %fusion.3), kind=kOutput, calls=%fused_computation.26 | convolution fusion | flops 956903424 | bytes 5095424 | tf_op jit(solution)/shard_map/hrb,fb->hrf/dot_general | solution.py:164
  115.9 3.7 %divide_convert_fusion.x_ref = bf16[2,2,152,4096]{3,2,1,0:T(8,128)(2,1)S(1)} fusion(f32[2,152,4096]{2,1,0:T(8,128)} %fusion.12, bf16[2,2,32,152,128]{4,3,2,1,0:T(8,128)(2,1)S(1)} %bitcast.72), kind=kLoop, calls=%fused_computation.3 | loop fusion | flops 7471104 | bytes 14942208 | tf_op jit(solution)/shard_map/convert_element_type | solution.py:167
  119.6 2.2 %copy-done = bf16[2,2,152,4096]{3,2,1,0:T(8,128)(2,1)} copy-done((bf16[2,2,152,4096]{3,2,1,0:T(8,128)(2,1)}, bf16[2,2,152,4096]{3,2,1,0:T(8,128)(2,1)S(1)}, u32[]{:S(2)}) %copy-start) | copy-done | bytes 4980760
  121.8 0.9 fusion.39
  122.7 20.0 %shard_map.30 = f32[256,1024]{1,0:T(8,128)} custom-call(bf16[2,2,152,4096]{3,2,1,0:T(8,128)(2,1)} %copy-done, bf16[2,2,8,4096]{3,2,1,0:T(8,128)(2,1)} %get-tuple-element.6.y_ref, bf16[256,8192]{1,0:T(8,128)(2,1)} %pad_maximum_fusion.1.tre_ref.tim_ref, bf16[256,8192]{1,0:T(8,128)(2,1)} %pad_maximum_fusion.1.tre_ref.tim_ref), custom_call_target="tpu_custom_call" | custom-call | tf_op jit(solution)/shard_map/pallas_call | solution.py:102
  142.7 1.9 dynamic-slice_bitcast_fusion
  144.6 1.8 collective-permute-start.4
  146.4 20.0 %shard_map.29 = f32[256,1024]{1,0:T(8,128)} custom-call(bf16[2,2,152,4096]{3,2,1,0:T(8,128)(2,1)} %copy-done, bf16[2,2,8,4096]{3,2,1,0:T(8,128)(2,1)} %get-tuple-element.7.y_ref, bf16[256,8192]{1,0:T(8,128)(2,1)} %pad_maximum_fusion.1.tre_ref.tim_ref, bf16[256,8192]{1,0:T(8,128)(2,1)} %pad_maximum_fusion.1.tre_ref.tim_ref), custom_call_target="tpu_custom_call" | custom-call | tf_op jit(solution)/shard_map/pallas_call | solution.py:102
  166.4 1.9 dynamic-slice_bitcast_fusion.1
  168.4 20.1 %shard_map.28 = f32[256,1024]{1,0:T(8,128)} custom-call(bf16[2,2,152,4096]{3,2,1,0:T(8,128)(2,1)} %copy-done, bf16[2,2,8,4096]{3,2,1,0:T(8,128)(2,1)} %get-tuple-element.5.y_ref, bf16[256,8192]{1,0:T(8,128)(2,1)} %pad_maximum_fusion.1.tre_ref.tim_ref, bf16[256,8192]{1,0:T(8,128)(2,1)} %pad_maximum_fusion.1.tre_ref.tim_ref), custom_call_target="tpu_custom_call" | custom-call | tf_op jit(solution)/shard_map/pallas_call | solution.py:102
  188.5 1.2 dynamic-slice_bitcast_fusion.2
  189.7 0.6 collective-permute-start
  190.4 0.8 collective-permute-start.5
  191.3 0.8 collective-permute-start.3
  192.3 0.8 collective-permute-start.1
  193.1 5.2 %collective-permute-done.5 = f32[64,1024]{1,0:T(8,128)S(1)} collective-permute-done((f32[64,1024]{1,0:T(8,128)S(1)}, f32[64,1024]{1,0:T(8,128)S(1)}, u32[]{:S(2)}, u32[]{:S(2)}) %collective-permute-start.5) | collective-permute-done | bytes 262176 | tf_op jit(solution)/shard_map/ppermute | solution.py:133
  198.4 5.5 %collective-permute-done.3 = f32[64,1024]{1,0:T(8,128)S(1)} collective-permute-done((f32[64,1024]{1,0:T(8,128)S(1)}, f32[64,1024]{1,0:T(8,128)S(1)}, u32[]{:S(2)}, u32[]{:S(2)}) %collective-permute-start.3) | collective-permute-done | bytes 262176 | tf_op jit(solution)/shard_map/ppermute | solution.py:133
  204.0 5.5 %collective-permute-done.1 = f32[64,1024]{1,0:T(8,128)S(1)} collective-permute-done((f32[64,1024]{1,0:T(8,128)S(1)}, f32[64,1024]{1,0:T(8,128)S(1)}, u32[]{:S(2)}, u32[]{:S(2)}) %collective-permute-start.1) | collective-permute-done | bytes 262176 | tf_op jit(solution)/shard_map/ppermute | solution.py:133
  209.6 0.9 pad_maximum_fusion.2
  (30 shorter events, 0.6 us)
Async XLA Ops:
  19.3 83.4 %all-to-all-start = ((bf16[2,2,4864,128]{3,1,0,2:T(2,128)(2,1)}), bf16[2,2,4864,128]{3,1,0,2:T(2,128)(2,1)}, u32[]{:S(2)}, u32[]{:S(2)}) async-start(bf16[2,2,4864,128]{3,1,0,2:T(2,128)(2,1)} %bitcast.73), calls=%async_computation | async-start | bytes 9961472 | tf_op jit(solution)/shard_map/all_to_all | solution.py:151
  119.6 2.2 %copy-start = (bf16[2,2,152,4096]{3,2,1,0:T(8,128)(2,1)}, bf16[2,2,152,4096]{3,2,1,0:T(8,128)(2,1)S(1)}, u32[]{:S(2)}) copy-start(bf16[2,2,152,4096]{3,2,1,0:T(8,128)(2,1)S(1)} %divide_convert_fusion.x_ref) | copy-start | bytes 14942212
  144.6 45.7 %collective-permute-start.4 = (f32[2,64,1024]{2,1,0:T(8,128)}, f32[2,64,1024]{2,1,0:T(8,128)S(1)}, u32[]{:S(2)}, u32[]{:S(2)}) collective-permute-start(f32[2,64,1024]{2,1,0:T(8,128)} %dynamic-slice_bitcast_fusion), channel_id=1, source_target_pairs={{0,1},{1,0},{2,3},{3,2},{4,5},{5,4},{6,7},{7,6},{8,9},{9,8},{10,11... | collective-permute-start | bytes 1572872 | tf_op jit(solution)/shard_map/ppermute | solution.py:130
  168.4 22.8 %collective-permute-start.2 = (f32[2,64,1024]{2,1,0:T(8,128)}, f32[2,64,1024]{2,1,0:T(8,128)S(1)}, u32[]{:S(2)}, u32[]{:S(2)}) collective-permute-start(f32[2,64,1024]{2,1,0:T(8,128)} %dynamic-slice_bitcast_fusion.1), channel_id=1, source_target_pairs={{0,1},{1,0},{2,3},{3,2},{4,5},{5,4},{6,7},{7,6},{8,9},{9,8},{10,11... | collective-permute-start | bytes 1572872 | tf_op jit(solution)/shard_map/ppermute | solution.py:130
  168.4 21.9 %copy-start.2 = (f32[256,1024]{1,0:T(8,128)S(1)}, f32[256,1024]{1,0:T(8,128)}, u32[]{:S(2)}) copy-start(f32[256,1024]{1,0:T(8,128)} %shard_map.30) | copy-start | bytes 3145732
  168.4 22.8 %copy-start.1 = (f32[256,1024]{1,0:T(8,128)S(1)}, f32[256,1024]{1,0:T(8,128)}, u32[]{:S(2)}) copy-start(f32[256,1024]{1,0:T(8,128)} %shard_map.29) | copy-start | bytes 3145732
  188.5 3.6 %copy-start.3 = (f32[256,1024]{1,0:T(8,128)S(1)}, f32[256,1024]{1,0:T(8,128)}, u32[]{:S(2)}) copy-start(f32[256,1024]{1,0:T(8,128)} %shard_map.28) | copy-start | bytes 3145732
  189.7 2.5 %collective-permute-start = (f32[2,64,1024]{2,1,0:T(8,128)S(1)}, f32[2,64,1024]{2,1,0:T(8,128)S(1)}, u32[]{:S(2)}, u32[]{:S(2)}) collective-permute-start(f32[2,64,1024]{2,1,0:T(8,128)S(1)} %dynamic-slice_bitcast_fusion.2), channel_id=1, source_target_pairs={{0,1},{1,0},{2,3},{3,2},{4,5},{5,4},{6,7},{7,6},{8,9},{9,8},{10,11... | collective-permute-start | bytes 1572872 | tf_op jit(solution)/shard_map/ppermute | solution.py:130
  190.4 7.9 %collective-permute-start.5 = (f32[64,1024]{1,0:T(8,128)S(1)}, f32[64,1024]{1,0:T(8,128)S(1)}, u32[]{:S(2)}, u32[]{:S(2)}) collective-permute-start(f32[64,1024]{1,0:T(8,128)S(1)} %dynamic-slice_bitcast_fusion.3), channel_id=1, source_target_pairs={{0,2},{2,0},{1,3},{3,1},{4,6},{6,4},{5,7},{7,5},{8,10},{10,8},{9,1... | collective-permute-start | bytes 786440 | tf_op jit(solution)/shard_map/ppermute | solution.py:133
  191.3 12.6 %collective-permute-start.3 = (f32[64,1024]{1,0:T(8,128)S(1)}, f32[64,1024]{1,0:T(8,128)S(1)}, u32[]{:S(2)}, u32[]{:S(2)}) collective-permute-start(f32[64,1024]{1,0:T(8,128)S(1)} %dynamic-slice_bitcast_fusion.4), channel_id=1, source_target_pairs={{0,2},{2,0},{1,3},{3,1},{4,6},{6,4},{5,7},{7,5},{8,10},{10,8},{9,1... | collective-permute-start | bytes 786440 | tf_op jit(solution)/shard_map/ppermute | solution.py:133
  192.3 17.3 %collective-permute-start.1 = (f32[64,1024]{1,0:T(8,128)S(1)}, f32[64,1024]{1,0:T(8,128)S(1)}, u32[]{:S(2)}, u32[]{:S(2)}) collective-permute-start(f32[64,1024]{1,0:T(8,128)S(1)} %dynamic-slice_bitcast_fusion.5), channel_id=1, source_target_pairs={{0,2},{2,0},{1,3},{3,1},{4,6},{6,4},{5,7},{7,5},{8,10},{10,8},{9,1... | collective-permute-start | bytes 786440 | tf_op jit(solution)/shard_map/ppermute | solution.py:133

commit v4 on v3

--- a/solution.py
+++ b/solution.py
@@ -133,22 +133,8 @@
     return keep + lax.ppermute(send, "tm", perm=[(0, 2), (2, 0), (1, 3), (3, 1)])
 
 
-def local(spectra, src_ids):
-    hours_dev, stations, _, bins_dev = spectra.shape
-    shards = lax.axis_size("sta")
-    stations_dev = stations // shards
-    flat_ids = src_ids.reshape(-1)
-    count_all = flat_ids.shape[0]
-    by_part = jnp.transpose(spectra, (0, 2, 1, 3))
-    src_raw = jnp.take(by_part, flat_ids, axis=2)
-    chunks = by_part.reshape(hours_dev, 2, shards, stations_dev, bins_dev)
-    src_copies = jnp.broadcast_to(
-        src_raw[:, :, None], (hours_dev, 2, shards, count_all, bins_dev)
-    )
-    send = jnp.concatenate([chunks, src_copies], axis=3).reshape(
-        hours_dev, 2, shards * (stations_dev + count_all), bins_dev
-    )
-    joined = lax.all_to_all(send, "sta", split_axis=2, concat_axis=3, tiled=True)
+def whiten(joined):
+    hours_dev = joined.shape[0]
     values = joined.astype(jnp.float32)
     magnitude = jnp.sqrt(values[:, 0] * values[:, 0] + values[:, 1] * values[:, 1])
     block_num = BINS // BLOCK
@@ -164,16 +150,55 @@
     denom = jnp.einsum(
         "hrb,fb->hrf", level_mean + EPSILON, indicator, precision=lax.Precision.HIGHEST
     )
-    white = (values / denom[:, None]).astype(jnp.bfloat16)
+    return (values / denom[:, None]).astype(jnp.bfloat16)
+
+
+def local(spectra, src_ids):
+    hours_dev, stations, _, bins_dev = spectra.shape
+    shards = lax.axis_size("sta")
+    stations_dev = stations // shards
+    half = stations_dev // 2
+    flat_ids = src_ids.reshape(-1)
+    count_all = flat_ids.shape[0]
+    by_part = jnp.transpose(spectra, (0, 2, 1, 3))
+    src_raw = jnp.take(by_part, flat_ids, axis=2)
+    chunks = by_part.reshape(hours_dev, 2, shards, stations_dev, bins_dev)
+    src_copies = jnp.broadcast_to(
+        src_raw[:, :, None], (hours_dev, 2, shards, count_all, bins_dev)
+    )
+    send_a = jnp.concatenate([chunks[:, :, :, :half], src_copies], axis=3).reshape(
+        hours_dev, 2, shards * (half + count_all), bins_dev
+    )
+    send_b = chunks[:, :, :, half:].reshape(hours_dev, 2, shards * half, bins_dev)
+    joined_a = lax.all_to_all(send_a, "sta", split_axis=2, concat_axis=3, tiled=True)
+    send_b, joined_a = lax.optimization_barrier((send_b, joined_a))
+    joined_b = lax.all_to_all(send_b, "sta", split_axis=2, concat_axis=3, tiled=True)
+    white_a = whiten(joined_a)
     transform = make_table(hours_dev * lax.axis_size("tm"))
     row_count = transform.shape[0] // lax.axis_size("tm")
-    results = []
-    for step_no in range(ROUNDS):
-        first = stations_dev + step_no * NSRC
-        sources = white[:, :, first:first + NSRC]
-        projected = cross_project(white, sources, transform, stations_dev)
-        stacked = reduce_lags(projected)
-        results.append(stacked.reshape(row_count, NSRC, stations_dev))
+    sources = [
+        white_a[:, :, half + step_no * NSRC:half + (step_no + 1) * NSRC]
+        for step_no in range(ROUNDS)
+    ]
+    parts_a = [
+        reduce_lags(cross_project(white_a, sources[step_no], transform, half))
+        for step_no in range(ROUNDS)
+    ]
+    white_b = whiten(joined_b)
+    parts_b = [
+        reduce_lags(cross_project(white_b, sources[step_no], transform, half))
+        for step_no in range(ROUNDS)
+    ]
+    results = [
+        jnp.concatenate(
+            [
+                parts_a[step_no].reshape(row_count, NSRC, half),
+                parts_b[step_no].reshape(row_count, NSRC, half),
+            ],
+            axis=2,
+        )
+        for step_no in range(ROUNDS)
+    ]
     return jnp.stack(results)
 
 

time: 212 us -> 214 us (level)
  waiting for transfers between devices: 67.4 us -> 27.2 us
  Pallas kernels: 60.2 us -> 92.8 us
  local copies, waits for them, and re-layouts: 16.2 us -> 26.5 us
  starting transfers between devices: 16.3 us -> 26.2 us
  other arithmetic: 41.5 us -> 32.1 us
    all_to_all x1 -> x2, waiting for transfers between devices: 51.1 us -> 15.3 us  [the longest x1 15.3 us: local(): lax.all_to_all(send_a, 'sta', split_axis=2, concat_axis=3, tiled=True)]
    pallas_call x3 -> x6, Pallas kernels: 60.2 us -> 92.8 us  [cross_project(): pl.pallas_call(cross_project_kernel, grid=(steps,), in_specs=[pl.BlockSpe...]
    concatenate x1, other arithmetic: 14.4 us -> 4.26 us  [local(): jnp.concatenate([chunks[:, :, :, :half], src_copies], axis=3)]
    slice x1 -> x2, local copies, waits for them, and re-layouts: 0.91 us -> 7.51 us  [the longest x1 6.54 us: local(): chunks[:, :, :, :half]]
    all_to_all x1 -> x2, starting transfers between devices: 11.5 us -> 16.5 us  [the longest x1 11.2 us: local(): lax.all_to_all(send_a, 'sta', split_axis=2, concat_axis=3, tiled=True)]
    ppermute x3 -> x6, waiting for transfers between devices: 16.3 us -> 11.9 us  [reduce_lags(): lax.ppermute(send, 'tm', perm=[(0, 2), (2, 0), (1, 3), (3, 1)])]
    unnamed x11 -> x17, local copies, waits for them, and re-layouts: 2.38 us -> 5.59 us
    ppermute x3 -> x6, starting transfers between devices: 2.43 us -> 5.12 us  [reduce_lags(): lax.ppermute(send, 'tm', perm=[(0, 2), (2, 0), (1, 3), (3, 1)])]
  transfers between devices with their start and end apart: 7 -> 14, of which waited for: 4 -> 6; matrix products, arithmetic and copies ran while one was open for 12% -> 22% of each run, Pallas kernels for 19% -> 44%
where the time goes in v4:
time: 214 us; the launch traced here: 212 us
  Pallas kernels  92.8 us (43%)
  other arithmetic  32.1 us (15%)
  waiting for transfers between devices  27.2 us (13%)
  local copies, waits for them, and re-layouts  26.5 us (12%)
  starting transfers between devices  26.2 us (12%)
  matrix products  7.1 us (3%)
    pallas_call x6, Pallas kernels, cross_project(): pl.pallas_call(cross_project_kernel, grid=(steps,), in_specs=[pl.BlockSpe...  92.8 us
    another operation x1, other arithmetic  18.2 us
    all_to_all x1, waiting for transfers between devices, local(): lax.all_to_all(send_a, 'sta', split_axis=2, concat_axis=3, tiled=True)  15.3 us
    ppermute x6, waiting for transfers between devices, reduce_lags(): lax.ppermute(send, 'tm', perm=[(0, 2), (2, 0), (1, 3), (3, 1)])  11.9 us
    all_to_all x1, starting transfers between devices, local(): lax.all_to_all(send_a, 'sta', split_axis=2, concat_axis=3, tiled=True)  11.2 us
    slice x1, local copies, waits for them, and re-layouts, local(): chunks[:, :, :, :half]  6.54 us
    unnamed x17, local copies, waits for them, and re-layouts  5.59 us
    all_to_all x1, starting transfers between devices, local(): lax.all_to_all(send_b, 'sta', split_axis=2, concat_axis=3, tiled=True)  5.37 us
  transfers between devices with their start and end apart: 14, of which 6 were waited for; matrix products, arithmetic and copies ran while one was open for 22% of the time, Pallas kernels for 44%

profile of v4, /device:TPU:1, one launch (start us, length us, event | category | flops | bytes accessed | tf_op | source)
XLA Modules:
  0.0 212.2 jit_solution(11683860283982766329)
XLA Ops:
  1.5 6.5 %fusion.50 = (bf16[2,2,32,64,128]{4,1,3,2,0:T(2,128)(2,1)S(1)}, bf16[2,2,32,64,128]{4,1,3,2,0:T(2,128)(2,1)}) fusion(bf16[2,2,32,128,128]{4,1,3,2,0:T(2,128)(2,1)} %bitcast.106), kind=kLoop, calls=%fused_computation.101 | loop fusion | bytes 8388608 | tf_op jit(solution)/shard_map/slice | solution.py:169
  8.1 2.8 %gather_fusion = bf16[24,2,2,128]{3,2,1,0:T(2,128)(2,1)S(1)} fusion(bf16[2,2,4096,128]{3,1,2,0:T(2,128)(2,1)} %bitcast.107, s32[1024]{0:T(1024)S(1)} %pad_clamp_fusion), kind=kCustom, calls=%fused_computation | custom fusion | bytes 49248 | tf_op jit(solution)/shard_map/jit(_take)/gather | solution.py:164
  11.4 4.3 %pad_maximum_fusion.1 = bf16[2,2,32,88,128]{4,1,0,3,2:T(2,128)(2,1)} fusion(bf16[2,2,32,24,128]{4,1,0,3,2:T(2,128)(2,1)S(1)} %broadcast_in_dim.22, bf16[2,2,32,64,128]{4,1,3,2,0:T(2,128)(2,1)S(1)} %get-tuple-element.9), kind=kLoop, calls=%fused_computation.24 | loop fusion | flops 5767168 | bytes 5767168 | tf_op jit(solution)/shard_map/concatenate | solution.py:169
  15.7 11.2 %all-to-all-start = ((bf16[2,2,2816,128]{3,1,0,2:T(2,128)(2,1)}), bf16[2,2,2816,128]{3,1,0,2:T(2,128)(2,1)S(1)}, u32[]{:S(2)}, u32[]{:S(2)}) async-start(bf16[2,2,2816,128]{3,1,0,2:T(2,128)(2,1)} %bitcast.103), calls=%async_computation | async-start | bytes 5767168 | tf_op jit(solution)/shard_map/all_to_all | solution.py:173
  26.9 4.7 %copy.15 = bf16[2,2,32,64,128]{4,1,0,3,2:T(2,128)(2,1)} copy(bf16[2,2,32,64,128]{4,1,3,2,0:T(2,128)(2,1)} %get-tuple-element.10) | data formatting | bytes 4194304
  31.6 18.2 %multiply_convert_fusion.1 = (bf16[256,4096]{1,0:T(8,128)(2,1)S(1)}, bf16[256,4096]{1,0:T(8,128)(2,1)S(1)}) fusion(s32[256]{0:T(256)S(1)} %iota_add_fusion), kind=kLoop, calls=%fused_computation.13 | loop fusion | flops 19922944 | bytes 4195328 | tf_op jit(solution)/shard_map/convert.3
  49.8 2.4 %pad_maximum_fusion.tre_ref.tim_ref = bf16[256,8192]{1,0:T(8,128)(2,1)} fusion(bf16[256,4096]{1,0:T(8,128)(2,1)S(1)} %get-tuple-element.15, bf16[256,4096]{1,0:T(8,128)(2,1)S(1)} %get-tuple-element.14), kind=kLoop, calls=%fused_computation.9 | loop fusion | flops 8388608 | bytes 8388608 | tf_op jit(solution)/shard_map/concatenate | solution.py:46
  52.2 15.3 %all-to-all-done = bf16[2,2,2816,128]{3,1,0,2:T(2,128)(2,1)S(1)} async-done(((bf16[2,2,2816,128]{3,1,0,2:T(2,128)(2,1)}), bf16[2,2,2816,128]{3,1,0,2:T(2,128)(2,1)S(1)}, u32[]{:S(2)}, u32[]{:S(2)}) %all-to-all-start) | async-done | bytes 2883616 | tf_op jit(solution)/shard_map/all_to_all | solution.py:173
  68.7 5.4 %all-to-all-start.1 = ((bf16[2,2,2048,128]{3,1,0,2:T(2,128)(2,1)}), bf16[2,2,2048,128]{3,1,0,2:T(2,128)(2,1)}, u32[]{:S(2)}, u32[]{:S(2)}) async-start(bf16[2,2,2048,128]{3,1,0,2:T(2,128)(2,1)} %bitcast.105), calls=%async_computation.1 | async-start | bytes 4194304 | tf_op jit(solution)/shard_map/all_to_all | solution.py:175
  74.8 2.8 %fusion.9 = f32[2,88,64]{1,2,0:T(8,128)S(1)} fusion(f32[2,2,88,4096]{3,2,1,0:T(8,128)S(1)} %convert_element_type.33, s32[4096]{0:T(1024)S(1)} %get-tuple-element.16, s32[4096]{0:T(1024)S(1)} %get-tuple-element.17, pred[4096]{0:T(1024)(128)(4,1)S(1)} %fusion.38), kind=kOutput, calls=%fused_computation.22 | convolution fusion | flops 556335104 | bytes 5849088 | tf_op jit(solution)/shard_map/hrf,fb->hrb/dot_general | solution.py:145
  77.6 1.4 fusion.21
  79.0 1.4 divide_convert_fusion.x_ref
  82.2 15.5 %shard_map.32 = f32[256,512]{1,0:T(8,128)} custom-call(bf16[2,2,88,4096]{3,2,1,0:T(8,128)(2,1)} %copy-done, bf16[2,2,8,4096]{3,2,1,0:T(8,128)(2,1)} %get-tuple-element.12.y_ref, bf16[256,8192]{1,0:T(8,128)(2,1)} %pad_maximum_fusion.tre_ref.tim_ref, bf16[256,8192]{1,0:T(8,128)(2,1)} %pad_maximum_fusion.tre_ref.tim_ref), custom_call_target="tpu_custom_call" | custom-call | tf_op jit(solution)/shard_map/pallas_call | solution.py:102
  98.7 1.7 collective-permute-start.8
  100.4 15.5 %shard_map.30 = f32[256,512]{1,0:T(8,128)} custom-call(bf16[2,2,88,4096]{3,2,1,0:T(8,128)(2,1)} %copy-done, bf16[2,2,8,4096]{3,2,1,0:T(8,128)(2,1)} %get-tuple-element.13.y_ref, bf16[256,8192]{1,0:T(8,128)(2,1)} %pad_maximum_fusion.tre_ref.tim_ref, bf16[256,8192]{1,0:T(8,128)(2,1)} %pad_maximum_fusion.tre_ref.tim_ref), custom_call_target="tpu_custom_call" | custom-call | tf_op jit(solution)/shard_map/pallas_call | solution.py:102
  117.0 15.6 %shard_map.28 = f32[256,512]{1,0:T(8,128)} custom-call(bf16[2,2,88,4096]{3,2,1,0:T(8,128)(2,1)} %copy-done, bf16[2,2,8,4096]{3,2,1,0:T(8,128)(2,1)} %get-tuple-element.11.y_ref, bf16[256,8192]{1,0:T(8,128)(2,1)} %pad_maximum_fusion.tre_ref.tim_ref, bf16[256,8192]{1,0:T(8,128)(2,1)} %pad_maximum_fusion.tre_ref.tim_ref), custom_call_target="tpu_custom_call" | custom-call | tf_op jit(solution)/shard_map/pallas_call | solution.py:102
  135.8 1.0 bitcast_add_fusion.5
  136.8 1.0 collective-permute-start.1
  137.9 1.3 collective-permute-done.9
  139.2 2.8 %collective-permute-done.5 = f32[64,512]{1,0:T(8,128)S(1)} collective-permute-done((f32[64,512]{1,0:T(8,128)S(1)}, f32[64,512]{1,0:T(8,128)S(1)}, u32[]{:S(2)}, u32[]{:S(2)}) %collective-permute-start.5) | collective-permute-done | bytes 131104 | tf_op jit(solution)/shard_map/ppermute | solution.py:133
  142.0 1.9 copy.13
  144.4 1.9 fusion.14
  146.3 1.0 fusion.23
  147.3 1.9 divide_convert_fusion.1.x_ref
  149.2 15.4 %shard_map.33 = f32[256,512]{1,0:T(8,128)} custom-call(bf16[2,2,64,4096]{3,2,1,0:T(8,128)(2,1)} %divide_convert_fusion.1.x_ref, bf16[2,2,8,4096]{3,2,1,0:T(8,128)(2,1)} %get-tuple-element.12.y_ref, bf16[256,8192]{1,0:T(8,128)(2,1)} %pad_maximum_fusion.tre_ref.tim_ref, bf16[256,8192]{1,0:T(8,128)(2,1)} %pad_maximum_fusion.tre_ref.tim_ref), custom_call_target="tpu_custom_call" | custom-call | tf_op jit(solution)/shard_map/pallas_call | solution.py:102
  165.5 1.5 collective-permute-start.10
  167.4 15.4 %shard_map.31 = f32[256,512]{1,0:T(8,128)} custom-call(bf16[2,2,64,4096]{3,2,1,0:T(8,128)(2,1)} %divide_convert_fusion.1.x_ref, bf16[2,2,8,4096]{3,2,1,0:T(8,128)(2,1)} %get-tuple-element.13.y_ref, bf16[256,8192]{1,0:T(8,128)(2,1)} %pad_maximum_fusion.tre_ref.tim_ref, bf16[256,8192]{1,0:T(8,128)(2,1)} %pad_maximum_fusion.tre_ref.tim_ref), custom_call_target="tpu_custom_call" | custom-call | tf_op jit(solution)/shard_map/pallas_call | solution.py:102
  182.8 15.5 %shard_map.29 = f32[256,512]{1,0:T(8,128)} custom-call(bf16[2,2,64,4096]{3,2,1,0:T(8,128)(2,1)} %divide_convert_fusion.1.x_ref, bf16[2,2,8,4096]{3,2,1,0:T(8,128)(2,1)} %get-tuple-element.11.y_ref, bf16[256,8192]{1,0:T(8,128)(2,1)} %pad_maximum_fusion.tre_ref.tim_ref, bf16[256,8192]{1,0:T(8,128)(2,1)} %pad_maximum_fusion.tre_ref.tim_ref), custom_call_target="tpu_custom_call" | custom-call | tf_op jit(solution)/shard_map/pallas_call | solution.py:102
  198.5 1.0 dynamic-slice_bitcast_fusion.4
  202.7 2.5 %collective-permute-done.11 = f32[64,512]{1,0:T(8,128)S(1)} collective-permute-done((f32[64,512]{1,0:T(8,128)S(1)}, f32[64,512]{1,0:T(8,128)S(1)}, u32[]{:S(2)}, u32[]{:S(2)}) %collective-permute-start.11) | collective-permute-done | bytes 131104 | tf_op jit(solution)/shard_map/ppermute | solution.py:133
  205.3 2.7 %collective-permute-done.7 = f32[64,512]{1,0:T(8,128)S(1)} collective-permute-done((f32[64,512]{1,0:T(8,128)S(1)}, f32[64,512]{1,0:T(8,128)S(1)}, u32[]{:S(2)}, u32[]{:S(2)}) %collective-permute-start.7) | collective-permute-done | bytes 131104 | tf_op jit(solution)/shard_map/ppermute | solution.py:133
  208.1 2.7 %collective-permute-done.3 = f32[64,512]{1,0:T(8,128)S(1)} collective-permute-done((f32[64,512]{1,0:T(8,128)S(1)}, f32[64,512]{1,0:T(8,128)S(1)}, u32[]{:S(2)}, u32[]{:S(2)}) %collective-permute-start.3) | collective-permute-done | bytes 131104 | tf_op jit(solution)/shard_map/ppermute | solution.py:133
  (80 shorter events, 17.9 us)
Async XLA Ops:
  15.7 51.8 %all-to-all-start = ((bf16[2,2,2816,128]{3,1,0,2:T(2,128)(2,1)}), bf16[2,2,2816,128]{3,1,0,2:T(2,128)(2,1)S(1)}, u32[]{:S(2)}, u32[]{:S(2)}) async-start(bf16[2,2,2816,128]{3,1,0,2:T(2,128)(2,1)} %bitcast.103), calls=%async_computation | async-start | bytes 5767168 | tf_op jit(solution)/shard_map/all_to_all | solution.py:173
  68.7 6.1 %copy-start.1 = (bf16[2,2,32,11,8,128]{5,4,2,3,1,0:T(8,128)(2,1)}, bf16[2,2,32,11,8,128]{5,4,2,3,1,0:T(8,128)(2,1)S(1)}, u32[]{:S(2)}) copy-start(bf16[2,2,32,11,8,128]{5,4,2,3,1,0:T(8,128)(2,1)S(1)} %copy.25) | copy-start | bytes 8650756
  68.7 73.3 %all-to-all-start.1 = ((bf16[2,2,2048,128]{3,1,0,2:T(2,128)(2,1)}), bf16[2,2,2048,128]{3,1,0,2:T(2,128)(2,1)}, u32[]{:S(2)}, u32[]{:S(2)}) async-start(bf16[2,2,2048,128]{3,1,0,2:T(2,128)(2,1)} %bitcast.105), calls=%async_computation.1 | async-start | bytes 4194304 | tf_op jit(solution)/shard_map/all_to_all | solution.py:175
  74.8 4.2 %copy-start.2 = (bf16[2,2,32,11,8,128]{5,4,2,3,1,0:T(8,128)(2,1)S(1)}, bf16[2,2,32,11,8,128]{5,4,2,3,1,0:T(8,128)(2,1)}, u32[]{:S(2)}) copy-start(bf16[2,2,32,11,8,128]{5,4,2,3,1,0:T(8,128)(2,1)} %copy-done.1) | copy-start | bytes 8650756
  80.4 1.8 copy-start
  98.7 35.4 %collective-permute-start.8 = (f32[2,64,512]{2,1,0:T(8,128)S(1)}, f32[2,64,512]{2,1,0:T(8,128)S(1)}, u32[]{:S(2)}, u32[]{:S(2)}) collective-permute-start(f32[2,64,512]{2,1,0:T(8,128)S(1)} %dynamic-slice_bitcast_fusion.1), channel_id=1, source_target_pairs={{0,1},{1,0},{2,3},{3,2},{4,5},{5,4},{6,7},{7,6},{8,9},{9,8},{10,11... | collective-permute-start | bytes 786440 | tf_op jit(solution)/shard_map/ppermute | solution.py:130
  116.8 18.1 %collective-permute-start.4 = (f32[2,64,512]{2,1,0:T(8,128)S(1)}, f32[2,64,512]{2,1,0:T(8,128)S(1)}, u32[]{:S(2)}, u32[]{:S(2)}) collective-permute-start(f32[2,64,512]{2,1,0:T(8,128)S(1)} %dynamic-slice_bitcast_fusion.3), channel_id=1, source_target_pairs={{0,1},{1,0},{2,3},{3,2},{4,5},{5,4},{6,7},{7,6},{8,9},{9,8},{10,11... | collective-permute-start | bytes 786440 | tf_op jit(solution)/shard_map/ppermute | solution.py:130
  117.0 17.1 %copy-start.3 = (f32[256,512]{1,0:T(8,128)S(1)}, f32[256,512]{1,0:T(8,128)}, u32[]{:S(2)}) copy-start(f32[256,512]{1,0:T(8,128)} %shard_map.32) | copy-start | bytes 1572868
  117.0 18.0 %copy-start.7 = (f32[256,512]{1,0:T(8,128)S(1)}, f32[256,512]{1,0:T(8,128)}, u32[]{:S(2)}) copy-start(f32[256,512]{1,0:T(8,128)} %shard_map.30) | copy-start | bytes 1572868
  133.5 2.3 %collective-permute-start = (f32[2,64,512]{2,1,0:T(8,128)S(1)}, f32[2,64,512]{2,1,0:T(8,128)S(1)}, u32[]{:S(2)}, u32[]{:S(2)}) collective-permute-start(f32[2,64,512]{2,1,0:T(8,128)S(1)} %dynamic-slice_bitcast_fusion.5), channel_id=1, source_target_pairs={{0,1},{1,0},{2,3},{3,2},{4,5},{5,4},{6,7},{7,6},{8,9},{9,8},{10,11... | collective-permute-start | bytes 786440 | tf_op jit(solution)/shard_map/ppermute | solution.py:130
  134.1 5.1 %collective-permute-start.9 = (f32[64,512]{1,0:T(8,128)S(1)}, f32[64,512]{1,0:T(8,128)S(1)}, u32[]{:S(2)}, u32[]{:S(2)}) collective-permute-start(f32[64,512]{1,0:T(8,128)S(1)} %dynamic-slice_bitcast_fusion.7), channel_id=1, source_target_pairs={{0,2},{2,0},{1,3},{3,1},{4,6},{6,4},{5,7},{7,5},{8,10},{10,8},{9,1... | collective-permute-start | bytes 393224 | tf_op jit(solution)/shard_map/ppermute | solution.py:133
  135.0 7.0 %collective-permute-start.5 = (f32[64,512]{1,0:T(8,128)S(1)}, f32[64,512]{1,0:T(8,128)S(1)}, u32[]{:S(2)}, u32[]{:S(2)}) collective-permute-start(f32[64,512]{1,0:T(8,128)S(1)} %dynamic-slice_bitcast_fusion.9), channel_id=1, source_target_pairs={{0,2},{2,0},{1,3},{3,1},{4,6},{6,4},{5,7},{7,5},{8,10},{10,8},{9,1... | collective-permute-start | bytes 393224 | tf_op jit(solution)/shard_map/ppermute | solution.py:133
  136.8 30.2 %collective-permute-start.1 = (f32[64,512]{1,0:T(8,128)S(1)}, f32[64,512]{1,0:T(8,128)S(1)}, u32[]{:S(2)}, u32[]{:S(2)}) collective-permute-start(f32[64,512]{1,0:T(8,128)S(1)} %dynamic-slice_bitcast_fusion.11), channel_id=1, source_target_pairs={{0,2},{2,0},{1,3},{3,1},{4,6},{6,4},{5,7},{7,5},{8,10},{10,8},{9,1... | collective-permute-start | bytes 393224 | tf_op jit(solution)/shard_map/ppermute | solution.py:133
  165.5 34.4 %collective-permute-start.10 = (f32[2,64,512]{2,1,0:T(8,128)S(1)}, f32[2,64,512]{2,1,0:T(8,128)S(1)}, u32[]{:S(2)}, u32[]{:S(2)}) collective-permute-start(f32[2,64,512]{2,1,0:T(8,128)S(1)} %dynamic-slice_bitcast_fusion), channel_id=1, source_target_pairs={{0,1},{1,0},{2,3},{3,2},{4,5},{5,4},{6,7},{7,6},{8,9},{9,8},{10,11... | collective-permute-start | bytes 786440 | tf_op jit(solution)/shard_map/ppermute | solution.py:130
  182.8 15.5 %copy-start.6 = (f32[256,512]{1,0:T(8,128)S(1)}, f32[256,512]{1,0:T(8,128)}, u32[]{:S(2)}) copy-start(f32[256,512]{1,0:T(8,128)} %shard_map.31) | copy-start | bytes 1572868
  182.8 17.2 %copy-start.5 = (f32[256,512]{1,0:T(8,128)S(1)}, f32[256,512]{1,0:T(8,128)}, u32[]{:S(2)}) copy-start(f32[256,512]{1,0:T(8,128)} %shard_map.33) | copy-start | bytes 1572868
  198.3 3.5 %copy-start.4 = (f32[256,512]{1,0:T(8,128)S(1)}, f32[256,512]{1,0:T(8,128)}, u32[]{:S(2)}) copy-start(f32[256,512]{1,0:T(8,128)} %shard_map.29) | copy-start | bytes 1572868
  198.3 2.5 %collective-permute-start.6 = (f32[2,64,512]{2,1,0:T(8,128)S(1)}, f32[2,64,512]{2,1,0:T(8,128)S(1)}, u32[]{:S(2)}, u32[]{:S(2)}) collective-permute-start(f32[2,64,512]{2,1,0:T(8,128)S(1)} %dynamic-slice_bitcast_fusion.2), channel_id=1, source_target_pairs={{0,1},{1,0},{2,3},{3,2},{4,5},{5,4},{6,7},{7,6},{8,9},{9,8},{10,11... | collective-permute-start | bytes 786440 | tf_op jit(solution)/shard_map/ppermute | solution.py:130
  199.5 2.3 %collective-permute-start.2 = (f32[2,64,512]{2,1,0:T(8,128)S(1)}, f32[2,64,512]{2,1,0:T(8,128)S(1)}, u32[]{:S(2)}, u32[]{:S(2)}) collective-permute-start(f32[2,64,512]{2,1,0:T(8,128)S(1)} %dynamic-slice_bitcast_fusion.4), channel_id=1, source_target_pairs={{0,1},{1,0},{2,3},{3,2},{4,5},{5,4},{6,7},{7,6},{8,9},{9,8},{10,11... | collective-permute-start | bytes 786440 | tf_op jit(solution)/shard_map/ppermute | solution.py:130
  200.1 5.1 %collective-permute-start.11 = (f32[64,512]{1,0:T(8,128)S(1)}, f32[64,512]{1,0:T(8,128)S(1)}, u32[]{:S(2)}, u32[]{:S(2)}) collective-permute-start(f32[64,512]{1,0:T(8,128)S(1)} %dynamic-slice_bitcast_fusion.6), channel_id=1, source_target_pairs={{0,2},{2,0},{1,3},{3,1},{4,6},{6,4},{5,7},{7,5},{8,10},{10,8},{9,1... | collective-permute-start | bytes 393224 | tf_op jit(solution)/shard_map/ppermute | solution.py:133
  201.0 7.0 %collective-permute-start.7 = (f32[64,512]{1,0:T(8,128)S(1)}, f32[64,512]{1,0:T(8,128)S(1)}, u32[]{:S(2)}, u32[]{:S(2)}) collective-permute-start(f32[64,512]{1,0:T(8,128)S(1)} %dynamic-slice_bitcast_fusion.8), channel_id=1, source_target_pairs={{0,2},{2,0},{1,3},{3,1},{4,6},{6,4},{5,7},{7,5},{8,10},{10,8},{9,1... | collective-permute-start | bytes 393224 | tf_op jit(solution)/shard_map/ppermute | solution.py:133
  201.8 8.9 %collective-permute-start.3 = (f32[64,512]{1,0:T(8,128)S(1)}, f32[64,512]{1,0:T(8,128)S(1)}, u32[]{:S(2)}, u32[]{:S(2)}) collective-permute-start(f32[64,512]{1,0:T(8,128)S(1)} %dynamic-slice_bitcast_fusion.10), channel_id=1, source_target_pairs={{0,2},{2,0},{1,3},{3,1},{4,6},{6,4},{5,7},{7,5},{8,10},{10,8},{9,1... | collective-permute-start | bytes 393224 | tf_op jit(solution)/shard_map/ppermute | solution.py:133

commit v5 on v4

--- a/solution.py
+++ b/solution.py
@@ -89,9 +89,12 @@
 
     lax.fori_loop(0, stations // ROWS, body, 0)
     dims = (((1,), (1,)), ((), ()))
-    out_ref[...] += lax.dot_general(
-        tre_ref[...], cre_ref[...], dims, preferred_element_type=jnp.float32
-    ) + lax.dot_general(tim_ref[...], cim_ref[...], dims, preferred_element_type=jnp.float32)
+    span = NSRC * stations
+    for rnd in range(count_src // NSRC):
+        cols = pl.ds(rnd * span, span)
+        out_ref[:, cols] += lax.dot_general(
+            tre_ref[...], cre_ref[cols, :], dims, preferred_element_type=jnp.float32
+        ) + lax.dot_general(tim_ref[...], cim_ref[cols, :], dims, preferred_element_type=jnp.float32)
 
 
 def cross_project(receivers, sources, transform, stations):
@@ -176,30 +179,18 @@
     white_a = whiten(joined_a)
     transform = make_table(hours_dev * lax.axis_size("tm"))
     row_count = transform.shape[0] // lax.axis_size("tm")
-    sources = [
-        white_a[:, :, half + step_no * NSRC:half + (step_no + 1) * NSRC]
-        for step_no in range(ROUNDS)
-    ]
-    parts_a = [
-        reduce_lags(cross_project(white_a, sources[step_no], transform, half))
-        for step_no in range(ROUNDS)
-    ]
+    sources = white_a[:, :, half:half + count_all]
+    part_a = reduce_lags(cross_project(white_a, sources, transform, half))
     white_b = whiten(joined_b)
-    parts_b = [
-        reduce_lags(cross_project(white_b, sources[step_no], transform, half))
-        for step_no in range(ROUNDS)
-    ]
-    results = [
-        jnp.concatenate(
-            [
-                parts_a[step_no].reshape(row_count, NSRC, half),
-                parts_b[step_no].reshape(row_count, NSRC, half),
-            ],
-            axis=2,
-        )
-        for step_no in range(ROUNDS)
-    ]
-    return jnp.stack(results)
+    part_b = reduce_lags(cross_project(white_b, sources, transform, half))
+    both = jnp.concatenate(
+        [
+            part_a.reshape(row_count, ROUNDS, NSRC, half),
+            part_b.reshape(row_count, ROUNDS, NSRC, half),
+        ],
+        axis=3,
+    )
+    return jnp.transpose(both, (1, 0, 2, 3))
 
 
 def solution(mesh):

time: 214 us -> 172 us (0.80)
  Pallas kernels: 92.8 us -> 54 us
  starting transfers between devices: 26.2 us -> 19.8 us
  waiting for transfers between devices: 27.2 us -> 30.9 us
    pallas_call x6 -> x2, Pallas kernels: 92.8 us -> 54 us  [cross_project(): pl.pallas_call(cross_project_kernel, grid=(steps,), in_specs=[pl.BlockSpe...]
    ppermute x6 -> x2, starting transfers between devices: 5.12 us -> 1.64 us  [reduce_lags(): lax.ppermute(send, 'tm', perm=[(0, 2), (2, 0), (1, 3), (3, 1)])]
    ppermute x6 -> x2, waiting for transfers between devices: 11.9 us -> 15 us  [reduce_lags(): lax.ppermute(send, 'tm', perm=[(0, 2), (2, 0), (1, 3), (3, 1)])]
    ppermute x6 -> x2, starting transfers between devices: 4.56 us -> 1.64 us  [reduce_lags(): lax.ppermute(send, 'tm', perm=[(0, 1), (1, 0), (2, 3), (3, 2)])]
    another operation x5 -> x1, other arithmetic: 19.6 us -> 18.2 us
    unnamed x17 -> x7, local copies, waits for them, and re-layouts: 5.59 us -> 6.28 us
    squeeze x6 -> x2, local copies, waits for them, and re-layouts: 4.89 us -> 4.27 us  [reduce_lags(): send = lax.dynamic_index_in_dim(blocks, 1 - core, axis=1, keepdims=False)]
  transfers between devices with their start and end apart: 14 -> 6, of which waited for: 6 -> 4; matrix products, arithmetic and copies ran while one was open for 22% -> 27% of each run, Pallas kernels for 44% -> 32%
where the time goes in v5:
time: 172 us; the launch traced here: 171 us
  Pallas kernels  54 us (31%)
  other arithmetic  32.2 us (19%)
  waiting for transfers between devices  30.9 us (18%)
  local copies, waits for them, and re-layouts  27.2 us (16%)
  starting transfers between devices  19.8 us (12%)
  matrix products  7.11 us (4%)
    pallas_call x2, Pallas kernels, cross_project(): pl.pallas_call(cross_project_kernel, grid=(steps,), in_specs=[pl.BlockSpe...  54 us
    another operation x1, other arithmetic  18.2 us
    all_to_all x1, waiting for transfers between devices, local(): lax.all_to_all(send_a, 'sta', split_axis=2, concat_axis=3, tiled=True)  15.3 us
    ppermute x2, waiting for transfers between devices, reduce_lags(): lax.ppermute(send, 'tm', perm=[(0, 2), (2, 0), (1, 3), (3, 1)])  15 us
    all_to_all x1, starting transfers between devices, local(): lax.all_to_all(send_a, 'sta', split_axis=2, concat_axis=3, tiled=True)  11.2 us
    slice x1, local copies, waits for them, and re-layouts, local(): chunks[:, :, :, :half]  6.56 us
    unnamed x7, local copies, waits for them, and re-layouts  6.28 us
    all_to_all x1, starting transfers between devices, local(): lax.all_to_all(send_b, 'sta', split_axis=2, concat_axis=3, tiled=True)  5.37 us
  transfers between devices with their start and end apart: 6, of which 4 were waited for; matrix products, arithmetic and copies ran while one was open for 27% of the time, Pallas kernels for 32%

profile of v5, /device:TPU:1, one launch (start us, length us, event | category | flops | bytes accessed | tf_op | source)
XLA Modules:
  0.0 171.4 jit_solution(14386211161150359619)
XLA Ops:
  0.8 0.8 reshape.83
  1.5 6.6 %fusion.50 = (bf16[2,2,32,64,128]{4,1,3,2,0:T(2,128)(2,1)S(1)}, bf16[2,2,32,64,128]{4,1,3,2,0:T(2,128)(2,1)}) fusion(bf16[2,2,32,128,128]{4,1,3,2,0:T(2,128)(2,1)} %bitcast.70), kind=kLoop, calls=%fused_computation.82 | loop fusion | bytes 8388608 | tf_op jit(solution)/shard_map/slice | solution.py:172
  8.1 2.8 %gather_fusion = bf16[24,2,2,128]{3,2,1,0:T(2,128)(2,1)S(1)} fusion(bf16[2,2,4096,128]{3,1,2,0:T(2,128)(2,1)} %bitcast.71, s32[1024]{0:T(1024)S(1)} %pad_clamp_fusion), kind=kCustom, calls=%fused_computation | custom fusion | bytes 49248 | tf_op jit(solution)/shard_map/jit(_take)/gather | solution.py:167
  11.4 4.3 %pad_maximum_fusion.1 = bf16[2,2,32,88,128]{4,1,0,3,2:T(2,128)(2,1)} fusion(bf16[2,2,32,24,128]{4,1,0,3,2:T(2,128)(2,1)S(1)} %broadcast_in_dim.22, bf16[2,2,32,64,128]{4,1,3,2,0:T(2,128)(2,1)S(1)} %get-tuple-element.9), kind=kLoop, calls=%fused_computation.24 | loop fusion | flops 5767168 | bytes 5767168 | tf_op jit(solution)/shard_map/concatenate | solution.py:172
  15.7 11.2 %all-to-all-start = ((bf16[2,2,2816,128]{3,1,0,2:T(2,128)(2,1)}), bf16[2,2,2816,128]{3,1,0,2:T(2,128)(2,1)S(1)}, u32[]{:S(2)}, u32[]{:S(2)}) async-start(bf16[2,2,2816,128]{3,1,0,2:T(2,128)(2,1)} %bitcast.63), calls=%async_computation | async-start | bytes 5767168 | tf_op jit(solution)/shard_map/all_to_all | solution.py:176
  26.9 4.7 %copy.17 = bf16[2,2,32,64,128]{4,1,0,3,2:T(2,128)(2,1)} copy(bf16[2,2,32,64,128]{4,1,3,2,0:T(2,128)(2,1)} %get-tuple-element.10) | data formatting | bytes 4194304
  31.6 18.2 %multiply_convert_fusion.1 = (bf16[256,4096]{1,0:T(8,128)(2,1)S(1)}, bf16[256,4096]{1,0:T(8,128)(2,1)S(1)}) fusion(s32[256]{0:T(256)S(1)} %iota_add_fusion), kind=kLoop, calls=%fused_computation.13 | loop fusion | flops 19922944 | bytes 4195328 | tf_op jit(solution)/shard_map/convert.3
  49.8 2.4 %pad_maximum_fusion.tre_ref.tim_ref = bf16[256,8192]{1,0:T(8,128)(2,1)} fusion(bf16[256,4096]{1,0:T(8,128)(2,1)S(1)} %get-tuple-element.12, bf16[256,4096]{1,0:T(8,128)(2,1)S(1)} %get-tuple-element.11), kind=kLoop, calls=%fused_computation.9 | loop fusion | flops 8388608 | bytes 8388608 | tf_op jit(solution)/shard_map/concatenate | solution.py:46
  52.2 15.3 %all-to-all-done = bf16[2,2,2816,128]{3,1,0,2:T(2,128)(2,1)S(1)} async-done(((bf16[2,2,2816,128]{3,1,0,2:T(2,128)(2,1)}), bf16[2,2,2816,128]{3,1,0,2:T(2,128)(2,1)S(1)}, u32[]{:S(2)}, u32[]{:S(2)}) %all-to-all-start) | async-done | bytes 2883616 | tf_op jit(solution)/shard_map/all_to_all | solution.py:176
  67.9 0.8 copy.27
  68.7 5.4 %all-to-all-start.1 = ((bf16[2,2,2048,128]{3,1,0,2:T(2,128)(2,1)}), bf16[2,2,2048,128]{3,1,0,2:T(2,128)(2,1)}, u32[]{:S(2)}, u32[]{:S(2)}) async-start(bf16[2,2,2048,128]{3,1,0,2:T(2,128)(2,1)} %bitcast.65), calls=%async_computation.1 | async-start | bytes 4194304 | tf_op jit(solution)/shard_map/all_to_all | solution.py:178
  74.8 2.8 %fusion.9 = f32[2,88,64]{1,2,0:T(8,128)S(1)} fusion(f32[2,2,88,4096]{3,2,1,0:T(8,128)S(1)} %convert_element_type.33, s32[4096]{0:T(1024)S(1)} %get-tuple-element.13, s32[4096]{0:T(1024)S(1)} %get-tuple-element.14, pred[4096]{0:T(1024)(128)(4,1)S(1)} %fusion.38), kind=kOutput, calls=%fused_computation.22 | convolution fusion | flops 556335104 | bytes 5849088 | tf_op jit(solution)/shard_map/hrf,fb->hrb/dot_general | solution.py:148
  77.6 1.4 fusion.21
  79.0 1.4 divide_convert_fusion.x_ref
  80.4 1.6 copy-done
  82.0 0.9 slice.56.y_ref
  82.9 27.1 %shard_map.28 = f32[256,1536]{1,0:T(8,128)} custom-call(bf16[2,2,88,4096]{3,2,1,0:T(8,128)(2,1)} %copy-done, bf16[2,2,24,4096]{3,2,1,0:T(8,128)(2,1)} %slice.56.y_ref, bf16[256,8192]{1,0:T(8,128)(2,1)} %pad_maximum_fusion.tre_ref.tim_ref, bf16[256,8192]{1,0:T(8,128)(2,1)} %pad_maximum_fusion.tre_ref.tim_ref), custom_call_target="tpu_custom_call" | custom-call | tf_op jit(solution)/shard_map/pallas_call | solution.py:105
  110.0 2.1 %dynamic-slice_bitcast_fusion.1 = f32[2,64,1536]{2,1,0:T(8,128)} fusion(f32[2,2,64,1536]{3,2,1,0:T(8,128)} %bitcast.68, s32[]{:T(128)S(6)} %select_n.83), kind=kLoop, calls=%fused_computation.37 | loop fusion | bytes 1572868 | tf_op jit(solution)/shard_map/jit(dynamic_index_in_dim)/squeeze | solution.py:132
  112.1 1.6 collective-permute-start
  113.7 1.9 %copy.14 = bf16[2,2,2048,128]{3,2,1,0:T(8,128)(2,1)S(1)} copy(bf16[2,2,2048,128]{3,1,0,2:T(2,128)(2,1)} %all-to-all-done.1) | data formatting | bytes 4194304 | tf_op jit(solution)/shard_map/all_to_all | solution.py:178
  116.1 1.9 %fusion.14 = f32[2,64,64]{2,1,0:T(8,128)S(1)} fusion(f32[2,2,64,4096]{3,2,1,0:T(8,128)S(1)} %copy_bitcast_fusion, s32[4096]{0:T(1024)S(1)} %get-tuple-element.13, s32[4096]{0:T(1024)S(1)} %get-tuple-element.14, pred[4096]{0:T(1024)(128)(4,1)S(1)} %fusion.38), kind=kOutput, calls=%fused_computation.29 | convolution fusion | flops 404750336 | bytes 4263936 | tf_op jit(solution)/shard_map/hrf,fb->hrb/dot_general | solution.py:148
  118.0 1.0 fusion.23
  119.0 1.8 %divide_convert_fusion.1.x_ref = bf16[2,2,64,4096]{3,2,1,0:T(8,128)(2,1)} fusion(f32[2,64,4096]{2,1,0:T(8,128)S(1)} %fusion.23, bf16[2,2,32,64,128]{4,3,2,1,0:T(8,128)(2,1)S(1)} %bitcast.62), kind=kLoop, calls=%fused_computation.11 | loop fusion | flops 3145728 | bytes 6291456 | tf_op jit(solution)/shard_map/convert_element_type | solution.py:156
  120.9 26.9 %shard_map.29 = f32[256,1536]{1,0:T(8,128)} custom-call(bf16[2,2,64,4096]{3,2,1,0:T(8,128)(2,1)} %divide_convert_fusion.1.x_ref, bf16[2,2,24,4096]{3,2,1,0:T(8,128)(2,1)} %slice.56.y_ref, bf16[256,8192]{1,0:T(8,128)(2,1)} %pad_maximum_fusion.tre_ref.tim_ref, bf16[256,8192]{1,0:T(8,128)(2,1)} %pad_maximum_fusion.tre_ref.tim_ref), custom_call_target="tpu_custom_call" | custom-call | tf_op jit(solution)/shard_map/pallas_call | solution.py:105
  147.8 2.2 %dynamic-slice_bitcast_fusion = f32[2,64,1536]{2,1,0:T(8,128)} fusion(f32[2,2,64,1536]{3,2,1,0:T(8,128)} %bitcast.66, s32[]{:T(128)S(6)} %select_n.83), kind=kLoop, calls=%fused_computation.36 | loop fusion | bytes 1572868 | tf_op jit(solution)/shard_map/jit(dynamic_index_in_dim)/squeeze | solution.py:132
  150.0 1.2 bitcast_add_fusion.1
  151.3 0.8 collective-permute-start.1
  152.6 1.2 bitcast_add_fusion
  153.9 0.8 collective-permute-start.3
  154.7 6.8 %collective-permute-done.1 = f32[64,1536]{1,0:T(8,128)S(1)} collective-permute-done((f32[64,1536]{1,0:T(8,128)S(1)}, f32[64,1536]{1,0:T(8,128)S(1)}, u32[]{:S(2)}, u32[]{:S(2)}) %collective-permute-start.1) | collective-permute-done | bytes 393248 | tf_op jit(solution)/shard_map/ppermute | solution.py:136
  161.8 8.2 %collective-permute-done.3 = f32[64,1536]{1,0:T(8,128)S(1)} collective-permute-done((f32[64,1536]{1,0:T(8,128)S(1)}, f32[64,1536]{1,0:T(8,128)S(1)}, u32[]{:S(2)}, u32[]{:S(2)}) %collective-permute-start.3) | collective-permute-done | bytes 393248 | tf_op jit(solution)/shard_map/ppermute | solution.py:136
  170.5 0.9 copy.16
  (28 shorter events, 4.2 us)
Async XLA Ops:
  15.7 51.8 %all-to-all-start = ((bf16[2,2,2816,128]{3,1,0,2:T(2,128)(2,1)}), bf16[2,2,2816,128]{3,1,0,2:T(2,128)(2,1)S(1)}, u32[]{:S(2)}, u32[]{:S(2)}) async-start(bf16[2,2,2816,128]{3,1,0,2:T(2,128)(2,1)} %bitcast.63), calls=%async_computation | async-start | bytes 5767168 | tf_op jit(solution)/shard_map/all_to_all | solution.py:176
  68.7 45.0 %all-to-all-start.1 = ((bf16[2,2,2048,128]{3,1,0,2:T(2,128)(2,1)}), bf16[2,2,2048,128]{3,1,0,2:T(2,128)(2,1)}, u32[]{:S(2)}, u32[]{:S(2)}) async-start(bf16[2,2,2048,128]{3,1,0,2:T(2,128)(2,1)} %bitcast.65), calls=%async_computation.1 | async-start | bytes 4194304 | tf_op jit(solution)/shard_map/all_to_all | solution.py:178
  80.4 1.6 copy-start
  112.1 37.9 %collective-permute-start = (f32[2,64,1536]{2,1,0:T(8,128)}, f32[2,64,1536]{2,1,0:T(8,128)}, u32[]{:S(2)}, u32[]{:S(2)}) collective-permute-start(f32[2,64,1536]{2,1,0:T(8,128)} %dynamic-slice_bitcast_fusion.1), channel_id=1, source_target_pairs={{0,1},{1,0},{2,3},{3,2},{4,5},{5,4},{6,7},{7,6},{8,9},{9,8},{10,11... | collective-permute-start | bytes 2359304 | tf_op jit(solution)/shard_map/ppermute | solution.py:133
  120.9 29.1 %copy-start.2 = (f32[256,1536]{1,0:T(8,128)S(1)}, f32[256,1536]{1,0:T(8,128)}, u32[]{:S(2)}) copy-start(f32[256,1536]{1,0:T(8,128)} %shard_map.28) | copy-start | bytes 4718596
  147.8 4.8 %copy-start.1 = (f32[256,1536]{1,0:T(8,128)S(1)}, f32[256,1536]{1,0:T(8,128)}, u32[]{:S(2)}) copy-start(f32[256,1536]{1,0:T(8,128)} %shard_map.29) | copy-start | bytes 4718596
  150.0 2.6 %collective-permute-start.2 = (f32[2,64,1536]{2,1,0:T(8,128)}, f32[2,64,1536]{2,1,0:T(8,128)}, u32[]{:S(2)}, u32[]{:S(2)}) collective-permute-start(f32[2,64,1536]{2,1,0:T(8,128)} %dynamic-slice_bitcast_fusion), channel_id=1, source_target_pairs={{0,1},{1,0},{2,3},{3,2},{4,5},{5,4},{6,7},{7,6},{8,9},{9,8},{10,11... | collective-permute-start | bytes 2359304 | tf_op jit(solution)/shard_map/ppermute | solution.py:133
  151.3 10.3 %collective-permute-start.1 = (f32[64,1536]{1,0:T(8,128)S(1)}, f32[64,1536]{1,0:T(8,128)S(1)}, u32[]{:S(2)}, u32[]{:S(2)}) collective-permute-start(f32[64,1536]{1,0:T(8,128)S(1)} %dynamic-slice_bitcast_fusion.3), channel_id=1, source_target_pairs={{0,2},{2,0},{1,3},{3,1},{4,6},{6,4},{5,7},{7,5},{8,10},{10,8},{9,1... | collective-permute-start | bytes 1179656 | tf_op jit(solution)/shard_map/ppermute | solution.py:136
  153.9 16.1 %collective-permute-start.3 = (f32[64,1536]{1,0:T(8,128)S(1)}, f32[64,1536]{1,0:T(8,128)S(1)}, u32[]{:S(2)}, u32[]{:S(2)}) collective-permute-start(f32[64,1536]{1,0:T(8,128)S(1)} %dynamic-slice_bitcast_fusion.2), channel_id=1, source_target_pairs={{0,2},{2,0},{1,3},{3,1},{4,6},{6,4},{5,7},{7,5},{8,10},{10,8},{9,1... | collective-permute-start | bytes 1179656 | tf_op jit(solution)/shard_map/ppermute | solution.py:136

commit v6 on v5

--- a/solution.py
+++ b/solution.py
@@ -13,7 +13,7 @@
 NSRC = 8
 ROUNDS = 3
 
-CHUNK = 256
+CHUNK = 512
 ROWS = 16
 
 EPSILON = 1e-05

time: 172 us -> 168 us (0.977)
  Pallas kernels: 54 us -> 49.9 us
    pallas_call x2, Pallas kernels: 54 us -> 49.9 us  [cross_project(): pl.pallas_call(cross_project_kernel, grid=(steps,), in_specs=[pl.BlockSpe...]
  transfers between devices with their start and end apart: 6 -> 6, of which waited for: 4 -> 4; matrix products, arithmetic and copies ran while one was open for 27% -> 28% of each run, Pallas kernels for 32% -> 30%
where the time goes in v6:
time: 168 us; the launch traced here: 167 us
  Pallas kernels  49.9 us (30%)
  other arithmetic  32.2 us (19%)
  waiting for transfers between devices  30.9 us (18%)
  local copies, waits for them, and re-layouts  27.2 us (16%)
  starting transfers between devices  19.8 us (12%)
  matrix products  7.1 us (4%)
    pallas_call x2, Pallas kernels, cross_project(): pl.pallas_call(cross_project_kernel, grid=(steps,), in_specs=[pl.BlockSpe...  49.9 us
    another operation x1, other arithmetic  18.2 us
    all_to_all x1, waiting for transfers between devices, local(): lax.all_to_all(send_a, 'sta', split_axis=2, concat_axis=3, tiled=True)  15.3 us
    ppermute x2, waiting for transfers between devices, reduce_lags(): lax.ppermute(send, 'tm', perm=[(0, 2), (2, 0), (1, 3), (3, 1)])  15 us
    all_to_all x1, starting transfers between devices, local(): lax.all_to_all(send_a, 'sta', split_axis=2, concat_axis=3, tiled=True)  11.2 us
    slice x1, local copies, waits for them, and re-layouts, local(): chunks[:, :, :, :half]  6.56 us
    unnamed x7, local copies, waits for them, and re-layouts  6.28 us
    all_to_all x1, starting transfers between devices, local(): lax.all_to_all(send_b, 'sta', split_axis=2, concat_axis=3, tiled=True)  5.37 us
  transfers between devices with their start and end apart: 6, of which 4 were waited for; matrix products, arithmetic and copies ran while one was open for 28% of the time, Pallas kernels for 30%

profile of v6, /device:TPU:1, one launch (start us, length us, event | category | flops | bytes accessed | tf_op | source)
XLA Modules:
  0.0 167.3 jit_solution(17376986948084335733)
XLA Ops:
  0.8 0.8 reshape.83
  1.5 6.6 %fusion.50 = (bf16[2,2,32,64,128]{4,1,3,2,0:T(2,128)(2,1)S(1)}, bf16[2,2,32,64,128]{4,1,3,2,0:T(2,128)(2,1)}) fusion(bf16[2,2,32,128,128]{4,1,3,2,0:T(2,128)(2,1)} %bitcast.70), kind=kLoop, calls=%fused_computation.82 | loop fusion | bytes 8388608 | tf_op jit(solution)/shard_map/slice | solution.py:172
  8.1 2.8 %gather_fusion = bf16[24,2,2,128]{3,2,1,0:T(2,128)(2,1)S(1)} fusion(bf16[2,2,4096,128]{3,1,2,0:T(2,128)(2,1)} %bitcast.71, s32[1024]{0:T(1024)S(1)} %pad_clamp_fusion), kind=kCustom, calls=%fused_computation | custom fusion | bytes 49248 | tf_op jit(solution)/shard_map/jit(_take)/gather | solution.py:167
  11.4 4.3 %pad_maximum_fusion.1 = bf16[2,2,32,88,128]{4,1,0,3,2:T(2,128)(2,1)} fusion(bf16[2,2,32,24,128]{4,1,0,3,2:T(2,128)(2,1)S(1)} %broadcast_in_dim.22, bf16[2,2,32,64,128]{4,1,3,2,0:T(2,128)(2,1)S(1)} %get-tuple-element.9), kind=kLoop, calls=%fused_computation.24 | loop fusion | flops 5767168 | bytes 5767168 | tf_op jit(solution)/shard_map/concatenate | solution.py:172
  15.7 11.2 %all-to-all-start = ((bf16[2,2,2816,128]{3,1,0,2:T(2,128)(2,1)}), bf16[2,2,2816,128]{3,1,0,2:T(2,128)(2,1)S(1)}, u32[]{:S(2)}, u32[]{:S(2)}) async-start(bf16[2,2,2816,128]{3,1,0,2:T(2,128)(2,1)} %bitcast.63), calls=%async_computation | async-start | bytes 5767168 | tf_op jit(solution)/shard_map/all_to_all | solution.py:176
  26.9 4.7 %copy.17 = bf16[2,2,32,64,128]{4,1,0,3,2:T(2,128)(2,1)} copy(bf16[2,2,32,64,128]{4,1,3,2,0:T(2,128)(2,1)} %get-tuple-element.10) | data formatting | bytes 4194304
  31.6 18.2 %multiply_convert_fusion.1 = (bf16[256,4096]{1,0:T(8,128)(2,1)S(1)}, bf16[256,4096]{1,0:T(8,128)(2,1)S(1)}) fusion(s32[256]{0:T(256)S(1)} %iota_add_fusion), kind=kLoop, calls=%fused_computation.13 | loop fusion | flops 19922944 | bytes 4195328 | tf_op jit(solution)/shard_map/convert.3
  49.8 2.4 %pad_maximum_fusion.tre_ref.tim_ref = bf16[256,8192]{1,0:T(8,128)(2,1)} fusion(bf16[256,4096]{1,0:T(8,128)(2,1)S(1)} %get-tuple-element.12, bf16[256,4096]{1,0:T(8,128)(2,1)S(1)} %get-tuple-element.11), kind=kLoop, calls=%fused_computation.9 | loop fusion | flops 8388608 | bytes 8388608 | tf_op jit(solution)/shard_map/concatenate | solution.py:46
  52.2 15.3 %all-to-all-done = bf16[2,2,2816,128]{3,1,0,2:T(2,128)(2,1)S(1)} async-done(((bf16[2,2,2816,128]{3,1,0,2:T(2,128)(2,1)}), bf16[2,2,2816,128]{3,1,0,2:T(2,128)(2,1)S(1)}, u32[]{:S(2)}, u32[]{:S(2)}) %all-to-all-start) | async-done | bytes 2883616 | tf_op jit(solution)/shard_map/all_to_all | solution.py:176
  67.9 0.8 copy.27
  68.7 5.4 %all-to-all-start.1 = ((bf16[2,2,2048,128]{3,1,0,2:T(2,128)(2,1)}), bf16[2,2,2048,128]{3,1,0,2:T(2,128)(2,1)}, u32[]{:S(2)}, u32[]{:S(2)}) async-start(bf16[2,2,2048,128]{3,1,0,2:T(2,128)(2,1)} %bitcast.65), calls=%async_computation.1 | async-start | bytes 4194304 | tf_op jit(solution)/shard_map/all_to_all | solution.py:178
  74.8 2.8 %fusion.9 = f32[2,88,64]{1,2,0:T(8,128)S(1)} fusion(f32[2,2,88,4096]{3,2,1,0:T(8,128)S(1)} %convert_element_type.33, s32[4096]{0:T(1024)S(1)} %get-tuple-element.13, s32[4096]{0:T(1024)S(1)} %get-tuple-element.14, pred[4096]{0:T(1024)(128)(4,1)S(1)} %fusion.38), kind=kOutput, calls=%fused_computation.22 | convolution fusion | flops 556335104 | bytes 5849088 | tf_op jit(solution)/shard_map/hrf,fb->hrb/dot_general | solution.py:148
  77.6 1.4 fusion.21
  79.0 1.4 divide_convert_fusion.x_ref
  80.4 1.6 copy-done
  82.0 0.9 slice.56.y_ref
  82.9 24.9 %shard_map.28 = f32[256,1536]{1,0:T(8,128)} custom-call(bf16[2,2,88,4096]{3,2,1,0:T(8,128)(2,1)} %copy-done, bf16[2,2,24,4096]{3,2,1,0:T(8,128)(2,1)} %slice.56.y_ref, bf16[256,8192]{1,0:T(8,128)(2,1)} %pad_maximum_fusion.tre_ref.tim_ref, bf16[256,8192]{1,0:T(8,128)(2,1)} %pad_maximum_fusion.tre_ref.tim_ref), custom_call_target="tpu_custom_call" | custom-call | tf_op jit(solution)/shard_map/pallas_call | solution.py:105
  107.9 2.1 %dynamic-slice_bitcast_fusion.1 = f32[2,64,1536]{2,1,0:T(8,128)} fusion(f32[2,2,64,1536]{3,2,1,0:T(8,128)} %bitcast.68, s32[]{:T(128)S(6)} %select_n.83), kind=kLoop, calls=%fused_computation.37 | loop fusion | bytes 1572868 | tf_op jit(solution)/shard_map/jit(dynamic_index_in_dim)/squeeze | solution.py:132
  110.0 1.6 collective-permute-start
  111.6 1.9 %copy.14 = bf16[2,2,2048,128]{3,2,1,0:T(8,128)(2,1)S(1)} copy(bf16[2,2,2048,128]{3,1,0,2:T(2,128)(2,1)} %all-to-all-done.1) | data formatting | bytes 4194304 | tf_op jit(solution)/shard_map/all_to_all | solution.py:178
  114.0 1.9 %fusion.14 = f32[2,64,64]{2,1,0:T(8,128)S(1)} fusion(f32[2,2,64,4096]{3,2,1,0:T(8,128)S(1)} %copy_bitcast_fusion, s32[4096]{0:T(1024)S(1)} %get-tuple-element.13, s32[4096]{0:T(1024)S(1)} %get-tuple-element.14, pred[4096]{0:T(1024)(128)(4,1)S(1)} %fusion.38), kind=kOutput, calls=%fused_computation.29 | convolution fusion | flops 404750336 | bytes 4263936 | tf_op jit(solution)/shard_map/hrf,fb->hrb/dot_general | solution.py:148
  115.9 1.0 fusion.23
  116.9 1.8 %divide_convert_fusion.1.x_ref = bf16[2,2,64,4096]{3,2,1,0:T(8,128)(2,1)} fusion(f32[2,64,4096]{2,1,0:T(8,128)S(1)} %fusion.23, bf16[2,2,32,64,128]{4,3,2,1,0:T(8,128)(2,1)S(1)} %bitcast.62), kind=kLoop, calls=%fused_computation.11 | loop fusion | flops 3145728 | bytes 6291456 | tf_op jit(solution)/shard_map/convert_element_type | solution.py:156
  118.7 25.0 %shard_map.29 = f32[256,1536]{1,0:T(8,128)} custom-call(bf16[2,2,64,4096]{3,2,1,0:T(8,128)(2,1)} %divide_convert_fusion.1.x_ref, bf16[2,2,24,4096]{3,2,1,0:T(8,128)(2,1)} %slice.56.y_ref, bf16[256,8192]{1,0:T(8,128)(2,1)} %pad_maximum_fusion.tre_ref.tim_ref, bf16[256,8192]{1,0:T(8,128)(2,1)} %pad_maximum_fusion.tre_ref.tim_ref), custom_call_target="tpu_custom_call" | custom-call | tf_op jit(solution)/shard_map/pallas_call | solution.py:105
  143.7 2.2 %dynamic-slice_bitcast_fusion = f32[2,64,1536]{2,1,0:T(8,128)} fusion(f32[2,2,64,1536]{3,2,1,0:T(8,128)} %bitcast.66, s32[]{:T(128)S(6)} %select_n.83), kind=kLoop, calls=%fused_computation.36 | loop fusion | bytes 1572868 | tf_op jit(solution)/shard_map/jit(dynamic_index_in_dim)/squeeze | solution.py:132
  145.9 1.2 bitcast_add_fusion.1
  147.2 0.8 collective-permute-start.1
  148.5 1.2 bitcast_add_fusion
  149.8 0.8 collective-permute-start.3
  150.6 6.8 %collective-permute-done.1 = f32[64,1536]{1,0:T(8,128)S(1)} collective-permute-done((f32[64,1536]{1,0:T(8,128)S(1)}, f32[64,1536]{1,0:T(8,128)S(1)}, u32[]{:S(2)}, u32[]{:S(2)}) %collective-permute-start.1) | collective-permute-done | bytes 393248 | tf_op jit(solution)/shard_map/ppermute | solution.py:136
  157.7 8.2 %collective-permute-done.3 = f32[64,1536]{1,0:T(8,128)S(1)} collective-permute-done((f32[64,1536]{1,0:T(8,128)S(1)}, f32[64,1536]{1,0:T(8,128)S(1)}, u32[]{:S(2)}, u32[]{:S(2)}) %collective-permute-start.3) | collective-permute-done | bytes 393248 | tf_op jit(solution)/shard_map/ppermute | solution.py:136
  166.4 0.9 copy.16
  (28 shorter events, 4.2 us)
Async XLA Ops:
  15.7 51.8 %all-to-all-start = ((bf16[2,2,2816,128]{3,1,0,2:T(2,128)(2,1)}), bf16[2,2,2816,128]{3,1,0,2:T(2,128)(2,1)S(1)}, u32[]{:S(2)}, u32[]{:S(2)}) async-start(bf16[2,2,2816,128]{3,1,0,2:T(2,128)(2,1)} %bitcast.63), calls=%async_computation | async-start | bytes 5767168 | tf_op jit(solution)/shard_map/all_to_all | solution.py:176
  68.7 42.9 %all-to-all-start.1 = ((bf16[2,2,2048,128]{3,1,0,2:T(2,128)(2,1)}), bf16[2,2,2048,128]{3,1,0,2:T(2,128)(2,1)}, u32[]{:S(2)}, u32[]{:S(2)}) async-start(bf16[2,2,2048,128]{3,1,0,2:T(2,128)(2,1)} %bitcast.65), calls=%async_computation.1 | async-start | bytes 4194304 | tf_op jit(solution)/shard_map/all_to_all | solution.py:178
  80.4 1.6 copy-start
  110.0 35.9 %collective-permute-start = (f32[2,64,1536]{2,1,0:T(8,128)}, f32[2,64,1536]{2,1,0:T(8,128)}, u32[]{:S(2)}, u32[]{:S(2)}) collective-permute-start(f32[2,64,1536]{2,1,0:T(8,128)} %dynamic-slice_bitcast_fusion.1), channel_id=1, source_target_pairs={{0,1},{1,0},{2,3},{3,2},{4,5},{5,4},{6,7},{7,6},{8,9},{9,8},{10,11... | collective-permute-start | bytes 2359304 | tf_op jit(solution)/shard_map/ppermute | solution.py:133
  118.7 27.2 %copy-start.2 = (f32[256,1536]{1,0:T(8,128)S(1)}, f32[256,1536]{1,0:T(8,128)}, u32[]{:S(2)}) copy-start(f32[256,1536]{1,0:T(8,128)} %shard_map.28) | copy-start | bytes 4718596
  143.7 4.8 %copy-start.1 = (f32[256,1536]{1,0:T(8,128)S(1)}, f32[256,1536]{1,0:T(8,128)}, u32[]{:S(2)}) copy-start(f32[256,1536]{1,0:T(8,128)} %shard_map.29) | copy-start | bytes 4718596
  145.9 2.6 %collective-permute-start.2 = (f32[2,64,1536]{2,1,0:T(8,128)}, f32[2,64,1536]{2,1,0:T(8,128)}, u32[]{:S(2)}, u32[]{:S(2)}) collective-permute-start(f32[2,64,1536]{2,1,0:T(8,128)} %dynamic-slice_bitcast_fusion), channel_id=1, source_target_pairs={{0,1},{1,0},{2,3},{3,2},{4,5},{5,4},{6,7},{7,6},{8,9},{9,8},{10,11... | collective-permute-start | bytes 2359304 | tf_op jit(solution)/shard_map/ppermute | solution.py:133
  147.2 10.3 %collective-permute-start.1 = (f32[64,1536]{1,0:T(8,128)S(1)}, f32[64,1536]{1,0:T(8,128)S(1)}, u32[]{:S(2)}, u32[]{:S(2)}) collective-permute-start(f32[64,1536]{1,0:T(8,128)S(1)} %dynamic-slice_bitcast_fusion.3), channel_id=1, source_target_pairs={{0,2},{2,0},{1,3},{3,1},{4,6},{6,4},{5,7},{7,5},{8,10},{10,8},{9,1... | collective-permute-start | bytes 1179656 | tf_op jit(solution)/shard_map/ppermute | solution.py:136
  149.8 16.1 %collective-permute-start.3 = (f32[64,1536]{1,0:T(8,128)S(1)}, f32[64,1536]{1,0:T(8,128)S(1)}, u32[]{:S(2)}, u32[]{:S(2)}) collective-permute-start(f32[64,1536]{1,0:T(8,128)S(1)} %dynamic-slice_bitcast_fusion.2), channel_id=1, source_target_pairs={{0,2},{2,0},{1,3},{3,1},{4,6},{6,4},{5,7},{7,5},{8,10},{10,8},{9,1... | collective-permute-start | bytes 1179656 | tf_op jit(solution)/shard_map/ppermute | solution.py:136

commit v7 on v6

--- a/solution.py
+++ b/solution.py
@@ -156,6 +156,19 @@
     return (values / denom[:, None]).astype(jnp.bfloat16)
 
 
+def to_send(spectra, first, count, extra):
+    hours_dev, stations, _, bins_dev = spectra.shape
+    shards = lax.axis_size("sta")
+    chunks = spectra.reshape(hours_dev, shards, stations // shards, 2, bins_dev)
+    chunks = jnp.transpose(chunks[:, :, first:first + count], (0, 3, 1, 2, 4))
+    if extra is not None:
+        copies = jnp.broadcast_to(
+            extra[:, :, None], (hours_dev, 2, shards, extra.shape[2], bins_dev)
+        )
+        chunks = jnp.concatenate([chunks, copies], axis=3)
+    return chunks.reshape(hours_dev, 2, -1, bins_dev)
+
+
 def local(spectra, src_ids):
     hours_dev, stations, _, bins_dev = spectra.shape
     shards = lax.axis_size("sta")
@@ -163,32 +176,31 @@
     half = stations_dev // 2
     flat_ids = src_ids.reshape(-1)
     count_all = flat_ids.shape[0]
-    by_part = jnp.transpose(spectra, (0, 2, 1, 3))
-    src_raw = jnp.take(by_part, flat_ids, axis=2)
-    chunks = by_part.reshape(hours_dev, 2, shards, stations_dev, bins_dev)
-    src_copies = jnp.broadcast_to(
-        src_raw[:, :, None], (hours_dev, 2, shards, count_all, bins_dev)
-    )
-    send_a = jnp.concatenate([chunks[:, :, :, :half], src_copies], axis=3).reshape(
-        hours_dev, 2, shards * (half + count_all), bins_dev
-    )
-    send_b = chunks[:, :, :, half:].reshape(hours_dev, 2, shards * half, bins_dev)
+    src_raw = jnp.transpose(jnp.take(spectra, flat_ids, axis=1), (0, 2, 1, 3))
+    send_a = to_send(spectra, 0, half, src_raw)
     joined_a = lax.all_to_all(send_a, "sta", split_axis=2, concat_axis=3, tiled=True)
+    transform = make_table(hours_dev * lax.axis_size("tm"))
+    spectra_b, transform = lax.optimization_barrier((spectra, transform))
+    send_b = to_send(spectra_b, half, stations_dev - half, None)
     send_b, joined_a = lax.optimization_barrier((send_b, joined_a))
     joined_b = lax.all_to_all(send_b, "sta", split_axis=2, concat_axis=3, tiled=True)
     white_a = whiten(joined_a)
-    transform = make_table(hours_dev * lax.axis_size("tm"))
     row_count = transform.shape[0] // lax.axis_size("tm")
     sources = white_a[:, :, half:half + count_all]
     part_a = reduce_lags(cross_project(white_a, sources, transform, half))
     white_b = whiten(joined_b)
-    part_b = reduce_lags(cross_project(white_b, sources, transform, half))
+    split = (ROUNDS - 1) * NSRC
+    part_b1 = reduce_lags(cross_project(white_b, sources[:, :, :split], transform, half))
+    part_b2 = reduce_lags(cross_project(white_b, sources[:, :, split:], transform, half))
+    part_b = jnp.concatenate(
+        [
+            part_b1.reshape(row_count, ROUNDS - 1, NSRC, half),
+            part_b2.reshape(row_count, 1, NSRC, half),
+        ],
+        axis=1,
+    )
     both = jnp.concatenate(
-        [
-            part_a.reshape(row_count, ROUNDS, NSRC, half),
-            part_b.reshape(row_count, ROUNDS, NSRC, half),
-        ],
-        axis=3,
+        [part_a.reshape(row_count, ROUNDS, NSRC, half), part_b], axis=3
     )
     return jnp.transpose(both, (1, 0, 2, 3))
 

time: 168 us -> 173 us (1.030)
  Pallas kernels: 49.9 us -> 54.3 us
  starting transfers between devices: 19.8 us -> 21.9 us
    pallas_call x2 -> x3, Pallas kernels: 49.9 us -> 54.3 us  [cross_project(): pl.pallas_call(cross_project_kernel, grid=(steps,), in_specs=[pl.BlockSpe...]
    transpose x0 -> x1, local copies, waits for them, and re-layouts: none -> 3.31 us  [to_send(): chunks = jnp.transpose(chunks[:, :, first:first + count], (0, 3, 1, 2, 4))]
    add x2 -> x3, other arithmetic: 2.44 us -> 0.19 us  [reduce_lags(): keep + lax.ppermute(send, 'tm', perm=[(0, 1), (1, 0), (2, 3), (3, 2)])]
    all_to_all x1, waiting for transfers between devices: 15.3 us -> 13.6 us  [local(): lax.all_to_all(send_a, 'sta', split_axis=2, concat_axis=3, tiled=True)]
    slice x1 -> x3, local copies, waits for them, and re-layouts: 6.56 us -> 5.36 us  [the longest x1 1.91 us: local(): sources[:, :, :split]]
    ppermute x2 -> x3, waiting for transfers between devices: 15 us -> 16.1 us  [reduce_lags(): lax.ppermute(send, 'tm', perm=[(0, 2), (2, 0), (1, 3), (3, 1)])]
    squeeze x2 -> x3, local copies, waits for them, and re-layouts: 4.27 us -> 3.44 us  [reduce_lags(): send = lax.dynamic_index_in_dim(blocks, 1 - core, axis=1, keepdims=False)]
    unnamed x7 -> x11, local copies, waits for them, and re-layouts: 6.28 us -> 5.86 us
  transfers between devices with their start and end apart: 6 -> 8, of which waited for: 4 -> 4; matrix products, arithmetic and copies ran while one was open for 28% -> 23% of each run, Pallas kernels for 30% -> 25%
where the time goes in v7:
time: 173 us
  Pallas kernels  54.3 us (31%)
  other arithmetic  31.3 us (18%)
  waiting for transfers between devices  29.7 us (17%)
  local copies, waits for them, and re-layouts  28.1 us (16%)
  starting transfers between devices  21.9 us (13%)
  matrix products  7.1 us (4%)
    pallas_call x3, Pallas kernels, cross_project(): pl.pallas_call(cross_project_kernel, grid=(steps,), in_specs=[pl.BlockSpe...  54.3 us
    another operation x1, other arithmetic  18.2 us
    ppermute x3, waiting for transfers between devices, reduce_lags(): lax.ppermute(send, 'tm', perm=[(0, 2), (2, 0), (1, 3), (3, 1)])  16.1 us
    all_to_all x1, waiting for transfers between devices, local(): lax.all_to_all(send_a, 'sta', split_axis=2, concat_axis=3, tiled=True)  13.6 us
    all_to_all x1, starting transfers between devices, local(): lax.all_to_all(send_a, 'sta', split_axis=2, concat_axis=3, tiled=True)  11.4 us
    unnamed x11, local copies, waits for them, and re-layouts  5.86 us
    all_to_all x1, starting transfers between devices, local(): lax.all_to_all(send_b, 'sta', split_axis=2, concat_axis=3, tiled=True)  5.41 us
    concatenate x1, other arithmetic, to_send(): chunks = jnp.concatenate([chunks, copies], axis=3)  5.31 us
  transfers between devices with their start and end apart: 8, of which 4 were waited for; matrix products, arithmetic and copies ran while one was open for 23% of the time, Pallas kernels for 25%

profile of v7, /device:TPU:1, one launch (start us, length us, event | category | flops | bytes accessed | tf_op | source)
XLA Modules:
  0.0 172.6 jit_solution(15568755457893559027)
XLA Ops:
  1.6 2.8 %gather_fusion = bf16[24,2,2,128]{3,2,1,0:T(2,128)(2,1)S(1)} fusion(bf16[2,4096,2,128]{3,2,1,0:T(2,128)(2,1)} %param.2, s32[1024]{0:T(1024)S(1)} %pad_clamp_fusion), kind=kCustom, calls=%fused_computation | custom fusion | bytes 49248 | tf_op jit(solution)/shard_map/jit(_take)/gather | solution.py:179
  4.4 3.3 %copy_bitcast_fusion.2 = bf16[2,2,32,64,128]{4,1,0,3,2:T(2,128)(2,1)S(1)} fusion(bf16[2,32,128,2,128]{4,3,2,1,0:T(2,128)(2,1)} %bitcast.80), kind=kLoop, calls=%fused_computation.31 | loop fusion | bytes 4194304 | tf_op jit(solution)/shard_map/transpose | solution.py:163
  8.2 5.3 %pad_maximum_fusion.1 = bf16[2,2,32,88,128]{4,1,0,3,2:T(2,128)(2,1)} fusion(bf16[2,2,32,24,128]{4,1,0,3,2:T(2,128)(2,1)S(1)} %broadcast_in_dim.22, bf16[2,2,32,64,128]{4,1,0,3,2:T(2,128)(2,1)S(1)} %copy_bitcast_fusion.2), kind=kLoop, calls=%fused_computation.24 | loop fusion | flops 1441792 | bytes 5767168 | tf_op jit(solution)/shard_map/concatenate | solution.py:168
  13.5 11.4 %all-to-all-start = ((bf16[2,2,2816,128]{3,1,0,2:T(2,128)(2,1)}), bf16[2,2,2816,128]{3,1,0,2:T(2,128)(2,1)S(1)}, u32[]{:S(2)}, u32[]{:S(2)}) async-start(bf16[2,2,2816,128]{3,1,0,2:T(2,128)(2,1)} %bitcast.75), calls=%async_computation | async-start | bytes 5767168 | tf_op jit(solution)/shard_map/all_to_all | solution.py:181
  24.9 18.2 %multiply_convert_fusion.1 = (bf16[256,4096]{1,0:T(8,128)(2,1)S(1)}, bf16[256,4096]{1,0:T(8,128)(2,1)S(1)}) fusion(s32[256]{0:T(256)S(1)} %iota_add_fusion), kind=kLoop, calls=%fused_computation.13 | loop fusion | flops 19922944 | bytes 4195328 | tf_op jit(solution)/shard_map/convert.3
  43.1 2.6 %pad_maximum_fusion.tre_ref.tim_ref = bf16[256,8192]{1,0:T(8,128)(2,1)} fusion(bf16[256,4096]{1,0:T(8,128)(2,1)S(1)} %get-tuple-element.14, bf16[256,4096]{1,0:T(8,128)(2,1)S(1)} %get-tuple-element.13), kind=kLoop, calls=%fused_computation.9 | loop fusion | flops 8388608 | bytes 8388608 | tf_op jit(solution)/shard_map/concatenate | solution.py:46
  45.7 1.1 copy-done.2
  46.8 1.8 %slice.62 = bf16[2,32,64,2,128]{4,3,2,1,0:T(2,128)(2,1)S(1)} slice(bf16[2,32,128,2,128]{4,3,2,1,0:T(2,128)(2,1)S(1)} %bitcast.81), slice={[0:2], [0:32], [64:128], [0:2], [0:128]} | slice | bytes 4194304 | tf_op jit(solution)/shard_map/slice | solution.py:163
  48.6 3.1 %copy.17 = bf16[2,32,64,2,128]{4,3,0,2,1:T(2,128)(2,1)} copy(bf16[2,32,64,2,128]{4,3,2,1,0:T(2,128)(2,1)S(1)} %slice.62) | data formatting | bytes 4194304
  51.8 13.6 %all-to-all-done = bf16[2,2,2816,128]{3,1,0,2:T(2,128)(2,1)S(1)} async-done(((bf16[2,2,2816,128]{3,1,0,2:T(2,128)(2,1)}), bf16[2,2,2816,128]{3,1,0,2:T(2,128)(2,1)S(1)}, u32[]{:S(2)}, u32[]{:S(2)}) %all-to-all-start) | async-done | bytes 2883616 | tf_op jit(solution)/shard_map/all_to_all | solution.py:181
  66.5 5.4 %all-to-all-start.1 = ((bf16[2,2,2048,128]{3,1,0,2:T(2,128)(2,1)}), bf16[2,2,2048,128]{3,1,0,2:T(2,128)(2,1)}, u32[]{:S(2)}, u32[]{:S(2)}) async-start(bf16[2,2,2048,128]{3,1,0,2:T(2,128)(2,1)} %bitcast.77), calls=%async_computation.1 | async-start | bytes 4194304 | tf_op jit(solution)/shard_map/all_to_all | solution.py:186
  72.6 2.8 %fusion.9 = f32[2,88,64]{1,2,0:T(8,128)S(1)} fusion(f32[2,2,88,4096]{3,2,1,0:T(8,128)S(1)} %convert_element_type.34, s32[4096]{0:T(1024)S(1)} %get-tuple-element.15, s32[4096]{0:T(1024)S(1)} %get-tuple-element.16, pred[4096]{0:T(1024)(128)(4,1)S(1)} %fusion.38), kind=kOutput, calls=%fused_computation.22 | convolution fusion | flops 556335104 | bytes 5849088 | tf_op jit(solution)/shard_map/hrf,fb->hrb/dot_general | solution.py:148
  75.4 1.4 fusion.21
  76.8 1.4 divide_convert_fusion.x_ref
  78.2 1.6 copy-done
  79.8 0.9 slice.66.y_ref
  80.8 25.0 %shard_map.28 = f32[256,1536]{1,0:T(8,128)} custom-call(bf16[2,2,88,4096]{3,2,1,0:T(8,128)(2,1)} %copy-done, bf16[2,2,24,4096]{3,2,1,0:T(8,128)(2,1)} %slice.66.y_ref, bf16[256,8192]{1,0:T(8,128)(2,1)} %pad_maximum_fusion.tre_ref.tim_ref, bf16[256,8192]{1,0:T(8,128)(2,1)} %pad_maximum_fusion.tre_ref.tim_ref), custom_call_target="tpu_custom_call" | custom-call | tf_op jit(solution)/shard_map/pallas_call | solution.py:105
  105.7 1.3 dynamic-slice_bitcast_fusion
  107.0 1.7 %collective-permute-start = (f32[2,64,1536]{2,1,0:T(8,128)S(1)}, f32[2,64,1536]{2,1,0:T(8,128)S(1)}, u32[]{:S(2)}, u32[]{:S(2)}) collective-permute-start(f32[2,64,1536]{2,1,0:T(8,128)S(1)} %dynamic-slice_bitcast_fusion), channel_id=1, source_target_pairs={{0,1},{1,0},{2,3},{3,2},{4,5},{5,4},{6,7},{7,6},{8,9},{9,8},{10,11... | collective-permute-start | bytes 2359304 | tf_op jit(solution)/shard_map/ppermute | solution.py:133
  108.8 1.7 slice.70.y_ref
  110.4 1.9 %slice.69.y_ref = bf16[2,2,16,4096]{3,2,1,0:T(8,128)(2,1)} slice(bf16[2,2,88,4096]{3,2,1,0:T(8,128)(2,1)} %copy-done), slice={[0:2], [0:2], [64:80], [0:4096]} | slice | bytes 1048576 | tf_op jit(solution)/shard_map/slice | solution.py:193
  112.5 1.9 %copy.14 = bf16[2,2,2048,128]{3,2,1,0:T(8,128)(2,1)S(1)} copy(bf16[2,2,2048,128]{3,1,0,2:T(2,128)(2,1)} %all-to-all-done.1) | data formatting | bytes 4194304 | tf_op jit(solution)/shard_map/all_to_all | solution.py:186
  114.8 1.9 %fusion.14 = f32[2,64,64]{2,1,0:T(8,128)S(1)} fusion(f32[2,2,64,4096]{3,2,1,0:T(8,128)S(1)} %copy_bitcast_fusion, s32[4096]{0:T(1024)S(1)} %get-tuple-element.15, s32[4096]{0:T(1024)S(1)} %get-tuple-element.16, pred[4096]{0:T(1024)(128)(4,1)S(1)} %fusion.38), kind=kOutput, calls=%fused_computation.29 | convolution fusion | flops 404750336 | bytes 4263936 | tf_op jit(solution)/shard_map/hrf,fb->hrb/dot_general | solution.py:148
  116.7 1.0 fusion.23
  117.8 1.9 %divide_convert_fusion.1.x_ref = bf16[2,2,64,4096]{3,2,1,0:T(8,128)(2,1)} fusion(f32[2,64,4096]{2,1,0:T(8,128)S(1)} %fusion.23, bf16[2,2,32,64,128]{4,3,2,1,0:T(8,128)(2,1)S(1)} %bitcast.74), kind=kLoop, calls=%fused_computation.11 | loop fusion | flops 3145728 | bytes 6291456 | tf_op jit(solution)/shard_map/convert_element_type | solution.py:156
  119.6 11.4 %shard_map.30 = f32[256,512]{1,0:T(8,128)} custom-call(bf16[2,2,64,4096]{3,2,1,0:T(8,128)(2,1)} %divide_convert_fusion.1.x_ref, bf16[2,2,8,4096]{3,2,1,0:T(8,128)(2,1)} %slice.70.y_ref, bf16[256,8192]{1,0:T(8,128)(2,1)} %pad_maximum_fusion.tre_ref.tim_ref, bf16[256,8192]{1,0:T(8,128)(2,1)} %pad_maximum_fusion.tre_ref.tim_ref), custom_call_target="tpu_custom_call" | custom-call | tf_op jit(solution)/shard_map/pallas_call | solution.py:105
  131.1 1.0 dynamic-slice_bitcast_fusion.3
  132.4 17.9 %shard_map.29 = f32[256,1024]{1,0:T(8,128)} custom-call(bf16[2,2,64,4096]{3,2,1,0:T(8,128)(2,1)} %divide_convert_fusion.1.x_ref, bf16[2,2,16,4096]{3,2,1,0:T(8,128)(2,1)} %slice.69.y_ref, bf16[256,8192]{1,0:T(8,128)(2,1)} %pad_maximum_fusion.tre_ref.tim_ref, bf16[256,8192]{1,0:T(8,128)(2,1)} %pad_maximum_fusion.tre_ref.tim_ref), custom_call_target="tpu_custom_call" | custom-call | tf_op jit(solution)/shard_map/pallas_call | solution.py:105
  150.3 1.2 dynamic-slice_bitcast_fusion.1
  154.7 8.1 %collective-permute-done.1 = f32[64,1536]{1,0:T(8,128)S(1)} collective-permute-done((f32[64,1536]{1,0:T(8,128)S(1)}, f32[64,1536]{1,0:T(8,128)S(1)}, u32[]{:S(2)}, u32[]{:S(2)}) %collective-permute-start.1) | collective-permute-done | bytes 393248 | tf_op jit(solution)/shard_map/ppermute | solution.py:136
  163.0 2.6 %collective-permute-done.5 = f32[64,512]{1,0:T(8,128)S(1)} collective-permute-done((f32[64,512]{1,0:T(8,128)S(1)}, f32[64,512]{1,0:T(8,128)S(1)}, u32[]{:S(2)}, u32[]{:S(2)}) %collective-permute-start.5) | collective-permute-done | bytes 131104 | tf_op jit(solution)/shard_map/ppermute | solution.py:136
  165.7 5.5 %collective-permute-done.3 = f32[64,1024]{1,0:T(8,128)S(1)} collective-permute-done((f32[64,1024]{1,0:T(8,128)S(1)}, f32[64,1024]{1,0:T(8,128)S(1)}, u32[]{:S(2)}, u32[]{:S(2)}) %collective-permute-start.3) | collective-permute-done | bytes 262176 | tf_op jit(solution)/shard_map/ppermute | solution.py:136
  (45 shorter events, 9.8 us)
Async XLA Ops:
  13.5 51.8 %all-to-all-start = ((bf16[2,2,2816,128]{3,1,0,2:T(2,128)(2,1)}), bf16[2,2,2816,128]{3,1,0,2:T(2,128)(2,1)S(1)}, u32[]{:S(2)}, u32[]{:S(2)}) async-start(bf16[2,2,2816,128]{3,1,0,2:T(2,128)(2,1)} %bitcast.75), calls=%async_computation | async-start | bytes 5767168 | tf_op jit(solution)/shard_map/all_to_all | solution.py:181
  43.1 3.7 %copy-start.2 = (bf16[2,4096,2,128]{3,2,1,0:T(2,128)(2,1)S(1)}, bf16[2,4096,2,128]{3,2,1,0:T(2,128)(2,1)}, u32[]{:S(2)}) copy-start(bf16[2,4096,2,128]{3,2,1,0:T(2,128)(2,1)} %param.2) | copy-start | bytes 12582916
  66.5 45.9 %all-to-all-start.1 = ((bf16[2,2,2048,128]{3,1,0,2:T(2,128)(2,1)}), bf16[2,2,2048,128]{3,1,0,2:T(2,128)(2,1)}, u32[]{:S(2)}, u32[]{:S(2)}) async-start(bf16[2,2,2048,128]{3,1,0,2:T(2,128)(2,1)} %bitcast.77), calls=%async_computation.1 | async-start | bytes 4194304 | tf_op jit(solution)/shard_map/all_to_all | solution.py:186
  78.2 1.6 copy-start
  105.7 6.6 %copy-start.1 = (f32[256,1536]{1,0:T(8,128)S(1)}, f32[256,1536]{1,0:T(8,128)}, u32[]{:S(2)}) copy-start(f32[256,1536]{1,0:T(8,128)} %shard_map.28) | copy-start | bytes 4718596
  107.0 5.3 %collective-permute-start = (f32[2,64,1536]{2,1,0:T(8,128)S(1)}, f32[2,64,1536]{2,1,0:T(8,128)S(1)}, u32[]{:S(2)}, u32[]{:S(2)}) collective-permute-start(f32[2,64,1536]{2,1,0:T(8,128)S(1)} %dynamic-slice_bitcast_fusion), channel_id=1, source_target_pairs={{0,1},{1,0},{2,3},{3,2},{4,5},{5,4},{6,7},{7,6},{8,9},{9,8},{10,11... | collective-permute-start | bytes 2359304 | tf_op jit(solution)/shard_map/ppermute | solution.py:133
  132.0 20.9 %copy-start.4 = (f32[256,512]{1,0:T(8,128)S(1)}, f32[256,512]{1,0:T(8,128)}, u32[]{:S(2)}) copy-start(f32[256,512]{1,0:T(8,128)} %shard_map.30) | copy-start | bytes 1572868
  132.0 20.9 %collective-permute-start.4 = (f32[2,64,512]{2,1,0:T(8,128)S(1)}, f32[2,64,512]{2,1,0:T(8,128)S(1)}, u32[]{:S(2)}, u32[]{:S(2)}) collective-permute-start(f32[2,64,512]{2,1,0:T(8,128)S(1)} %dynamic-slice_bitcast_fusion.3), channel_id=1, source_target_pairs={{0,1},{1,0},{2,3},{3,2},{4,5},{5,4},{6,7},{7,6},{8,9},{9,8},{10,11... | collective-permute-start | bytes 786440 | tf_op jit(solution)/shard_map/ppermute | solution.py:133
  150.3 3.4 %copy-start.3 = (f32[256,1024]{1,0:T(8,128)S(1)}, f32[256,1024]{1,0:T(8,128)}, u32[]{:S(2)}) copy-start(f32[256,1024]{1,0:T(8,128)} %shard_map.29) | copy-start | bytes 3145732
  151.5 2.3 %collective-permute-start.2 = (f32[2,64,1024]{2,1,0:T(8,128)S(1)}, f32[2,64,1024]{2,1,0:T(8,128)S(1)}, u32[]{:S(2)}, u32[]{:S(2)}) collective-permute-start(f32[2,64,1024]{2,1,0:T(8,128)S(1)} %dynamic-slice_bitcast_fusion.1), channel_id=1, source_target_pairs={{0,1},{1,0},{2,3},{3,2},{4,5},{5,4},{6,7},{7,6},{8,9},{9,8},{10,11... | collective-permute-start | bytes 1572872 | tf_op jit(solution)/shard_map/ppermute | solution.py:133
  152.1 10.7 %collective-permute-start.1 = (f32[64,1536]{1,0:T(8,128)S(1)}, f32[64,1536]{1,0:T(8,128)S(1)}, u32[]{:S(2)}, u32[]{:S(2)}) collective-permute-start(f32[64,1536]{1,0:T(8,128)S(1)} %dynamic-slice_bitcast_fusion.2), channel_id=1, source_target_pairs={{0,2},{2,0},{1,3},{3,1},{4,6},{6,4},{5,7},{7,5},{8,10},{10,8},{9,1... | collective-permute-start | bytes 1179656 | tf_op jit(solution)/shard_map/ppermute | solution.py:136
  153.0 12.6 %collective-permute-start.5 = (f32[64,512]{1,0:T(8,128)S(1)}, f32[64,512]{1,0:T(8,128)S(1)}, u32[]{:S(2)}, u32[]{:S(2)}) collective-permute-start(f32[64,512]{1,0:T(8,128)S(1)} %dynamic-slice_bitcast_fusion.5), channel_id=1, source_target_pairs={{0,2},{2,0},{1,3},{3,1},{4,6},{6,4},{5,7},{7,5},{8,10},{10,8},{9,1... | collective-permute-start | bytes 393224 | tf_op jit(solution)/shard_map/ppermute | solution.py:136
  153.9 17.3 %collective-permute-start.3 = (f32[64,1024]{1,0:T(8,128)S(1)}, f32[64,1024]{1,0:T(8,128)S(1)}, u32[]{:S(2)}, u32[]{:S(2)}) collective-permute-start(f32[64,1024]{1,0:T(8,128)S(1)} %dynamic-slice_bitcast_fusion.4), channel_id=1, source_target_pairs={{0,2},{2,0},{1,3},{3,1},{4,6},{6,4},{5,7},{7,5},{8,10},{10,8},{9,1... | collective-permute-start | bytes 786440 | tf_op jit(solution)/shard_map/ppermute | solution.py:136

commit v8 on v7

--- a/solution.py
+++ b/solution.py
@@ -7,6 +7,7 @@
 from jax.experimental.pallas import tpu as pltpu
 from jax.sharding import PartitionSpec as P
 
+
 BINS = 4096
 BLOCK = 64
 LAGS = 256
@@ -17,24 +18,6 @@
 ROWS = 16
 
 EPSILON = 1e-05
-
-
-def block_sums(spec):
-    values = spec.astype(jnp.float32)
-    magnitude = jnp.sqrt(
-        values[..., 0, :] * values[..., 0, :] + values[..., 1, :] * values[..., 1, :]
-    )
-    full_shape = magnitude.shape
-    return magnitude.reshape(full_shape[:-1] + (full_shape[-1] // BLOCK, BLOCK)).sum(axis=-1)
-
-
-def level_divide(spec, padded):
-    block_num = padded.shape[-1] - 2
-    level_mean = (padded[..., :-2] + padded[..., 1:-1] + padded[..., 2:]) / (3.0 * BLOCK)
-    full_shape = spec.shape
-    grid_view = spec.astype(jnp.float32).reshape(full_shape[:-1] + (block_num, BLOCK))
-    whitened = grid_view / (level_mean[..., None, :, None] + EPSILON)
-    return whitened.reshape(full_shape).astype(jnp.bfloat16)
 
 
 def make_table(total_hours):
@@ -130,14 +113,15 @@
     blocks = projected.reshape(2, 2, lags // 4, width)
     keep = lax.dynamic_index_in_dim(blocks, core, axis=1, keepdims=False)
     send = lax.dynamic_index_in_dim(blocks, 1 - core, axis=1, keepdims=False)
-    half = keep + lax.ppermute(send, "tm", perm=[(0, 1), (1, 0), (2, 3), (3, 2)])
+    got = lax.ppermute(send, "tm", perm=[(0, 1), (1, 0), (2, 3), (3, 2)])
+    half = keep + got
     keep = lax.dynamic_index_in_dim(half, z_lo, axis=0, keepdims=False)
     send = lax.dynamic_index_in_dim(half, 1 - z_lo, axis=0, keepdims=False)
-    return keep + lax.ppermute(send, "tm", perm=[(0, 2), (2, 0), (1, 3), (3, 1)])
+    got = lax.ppermute(send, "tm", perm=[(0, 2), (2, 0), (1, 3), (3, 1)])
+    return keep + got
 
 
 def whiten(joined):
-    hours_dev = joined.shape[0]
     values = joined.astype(jnp.float32)
     magnitude = jnp.sqrt(values[:, 0] * values[:, 0] + values[:, 1] * values[:, 1])
     block_num = BINS // BLOCK
@@ -170,7 +154,7 @@
 
 
 def local(spectra, src_ids):
-    hours_dev, stations, _, bins_dev = spectra.shape
+    hours_dev, stations, _, _ = spectra.shape
     shards = lax.axis_size("sta")
     stations_dev = stations // shards
     half = stations_dev // 2
@@ -187,11 +171,15 @@
     white_a = whiten(joined_a)
     row_count = transform.shape[0] // lax.axis_size("tm")
     sources = white_a[:, :, half:half + count_all]
-    part_a = reduce_lags(cross_project(white_a, sources, transform, half))
+    out_a = cross_project(white_a, sources, transform, half)
+    part_a = reduce_lags(out_a)
     white_b = whiten(joined_b)
     split = (ROUNDS - 1) * NSRC
-    part_b1 = reduce_lags(cross_project(white_b, sources[:, :, :split], transform, half))
-    part_b2 = reduce_lags(cross_project(white_b, sources[:, :, split:], transform, half))
+    out_b1 = cross_project(white_b, sources[:, :, :split], transform, half)
+    white_b, out_b1 = lax.optimization_barrier((white_b, out_b1))
+    part_b1 = reduce_lags(out_b1)
+    out_b2 = cross_project(white_b, sources[:, :, split:], transform, half)
+    part_b2 = reduce_lags(out_b2)
     part_b = jnp.concatenate(
         [
             part_b1.reshape(row_count, ROUNDS - 1, NSRC, half),

time: 173 us -> 172 us (level)
  waiting for transfers between devices: 29.7 us -> 27.2 us
  other arithmetic: 31.3 us -> 33.1 us
    ppermute x6, waiting for transfers between devices: 16.1 us -> 13.7 us  [the longest x3 13.7 us: reduce_lags(): got = lax.ppermute(send, 'tm', perm=[(0, 2), (2, 0), (1, 3), (3, 1)])]
    add x6, other arithmetic: 0.29 us -> 2.17 us  [the longest x3 1.16 us: reduce_lags(): half = keep + got]
    unnamed x11 -> x9, local copies, waits for them, and re-layouts: 5.86 us -> 5.86 us
  transfers between devices with their start and end apart: 8 -> 8, of which waited for: 4 -> 4; matrix products, arithmetic and copies ran while one was open for 23% -> 24% of each run, Pallas kernels for 25% -> 15%
where the time goes in v8:
time: 172 us
  Pallas kernels  54.4 us (32%)
  other arithmetic  33.1 us (19%)
  local copies, waits for them, and re-layouts  27.6 us (16%)
  waiting for transfers between devices  27.2 us (16%)
  starting transfers between devices  21.8 us (13%)
  matrix products  7.11 us (4%)
    pallas_call x3, Pallas kernels, cross_project(): pl.pallas_call(cross_project_kernel, grid=(steps,), in_specs=[pl.BlockSpe...  54.4 us
    another operation x1, other arithmetic  18.2 us
    ppermute x3, waiting for transfers between devices, reduce_lags(): got = lax.ppermute(send, 'tm', perm=[(0, 2), (2, 0), (1, 3), (3, 1)])  13.7 us
    all_to_all x1, waiting for transfers between devices, local(): lax.all_to_all(send_a, 'sta', split_axis=2, concat_axis=3, tiled=True)  13.5 us
    all_to_all x1, starting transfers between devices, local(): lax.all_to_all(send_a, 'sta', split_axis=2, concat_axis=3, tiled=True)  11.4 us
    unnamed x9, local copies, waits for them, and re-layouts  5.86 us
    all_to_all x1, starting transfers between devices, local(): lax.all_to_all(send_b, 'sta', split_axis=2, concat_axis=3, tiled=True)  5.41 us
    concatenate x1, other arithmetic, to_send(): chunks = jnp.concatenate([chunks, copies], axis=3)  5.31 us
  transfers between devices with their start and end apart: 8, of which 4 were waited for; matrix products, arithmetic and copies ran while one was open for 24% of the time, Pallas kernels for 15%

profile of v8, /device:TPU:1, one launch (start us, length us, event | category | flops | bytes accessed | tf_op | source)
XLA Modules:
  0.0 171.5 jit_solution(14739139309633499147)
XLA Ops:
  1.6 2.8 %gather_fusion = bf16[24,2,2,128]{3,2,1,0:T(2,128)(2,1)S(1)} fusion(bf16[2,4096,2,128]{3,2,1,0:T(2,128)(2,1)} %param.2, s32[1024]{0:T(1024)S(1)} %pad_clamp_fusion), kind=kCustom, calls=%fused_computation | custom fusion | bytes 49248 | tf_op jit(solution)/shard_map/jit(_take)/gather | solution.py:163
  4.4 3.3 %copy_bitcast_fusion.2 = bf16[2,2,32,64,128]{4,1,0,3,2:T(2,128)(2,1)S(1)} fusion(bf16[2,32,128,2,128]{4,3,2,1,0:T(2,128)(2,1)} %bitcast.80), kind=kLoop, calls=%fused_computation.31 | loop fusion | bytes 4194304 | tf_op jit(solution)/shard_map/transpose | solution.py:147
  8.2 5.3 %pad_maximum_fusion.1 = bf16[2,2,32,88,128]{4,1,0,3,2:T(2,128)(2,1)} fusion(bf16[2,2,32,24,128]{4,1,0,3,2:T(2,128)(2,1)S(1)} %broadcast_in_dim.22, bf16[2,2,32,64,128]{4,1,0,3,2:T(2,128)(2,1)S(1)} %copy_bitcast_fusion.2), kind=kLoop, calls=%fused_computation.24 | loop fusion | flops 1441792 | bytes 5767168 | tf_op jit(solution)/shard_map/concatenate | solution.py:152
  13.5 11.4 %all-to-all-start = ((bf16[2,2,2816,128]{3,1,0,2:T(2,128)(2,1)}), bf16[2,2,2816,128]{3,1,0,2:T(2,128)(2,1)S(1)}, u32[]{:S(2)}, u32[]{:S(2)}) async-start(bf16[2,2,2816,128]{3,1,0,2:T(2,128)(2,1)} %bitcast.75), calls=%async_computation | async-start | bytes 5767168 | tf_op jit(solution)/shard_map/all_to_all | solution.py:165
  24.9 18.2 %multiply_convert_fusion.1 = (bf16[256,4096]{1,0:T(8,128)(2,1)S(1)}, bf16[256,4096]{1,0:T(8,128)(2,1)S(1)}) fusion(s32[256]{0:T(256)S(1)} %iota_add_fusion), kind=kLoop, calls=%fused_computation.13 | loop fusion | flops 19922944 | bytes 4195328 | tf_op jit(solution)/shard_map/convert.3
  43.1 2.6 %pad_maximum_fusion.tre_ref.tim_ref = bf16[256,8192]{1,0:T(8,128)(2,1)} fusion(bf16[256,4096]{1,0:T(8,128)(2,1)S(1)} %get-tuple-element.18, bf16[256,4096]{1,0:T(8,128)(2,1)S(1)} %get-tuple-element.17), kind=kLoop, calls=%fused_computation.9 | loop fusion | flops 8388608 | bytes 8388608 | tf_op jit(solution)/shard_map/concatenate | solution.py:29
  45.7 1.1 copy-done.2
  46.8 1.8 %slice.62 = bf16[2,32,64,2,128]{4,3,2,1,0:T(2,128)(2,1)S(1)} slice(bf16[2,32,128,2,128]{4,3,2,1,0:T(2,128)(2,1)S(1)} %bitcast.81), slice={[0:2], [0:32], [64:128], [0:2], [0:128]} | slice | bytes 4194304 | tf_op jit(solution)/shard_map/slice | solution.py:147
  48.6 3.1 %copy.17 = bf16[2,32,64,2,128]{4,3,0,2,1:T(2,128)(2,1)} copy(bf16[2,32,64,2,128]{4,3,2,1,0:T(2,128)(2,1)S(1)} %slice.62) | data formatting | bytes 4194304
  51.8 13.5 %all-to-all-done = bf16[2,2,2816,128]{3,1,0,2:T(2,128)(2,1)S(1)} async-done(((bf16[2,2,2816,128]{3,1,0,2:T(2,128)(2,1)}), bf16[2,2,2816,128]{3,1,0,2:T(2,128)(2,1)S(1)}, u32[]{:S(2)}, u32[]{:S(2)}) %all-to-all-start) | async-done | bytes 2883616 | tf_op jit(solution)/shard_map/all_to_all | solution.py:165
  66.5 5.4 %all-to-all-start.1 = ((bf16[2,2,2048,128]{3,1,0,2:T(2,128)(2,1)}), bf16[2,2,2048,128]{3,1,0,2:T(2,128)(2,1)}, u32[]{:S(2)}, u32[]{:S(2)}) async-start(bf16[2,2,2048,128]{3,1,0,2:T(2,128)(2,1)} %bitcast.77), calls=%async_computation.1 | async-start | bytes 4194304 | tf_op jit(solution)/shard_map/all_to_all | solution.py:170
  72.6 2.8 %fusion.9 = f32[2,88,64]{1,2,0:T(8,128)S(1)} fusion(f32[2,2,88,4096]{3,2,1,0:T(8,128)S(1)} %convert_element_type.34, s32[4096]{0:T(1024)S(1)} %get-tuple-element.19, s32[4096]{0:T(1024)S(1)} %get-tuple-element.20, pred[4096]{0:T(1024)(128)(4,1)S(1)} %fusion.38), kind=kOutput, calls=%fused_computation.22 | convolution fusion | flops 556335104 | bytes 5849088 | tf_op jit(solution)/shard_map/hrf,fb->hrb/dot_general | solution.py:132
  75.5 1.4 fusion.21
  76.8 1.4 divide_convert_fusion.x_ref
  78.2 1.6 copy-done
  79.8 0.9 slice.66.y_ref
  80.8 25.0 %shard_map.28 = f32[256,1536]{1,0:T(8,128)} custom-call(bf16[2,2,88,4096]{3,2,1,0:T(8,128)(2,1)} %copy-done, bf16[2,2,24,4096]{3,2,1,0:T(8,128)(2,1)} %slice.66.y_ref, bf16[256,8192]{1,0:T(8,128)(2,1)} %pad_maximum_fusion.tre_ref.tim_ref, bf16[256,8192]{1,0:T(8,128)(2,1)} %pad_maximum_fusion.tre_ref.tim_ref), custom_call_target="tpu_custom_call" | custom-call | tf_op jit(solution)/shard_map/pallas_call | solution.py:88
  105.7 1.3 dynamic-slice_bitcast_fusion
  107.0 2.0 %collective-permute-start = (f32[2,64,1536]{2,1,0:T(8,128)S(1)}, f32[2,64,1536]{2,1,0:T(8,128)S(1)}, u32[]{:S(2)}, u32[]{:S(2)}) collective-permute-start(f32[2,64,1536]{2,1,0:T(8,128)S(1)} %dynamic-slice_bitcast_fusion), channel_id=1, source_target_pairs={{0,1},{1,0},{2,3},{3,2},{4,5},{5,4},{6,7},{7,6},{8,9},{9,8},{10,11... | collective-permute-start | bytes 2359304 | tf_op jit(solution)/shard_map/ppermute | solution.py:116
  109.0 1.9 %slice.69.y_ref = bf16[2,2,16,4096]{3,2,1,0:T(8,128)(2,1)} slice(bf16[2,2,88,4096]{3,2,1,0:T(8,128)(2,1)} %copy-done), slice={[0:2], [0:2], [64:80], [0:4096]} | slice | bytes 1048576 | tf_op jit(solution)/shard_map/slice | solution.py:178
  110.9 1.7 slice.70.y_ref
  112.7 1.9 %copy.14 = bf16[2,2,2048,128]{3,2,1,0:T(8,128)(2,1)S(1)} copy(bf16[2,2,2048,128]{3,1,0,2:T(2,128)(2,1)} %all-to-all-done.1) | data formatting | bytes 4194304 | tf_op jit(solution)/shard_map/all_to_all | solution.py:170
  115.1 1.9 %fusion.14 = f32[2,64,64]{2,1,0:T(8,128)S(1)} fusion(f32[2,2,64,4096]{3,2,1,0:T(8,128)S(1)} %copy_bitcast_fusion, s32[4096]{0:T(1024)S(1)} %get-tuple-element.19, s32[4096]{0:T(1024)S(1)} %get-tuple-element.20, pred[4096]{0:T(1024)(128)(4,1)S(1)} %fusion.38), kind=kOutput, calls=%fused_computation.29 | convolution fusion | flops 404750336 | bytes 4263936 | tf_op jit(solution)/shard_map/hrf,fb->hrb/dot_general | solution.py:132
  117.0 1.0 fusion.23
  118.0 1.8 %divide_convert_fusion.1.x_ref = bf16[2,2,64,4096]{3,2,1,0:T(8,128)(2,1)} fusion(f32[2,64,4096]{2,1,0:T(8,128)S(1)} %fusion.23, bf16[2,2,32,64,128]{4,3,2,1,0:T(8,128)(2,1)S(1)} %bitcast.74), kind=kLoop, calls=%fused_computation.11 | loop fusion | flops 3145728 | bytes 6291456 | tf_op jit(solution)/shard_map/convert_element_type | solution.py:140
  119.8 17.9 %shard_map.29 = f32[256,1024]{1,0:T(8,128)} custom-call(bf16[2,2,64,4096]{3,2,1,0:T(8,128)(2,1)} %divide_convert_fusion.1.x_ref, bf16[2,2,16,4096]{3,2,1,0:T(8,128)(2,1)} %slice.69.y_ref, bf16[256,8192]{1,0:T(8,128)(2,1)} %pad_maximum_fusion.tre_ref.tim_ref, bf16[256,8192]{1,0:T(8,128)(2,1)} %pad_maximum_fusion.tre_ref.tim_ref), custom_call_target="tpu_custom_call" | custom-call | tf_op jit(solution)/shard_map/pallas_call | solution.py:88
  137.8 11.5 %shard_map.30 = f32[256,512]{1,0:T(8,128)} custom-call(bf16[2,2,64,4096]{3,2,1,0:T(8,128)(2,1)} %divide_convert_fusion.1.x_ref, bf16[2,2,8,4096]{3,2,1,0:T(8,128)(2,1)} %slice.70.y_ref, bf16[256,8192]{1,0:T(8,128)(2,1)} %pad_maximum_fusion.tre_ref.tim_ref, bf16[256,8192]{1,0:T(8,128)(2,1)} %pad_maximum_fusion.tre_ref.tim_ref), custom_call_target="tpu_custom_call" | custom-call | tf_op jit(solution)/shard_map/pallas_call | solution.py:88
  149.3 1.0 dynamic-slice_bitcast_fusion.3
  151.9 1.0 bitcast_add_fusion.3
  155.2 6.5 %collective-permute-done.1 = f32[64,1536]{1,0:T(8,128)S(1)} collective-permute-done((f32[64,1536]{1,0:T(8,128)S(1)}, f32[64,1536]{1,0:T(8,128)S(1)}, u32[]{:S(2)}, u32[]{:S(2)}) %collective-permute-start.1) | collective-permute-done | bytes 393248 | tf_op jit(solution)/shard_map/ppermute | solution.py:120
  162.0 2.7 %collective-permute-done.5 = f32[64,512]{1,0:T(8,128)} collective-permute-done((f32[64,512]{1,0:T(8,128)}, f32[64,512]{1,0:T(8,128)}, u32[]{:S(2)}, u32[]{:S(2)}) %collective-permute-start.5) | collective-permute-done | bytes 131104 | tf_op jit(solution)/shard_map/ppermute | solution.py:120
  165.6 4.5 %collective-permute-done.3 = f32[64,1024]{1,0:T(8,128)S(1)} collective-permute-done((f32[64,1024]{1,0:T(8,128)S(1)}, f32[64,1024]{1,0:T(8,128)S(1)}, u32[]{:S(2)}, u32[]{:S(2)}) %collective-permute-start.3) | collective-permute-done | bytes 262176 | tf_op jit(solution)/shard_map/ppermute | solution.py:120
  (43 shorter events, 11.1 us)
Async XLA Ops:
  13.5 51.8 %all-to-all-start = ((bf16[2,2,2816,128]{3,1,0,2:T(2,128)(2,1)}), bf16[2,2,2816,128]{3,1,0,2:T(2,128)(2,1)S(1)}, u32[]{:S(2)}, u32[]{:S(2)}) async-start(bf16[2,2,2816,128]{3,1,0,2:T(2,128)(2,1)} %bitcast.75), calls=%async_computation | async-start | bytes 5767168 | tf_op jit(solution)/shard_map/all_to_all | solution.py:165
  43.1 3.7 %copy-start.2 = (bf16[2,4096,2,128]{3,2,1,0:T(2,128)(2,1)S(1)}, bf16[2,4096,2,128]{3,2,1,0:T(2,128)(2,1)}, u32[]{:S(2)}) copy-start(bf16[2,4096,2,128]{3,2,1,0:T(2,128)(2,1)} %param.2) | copy-start | bytes 12582916
  66.5 46.2 %all-to-all-start.1 = ((bf16[2,2,2048,128]{3,1,0,2:T(2,128)(2,1)}), bf16[2,2,2048,128]{3,1,0,2:T(2,128)(2,1)}, u32[]{:S(2)}, u32[]{:S(2)}) async-start(bf16[2,2,2048,128]{3,1,0,2:T(2,128)(2,1)} %bitcast.77), calls=%async_computation.1 | async-start | bytes 4194304 | tf_op jit(solution)/shard_map/all_to_all | solution.py:170
  78.2 1.6 copy-start
  105.7 6.9 %copy-start.1 = (f32[256,1536]{1,0:T(8,128)S(1)}, f32[256,1536]{1,0:T(8,128)}, u32[]{:S(2)}) copy-start(f32[256,1536]{1,0:T(8,128)} %shard_map.28) | copy-start | bytes 4718596
  107.0 5.5 %collective-permute-start = (f32[2,64,1536]{2,1,0:T(8,128)S(1)}, f32[2,64,1536]{2,1,0:T(8,128)S(1)}, u32[]{:S(2)}, u32[]{:S(2)}) collective-permute-start(f32[2,64,1536]{2,1,0:T(8,128)S(1)} %dynamic-slice_bitcast_fusion), channel_id=1, source_target_pairs={{0,1},{1,0},{2,3},{3,2},{4,5},{5,4},{6,7},{7,6},{8,9},{9,8},{10,11... | collective-permute-start | bytes 2359304 | tf_op jit(solution)/shard_map/ppermute | solution.py:116
  137.8 12.6 %copy-start.3 = (f32[256,1024]{1,0:T(8,128)S(1)}, f32[256,1024]{1,0:T(8,128)}, u32[]{:S(2)}) copy-start(f32[256,1024]{1,0:T(8,128)} %shard_map.29) | copy-start | bytes 3145732
  150.2 1.6 collective-permute-start.4
  150.4 3.8 %collective-permute-start.2 = (f32[2,64,1024]{2,1,0:T(8,128)S(1)}, f32[2,64,1024]{2,1,0:T(8,128)S(1)}, u32[]{:S(2)}, u32[]{:S(2)}) collective-permute-start(f32[2,64,1024]{2,1,0:T(8,128)S(1)} %dynamic-slice_bitcast_fusion.1), channel_id=1, source_target_pairs={{0,1},{1,0},{2,3},{3,2},{4,5},{5,4},{6,7},{7,6},{8,9},{9,8},{10,11... | collective-permute-start | bytes 1572872 | tf_op jit(solution)/shard_map/ppermute | solution.py:116
  151.0 10.7 %collective-permute-start.1 = (f32[64,1536]{1,0:T(8,128)S(1)}, f32[64,1536]{1,0:T(8,128)S(1)}, u32[]{:S(2)}, u32[]{:S(2)}) collective-permute-start(f32[64,1536]{1,0:T(8,128)S(1)} %dynamic-slice_bitcast_fusion.2), channel_id=1, source_target_pairs={{0,2},{2,0},{1,3},{3,1},{4,6},{6,4},{5,7},{7,5},{8,10},{10,8},{9,1... | collective-permute-start | bytes 1179656 | tf_op jit(solution)/shard_map/ppermute | solution.py:120
  153.5 11.1 %collective-permute-start.5 = (f32[64,512]{1,0:T(8,128)}, f32[64,512]{1,0:T(8,128)}, u32[]{:S(2)}, u32[]{:S(2)}) collective-permute-start(f32[64,512]{1,0:T(8,128)} %dynamic-slice_bitcast_fusion.5), channel_id=1, source_target_pairs={{0,2},{2,0},{1,3},{3,1},{4,6},{6,4},{5,7},{7,5},{8,10},{10,8},{9,1... | collective-permute-start | bytes 393224 | tf_op jit(solution)/shard_map/ppermute | solution.py:120
  154.4 15.7 %collective-permute-start.3 = (f32[64,1024]{1,0:T(8,128)S(1)}, f32[64,1024]{1,0:T(8,128)S(1)}, u32[]{:S(2)}, u32[]{:S(2)}) collective-permute-start(f32[64,1024]{1,0:T(8,128)S(1)} %dynamic-slice_bitcast_fusion.4), channel_id=1, source_target_pairs={{0,2},{2,0},{1,3},{3,1},{4,6},{6,4},{5,7},{7,5},{8,10},{10,8},{9,1... | collective-permute-start | bytes 786440 | tf_op jit(solution)/shard_map/ppermute | solution.py:120

commit v9 on v8

--- a/solution.py
+++ b/solution.py
@@ -174,19 +174,11 @@
     out_a = cross_project(white_a, sources, transform, half)
     part_a = reduce_lags(out_a)
     white_b = whiten(joined_b)
-    split = (ROUNDS - 1) * NSRC
-    out_b1 = cross_project(white_b, sources[:, :, :split], transform, half)
-    white_b, out_b1 = lax.optimization_barrier((white_b, out_b1))
-    part_b1 = reduce_lags(out_b1)
-    out_b2 = cross_project(white_b, sources[:, :, split:], transform, half)
-    part_b2 = reduce_lags(out_b2)
+    out_b = cross_project(white_b, sources, transform, half)
+    cols = out_b.shape[1] // 2
     part_b = jnp.concatenate(
-        [
-            part_b1.reshape(row_count, ROUNDS - 1, NSRC, half),
-            part_b2.reshape(row_count, 1, NSRC, half),
-        ],
-        axis=1,
-    )
+        [reduce_lags(out_b[:, :cols]), reduce_lags(out_b[:, cols:])], axis=1
+    ).reshape(row_count, ROUNDS, NSRC, half)
     both = jnp.concatenate(
         [part_a.reshape(row_count, ROUNDS, NSRC, half), part_b], axis=3
     )

time: 172 us -> 163 us (0.948)
  Pallas kernels: 54.4 us -> 49.8 us
  waiting for transfers between devices: 27.2 us -> 24.8 us
  local copies, waits for them, and re-layouts: 27.6 us -> 25.3 us
    ppermute x3, waiting for transfers between devices: 13.7 us -> 8.65 us  [reduce_lags(): got = lax.ppermute(send, 'tm', perm=[(0, 2), (2, 0), (1, 3), (3, 1)])]
    pallas_call x3 -> x2, Pallas kernels: 54.4 us -> 49.8 us  [cross_project(): pl.pallas_call(cross_project_kernel, grid=(steps,), in_specs=[pl.BlockSpe...]
    ppermute x3, waiting for transfers between devices: 0.05 us -> 2.58 us  [reduce_lags(): got = lax.ppermute(send, 'tm', perm=[(0, 1), (1, 0), (2, 3), (3, 2)])]
    slice x2 -> x1, local copies, waits for them, and re-layouts: 3.55 us -> 1.47 us  [local(): out_b[:, :cols]]
    unnamed x9 -> x5, local copies, waits for them, and re-layouts: 5.86 us -> 5.86 us
  transfers between devices with their start and end apart: 8 -> 8, of which waited for: 4 -> 5; matrix products, arithmetic and copies ran while one was open for 24% -> 29% of each run, Pallas kernels for 15% -> 31%
where the time goes in v9:
time: 163 us; the launch traced here: 162 us
  Pallas kernels  49.8 us (31%)
  other arithmetic  33.4 us (20%)
  local copies, waits for them, and re-layouts  25.3 us (16%)
  waiting for transfers between devices  24.8 us (15%)
  starting transfers between devices  21.9 us (13%)
  matrix products  7.1 us (4%)
    pallas_call x2, Pallas kernels, cross_project(): pl.pallas_call(cross_project_kernel, grid=(steps,), in_specs=[pl.BlockSpe...  49.8 us
    another operation x1, other arithmetic  18.2 us
    all_to_all x1, waiting for transfers between devices, local(): lax.all_to_all(send_a, 'sta', split_axis=2, concat_axis=3, tiled=True)  13.5 us
    all_to_all x1, starting transfers between devices, local(): lax.all_to_all(send_a, 'sta', split_axis=2, concat_axis=3, tiled=True)  11.4 us
    ppermute x3, waiting for transfers between devices, reduce_lags(): got = lax.ppermute(send, 'tm', perm=[(0, 2), (2, 0), (1, 3), (3, 1)])  8.65 us
    unnamed x5, local copies, waits for them, and re-layouts  5.86 us
    all_to_all x1, starting transfers between devices, local(): lax.all_to_all(send_b, 'sta', split_axis=2, concat_axis=3, tiled=True)  5.41 us
    concatenate x1, other arithmetic, to_send(): chunks = jnp.concatenate([chunks, copies], axis=3)  5.31 us
  transfers between devices with their start and end apart: 8, of which 5 were waited for; matrix products, arithmetic and copies ran while one was open for 29% of the time, Pallas kernels for 31%

profile of v9, /device:TPU:1, one launch (start us, length us, event | category | flops | bytes accessed | tf_op | source)
XLA Modules:
  0.0 162.4 jit_solution(15157331178348179917)
XLA Ops:
  1.6 2.8 %gather_fusion = bf16[24,2,2,128]{3,2,1,0:T(2,128)(2,1)S(1)} fusion(bf16[2,4096,2,128]{3,2,1,0:T(2,128)(2,1)} %param.2, s32[1024]{0:T(1024)S(1)} %pad_clamp_fusion), kind=kCustom, calls=%fused_computation | custom fusion | bytes 49248 | tf_op jit(solution)/shard_map/jit(_take)/gather | solution.py:163
  4.4 3.3 %copy_bitcast_fusion.2 = bf16[2,2,32,64,128]{4,1,0,3,2:T(2,128)(2,1)S(1)} fusion(bf16[2,32,128,2,128]{4,3,2,1,0:T(2,128)(2,1)} %bitcast.80), kind=kLoop, calls=%fused_computation.31 | loop fusion | bytes 4194304 | tf_op jit(solution)/shard_map/transpose | solution.py:147
  8.2 5.3 %pad_maximum_fusion.1 = bf16[2,2,32,88,128]{4,1,0,3,2:T(2,128)(2,1)} fusion(bf16[2,2,32,24,128]{4,1,0,3,2:T(2,128)(2,1)S(1)} %broadcast_in_dim.22, bf16[2,2,32,64,128]{4,1,0,3,2:T(2,128)(2,1)S(1)} %copy_bitcast_fusion.2), kind=kLoop, calls=%fused_computation.24 | loop fusion | flops 1441792 | bytes 5767168 | tf_op jit(solution)/shard_map/concatenate | solution.py:152
  13.5 11.4 %all-to-all-start = ((bf16[2,2,2816,128]{3,1,0,2:T(2,128)(2,1)}), bf16[2,2,2816,128]{3,1,0,2:T(2,128)(2,1)S(1)}, u32[]{:S(2)}, u32[]{:S(2)}) async-start(bf16[2,2,2816,128]{3,1,0,2:T(2,128)(2,1)} %bitcast.75), calls=%async_computation | async-start | bytes 5767168 | tf_op jit(solution)/shard_map/all_to_all | solution.py:165
  24.9 18.2 %multiply_convert_fusion.1 = (bf16[256,4096]{1,0:T(8,128)(2,1)S(1)}, bf16[256,4096]{1,0:T(8,128)(2,1)S(1)}) fusion(s32[256]{0:T(256)S(1)} %iota_add_fusion), kind=kLoop, calls=%fused_computation.13 | loop fusion | flops 19922944 | bytes 4195328 | tf_op jit(solution)/shard_map/convert.3
  43.1 2.6 %pad_maximum_fusion.tre_ref.tim_ref = bf16[256,8192]{1,0:T(8,128)(2,1)} fusion(bf16[256,4096]{1,0:T(8,128)(2,1)S(1)} %get-tuple-element.16, bf16[256,4096]{1,0:T(8,128)(2,1)S(1)} %get-tuple-element.15), kind=kLoop, calls=%fused_computation.9 | loop fusion | flops 8388608 | bytes 8388608 | tf_op jit(solution)/shard_map/concatenate | solution.py:29
  45.7 1.1 copy-done.1
  46.8 1.8 %slice.60 = bf16[2,32,64,2,128]{4,3,2,1,0:T(2,128)(2,1)S(1)} slice(bf16[2,32,128,2,128]{4,3,2,1,0:T(2,128)(2,1)S(1)} %bitcast.81), slice={[0:2], [0:32], [64:128], [0:2], [0:128]} | slice | bytes 4194304 | tf_op jit(solution)/shard_map/slice | solution.py:147
  48.6 3.1 %copy.17 = bf16[2,32,64,2,128]{4,3,0,2,1:T(2,128)(2,1)} copy(bf16[2,32,64,2,128]{4,3,2,1,0:T(2,128)(2,1)S(1)} %slice.60) | data formatting | bytes 4194304
  51.8 13.5 %all-to-all-done = bf16[2,2,2816,128]{3,1,0,2:T(2,128)(2,1)S(1)} async-done(((bf16[2,2,2816,128]{3,1,0,2:T(2,128)(2,1)}), bf16[2,2,2816,128]{3,1,0,2:T(2,128)(2,1)S(1)}, u32[]{:S(2)}, u32[]{:S(2)}) %all-to-all-start) | async-done | bytes 2883616 | tf_op jit(solution)/shard_map/all_to_all | solution.py:165
  66.5 5.4 %all-to-all-start.1 = ((bf16[2,2,2048,128]{3,1,0,2:T(2,128)(2,1)}), bf16[2,2,2048,128]{3,1,0,2:T(2,128)(2,1)}, u32[]{:S(2)}, u32[]{:S(2)}) async-start(bf16[2,2,2048,128]{3,1,0,2:T(2,128)(2,1)} %bitcast.77), calls=%async_computation.1 | async-start | bytes 4194304 | tf_op jit(solution)/shard_map/all_to_all | solution.py:170
  72.6 2.8 %fusion.9 = f32[2,88,64]{1,2,0:T(8,128)S(1)} fusion(f32[2,2,88,4096]{3,2,1,0:T(8,128)S(1)} %convert_element_type.34, s32[4096]{0:T(1024)S(1)} %get-tuple-element.17, s32[4096]{0:T(1024)S(1)} %get-tuple-element.18, pred[4096]{0:T(1024)(128)(4,1)S(1)} %fusion.38), kind=kOutput, calls=%fused_computation.22 | convolution fusion | flops 556335104 | bytes 5849088 | tf_op jit(solution)/shard_map/hrf,fb->hrb/dot_general | solution.py:132
  75.5 1.4 fusion.21
  76.8 1.4 divide_convert_fusion.x_ref
  78.2 1.6 copy-done
  79.8 0.9 slice.64.y_ref
  80.8 25.0 %shard_map.28 = f32[256,1536]{1,0:T(8,128)} custom-call(bf16[2,2,88,4096]{3,2,1,0:T(8,128)(2,1)} %copy-done, bf16[2,2,24,4096]{3,2,1,0:T(8,128)(2,1)} %slice.64.y_ref, bf16[256,8192]{1,0:T(8,128)(2,1)} %pad_maximum_fusion.tre_ref.tim_ref, bf16[256,8192]{1,0:T(8,128)(2,1)} %pad_maximum_fusion.tre_ref.tim_ref), custom_call_target="tpu_custom_call" | custom-call | tf_op jit(solution)/shard_map/pallas_call | solution.py:88
  105.7 1.2 dynamic-slice_bitcast_fusion
  106.9 1.7 %collective-permute-start = (f32[2,64,1536]{2,1,0:T(8,128)S(1)}, f32[2,64,1536]{2,1,0:T(8,128)S(1)}, u32[]{:S(2)}, u32[]{:S(2)}) collective-permute-start(f32[2,64,1536]{2,1,0:T(8,128)S(1)} %dynamic-slice_bitcast_fusion), channel_id=1, source_target_pairs={{0,1},{1,0},{2,3},{3,2},{4,5},{5,4},{6,7},{7,6},{8,9},{9,8},{10,11... | collective-permute-start | bytes 2359304 | tf_op jit(solution)/shard_map/ppermute | solution.py:116
  108.7 1.9 %collective-permute-done = f32[2,64,1536]{2,1,0:T(8,128)S(1)} collective-permute-done((f32[2,64,1536]{2,1,0:T(8,128)S(1)}, f32[2,64,1536]{2,1,0:T(8,128)S(1)}, u32[]{:S(2)}, u32[]{:S(2)}) %collective-permute-start) | collective-permute-done | bytes 786464 | tf_op jit(solution)/shard_map/ppermute | solution.py:116
  110.6 1.2 bitcast_add_fusion
  111.8 1.1 collective-permute-start.1
  112.9 1.9 %copy.14 = bf16[2,2,2048,128]{3,2,1,0:T(8,128)(2,1)S(1)} copy(bf16[2,2,2048,128]{3,1,0,2:T(2,128)(2,1)} %all-to-all-done.1) | data formatting | bytes 4194304 | tf_op jit(solution)/shard_map/all_to_all | solution.py:170
  115.3 1.9 %fusion.14 = f32[2,64,64]{2,1,0:T(8,128)S(1)} fusion(f32[2,2,64,4096]{3,2,1,0:T(8,128)S(1)} %copy_bitcast_fusion, s32[4096]{0:T(1024)S(1)} %get-tuple-element.17, s32[4096]{0:T(1024)S(1)} %get-tuple-element.18, pred[4096]{0:T(1024)(128)(4,1)S(1)} %fusion.38), kind=kOutput, calls=%fused_computation.29 | convolution fusion | flops 404750336 | bytes 4263936 | tf_op jit(solution)/shard_map/hrf,fb->hrb/dot_general | solution.py:132
  117.2 1.0 fusion.23
  118.2 1.8 %divide_convert_fusion.1.x_ref = bf16[2,2,64,4096]{3,2,1,0:T(8,128)(2,1)} fusion(f32[2,64,4096]{2,1,0:T(8,128)S(1)} %fusion.23, bf16[2,2,32,64,128]{4,3,2,1,0:T(8,128)(2,1)S(1)} %bitcast.74), kind=kLoop, calls=%fused_computation.11 | loop fusion | flops 3145728 | bytes 6291456 | tf_op jit(solution)/shard_map/convert_element_type | solution.py:140
  120.1 24.9 %shard_map.29 = f32[256,1536]{1,0:T(8,128)} custom-call(bf16[2,2,64,4096]{3,2,1,0:T(8,128)(2,1)} %divide_convert_fusion.1.x_ref, bf16[2,2,24,4096]{3,2,1,0:T(8,128)(2,1)} %slice.64.y_ref, bf16[256,8192]{1,0:T(8,128)(2,1)} %pad_maximum_fusion.tre_ref.tim_ref, bf16[256,8192]{1,0:T(8,128)(2,1)} %pad_maximum_fusion.tre_ref.tim_ref), custom_call_target="tpu_custom_call" | custom-call | tf_op jit(solution)/shard_map/pallas_call | solution.py:88
  144.9 1.5 fusion.50
  149.5 1.0 bitcast_add_fusion.1
  152.3 4.5 %collective-permute-done.5 = f32[64,768]{1,0:T(8,128)S(1)} collective-permute-done((f32[64,768]{1,0:T(8,128)S(1)}, f32[64,768]{1,0:T(8,128)S(1)}, u32[]{:S(2)}, u32[]{:S(2)}) %collective-permute-start.5) | collective-permute-done | bytes 196640 | tf_op jit(solution)/shard_map/ppermute | solution.py:120
  156.8 4.2 %collective-permute-done.3 = f32[64,768]{1,0:T(8,128)S(1)} collective-permute-done((f32[64,768]{1,0:T(8,128)S(1)}, f32[64,768]{1,0:T(8,128)S(1)}, u32[]{:S(2)}, u32[]{:S(2)}) %collective-permute-start.3) | collective-permute-done | bytes 196640 | tf_op jit(solution)/shard_map/ppermute | solution.py:120
  161.5 0.9 copy.16
  (37 shorter events, 9.8 us)
Async XLA Ops:
  13.5 51.8 %all-to-all-start = ((bf16[2,2,2816,128]{3,1,0,2:T(2,128)(2,1)}), bf16[2,2,2816,128]{3,1,0,2:T(2,128)(2,1)S(1)}, u32[]{:S(2)}, u32[]{:S(2)}) async-start(bf16[2,2,2816,128]{3,1,0,2:T(2,128)(2,1)} %bitcast.75), calls=%async_computation | async-start | bytes 5767168 | tf_op jit(solution)/shard_map/all_to_all | solution.py:165
  43.1 3.7 %copy-start.1 = (bf16[2,4096,2,128]{3,2,1,0:T(2,128)(2,1)S(1)}, bf16[2,4096,2,128]{3,2,1,0:T(2,128)(2,1)}, u32[]{:S(2)}) copy-start(bf16[2,4096,2,128]{3,2,1,0:T(2,128)(2,1)} %param.2) | copy-start | bytes 12582916
  66.5 46.4 %all-to-all-start.1 = ((bf16[2,2,2048,128]{3,1,0,2:T(2,128)(2,1)}), bf16[2,2,2048,128]{3,1,0,2:T(2,128)(2,1)}, u32[]{:S(2)}, u32[]{:S(2)}) async-start(bf16[2,2,2048,128]{3,1,0,2:T(2,128)(2,1)} %bitcast.77), calls=%async_computation.1 | async-start | bytes 4194304 | tf_op jit(solution)/shard_map/all_to_all | solution.py:170
  78.2 1.6 copy-start
  106.9 3.6 %collective-permute-start = (f32[2,64,1536]{2,1,0:T(8,128)S(1)}, f32[2,64,1536]{2,1,0:T(8,128)S(1)}, u32[]{:S(2)}, u32[]{:S(2)}) collective-permute-start(f32[2,64,1536]{2,1,0:T(8,128)S(1)} %dynamic-slice_bitcast_fusion), channel_id=1, source_target_pairs={{0,1},{1,0},{2,3},{3,2},{4,5},{5,4},{6,7},{7,6},{8,9},{9,8},{10,11... | collective-permute-start | bytes 2359304 | tf_op jit(solution)/shard_map/ppermute | solution.py:116
  111.8 36.8 %collective-permute-start.1 = (f32[64,1536]{1,0:T(8,128)S(1)}, f32[64,1536]{1,0:T(8,128)S(1)}, u32[]{:S(2)}, u32[]{:S(2)}) collective-permute-start(f32[64,1536]{1,0:T(8,128)S(1)} %dynamic-slice_bitcast_fusion.3), channel_id=1, source_target_pairs={{0,2},{2,0},{1,3},{3,1},{4,6},{6,4},{5,7},{7,5},{8,10},{10,8},{9,1... | collective-permute-start | bytes 1179656 | tf_op jit(solution)/shard_map/ppermute | solution.py:120
  147.2 2.4 %collective-permute-start.4 = (f32[2,64,768]{2,1,0:T(8,128)}, f32[2,64,768]{2,1,0:T(8,128)}, u32[]{:S(2)}, u32[]{:S(2)}) collective-permute-start(f32[2,64,768]{2,1,0:T(8,128)} %dynamic-slice_bitcast_fusion.1), channel_id=1, source_target_pairs={{0,1},{1,0},{2,3},{3,2},{4,5},{5,4},{6,7},{7,6},{8,9},{9,8},{10,11... | collective-permute-start | bytes 1179656 | tf_op jit(solution)/shard_map/ppermute | solution.py:116
  148.6 2.8 %collective-permute-start.2 = (f32[2,64,768]{2,1,0:T(8,128)}, f32[2,64,768]{2,1,0:T(8,128)S(1)}, u32[]{:S(2)}, u32[]{:S(2)}) collective-permute-start(f32[2,64,768]{2,1,0:T(8,128)} %dynamic-slice_bitcast_fusion.2), channel_id=1, source_target_pairs={{0,1},{1,0},{2,3},{3,2},{4,5},{5,4},{6,7},{7,6},{8,9},{9,8},{10,11... | collective-permute-start | bytes 1179656 | tf_op jit(solution)/shard_map/ppermute | solution.py:116
  150.6 6.2 %collective-permute-start.5 = (f32[64,768]{1,0:T(8,128)S(1)}, f32[64,768]{1,0:T(8,128)S(1)}, u32[]{:S(2)}, u32[]{:S(2)}) collective-permute-start(f32[64,768]{1,0:T(8,128)S(1)} %dynamic-slice_bitcast_fusion.4), channel_id=1, source_target_pairs={{0,2},{2,0},{1,3},{3,1},{4,6},{6,4},{5,7},{7,5},{8,10},{10,8},{9,1... | collective-permute-start | bytes 589832 | tf_op jit(solution)/shard_map/ppermute | solution.py:120
  151.5 9.5 %collective-permute-start.3 = (f32[64,768]{1,0:T(8,128)S(1)}, f32[64,768]{1,0:T(8,128)S(1)}, u32[]{:S(2)}, u32[]{:S(2)}) collective-permute-start(f32[64,768]{1,0:T(8,128)S(1)} %dynamic-slice_bitcast_fusion.5), channel_id=1, source_target_pairs={{0,2},{2,0},{1,3},{3,1},{4,6},{6,4},{5,7},{7,5},{8,10},{10,8},{9,1... | collective-permute-start | bytes 589832 | tf_op jit(solution)/shard_map/ppermute | solution.py:120

commit v10 on v9

--- a/solution.py
+++ b/solution.py
@@ -153,35 +153,55 @@
     return chunks.reshape(hours_dev, 2, -1, bins_dev)
 
 
+def reduce_direct(projected):
+    index = lax.axis_index("tm")
+    lags, width = projected.shape
+    parts = lax.axis_size("tm")
+    blocks = projected.reshape(parts, lags // parts, width)
+    total = lax.dynamic_index_in_dim(blocks, index, axis=0, keepdims=False)
+    for mask in range(1, parts):
+        send = lax.dynamic_index_in_dim(blocks, index ^ mask, axis=0, keepdims=False)
+        total = total + lax.ppermute(
+            send, "tm", perm=[(i, i ^ mask) for i in range(parts)]
+        )
+    return total
+
+
+SPLITS = (32, 48, 48)
+
+
 def local(spectra, src_ids):
-    hours_dev, stations, _, _ = spectra.shape
-    shards = lax.axis_size("sta")
-    stations_dev = stations // shards
-    half = stations_dev // 2
+    hours_dev, _, _, _ = spectra.shape
     flat_ids = src_ids.reshape(-1)
     count_all = flat_ids.shape[0]
     src_raw = jnp.transpose(jnp.take(spectra, flat_ids, axis=1), (0, 2, 1, 3))
-    send_a = to_send(spectra, 0, half, src_raw)
-    joined_a = lax.all_to_all(send_a, "sta", split_axis=2, concat_axis=3, tiled=True)
+    starts = [sum(SPLITS[:i]) for i in range(len(SPLITS))]
+    send = to_send(spectra, 0, SPLITS[0], src_raw)
+    joined = [lax.all_to_all(send, "sta", split_axis=2, concat_axis=3, tiled=True)]
     transform = make_table(hours_dev * lax.axis_size("tm"))
-    spectra_b, transform = lax.optimization_barrier((spectra, transform))
-    send_b = to_send(spectra_b, half, stations_dev - half, None)
-    send_b, joined_a = lax.optimization_barrier((send_b, joined_a))
-    joined_b = lax.all_to_all(send_b, "sta", split_axis=2, concat_axis=3, tiled=True)
-    white_a = whiten(joined_a)
+    spectra_late, transform = lax.optimization_barrier((spectra, transform))
+    for part in range(1, len(SPLITS)):
+        send = to_send(spectra_late, starts[part], SPLITS[part], None)
+        send, last = lax.optimization_barrier((send, joined[-1]))
+        joined[-1] = last
+        joined.append(lax.all_to_all(send, "sta", split_axis=2, concat_axis=3, tiled=True))
     row_count = transform.shape[0] // lax.axis_size("tm")
-    sources = white_a[:, :, half:half + count_all]
-    out_a = cross_project(white_a, sources, transform, half)
-    part_a = reduce_lags(out_a)
-    white_b = whiten(joined_b)
-    out_b = cross_project(white_b, sources, transform, half)
-    cols = out_b.shape[1] // 2
-    part_b = jnp.concatenate(
-        [reduce_lags(out_b[:, :cols]), reduce_lags(out_b[:, cols:])], axis=1
-    ).reshape(row_count, ROUNDS, NSRC, half)
-    both = jnp.concatenate(
-        [part_a.reshape(row_count, ROUNDS, NSRC, half), part_b], axis=3
-    )
+    pieces = []
+    sources = None
+    for part, count in enumerate(SPLITS):
+        white = whiten(joined[part])
+        if sources is None:
+            sources = white[:, :, count:count + count_all]
+        out = cross_project(white, sources, transform, count)
+        if part + 1 < len(SPLITS):
+            reduced = reduce_direct(out)
+        else:
+            cols = out.shape[1] // 2
+            reduced = jnp.concatenate(
+                [reduce_lags(out[:, :cols]), reduce_lags(out[:, cols:])], axis=1
+            )
+        pieces.append(reduced.reshape(row_count, ROUNDS, NSRC, count))
+    both = jnp.concatenate(pieces, axis=3)
     return jnp.transpose(both, (1, 0, 2, 3))
 
 

time: 163 us -> 194 us (1.19)
  starting transfers between devices: 21.9 us -> 37.1 us
  local copies, waits for them, and re-layouts: 25.3 us -> 35.2 us
  Pallas kernels: 49.8 us -> 58 us
  waiting for transfers between devices: 24.8 us -> 20.1 us
    all_to_all x2 -> x3, starting transfers between devices: 16.8 us -> 30.7 us  [local(): lax.all_to_all(send, 'sta', split_axis=2, concat_axis=3, tiled=True)]
    all_to_all x2 -> x3, waiting for transfers between devices: 13.5 us -> 0.01 us  [local(): lax.all_to_all(send, 'sta', split_axis=2, concat_axis=3, tiled=True)]
    ppermute x0 -> x6, waiting for transfers between devices: none -> 11.9 us  [reduce_direct(): lax.ppermute(send, 'tm', perm=[(i, i ^ mask) for i in range(parts)])]
    pallas_call x2 -> x3, Pallas kernels: 49.8 us -> 58 us  [cross_project(): pl.pallas_call(cross_project_kernel, grid=(steps,), in_specs=[pl.BlockSpe...]
    dynamic_slice x0 -> x5, local copies, waits for them, and re-layouts: none -> 7 us  [the longest x3 4.69 us: reduce_direct(): lax.dynamic_index_in_dim(blocks, index ^ mask, axis=0, keepdims=False)]
    ppermute x0 -> x6, starting transfers between devices: none -> 5.11 us  [reduce_direct(): lax.ppermute(send, 'tm', perm=[(i, i ^ mask) for i in range(parts)])]
    squeeze x3 -> x2, local copies, waits for them, and re-layouts: 2.75 us -> 0.06 us  [reduce_lags(): send = lax.dynamic_index_in_dim(blocks, 1 - core, axis=1, keepdims=False)]
    add x0 -> x2, other arithmetic: none -> 2.6 us  [reduce_direct(): total + lax.ppermute(send, 'tm', perm=[(i, i ^ mask) for i in range(parts)])]
  transfers between devices with their start and end apart: 8 -> 13, of which waited for: 5 -> 5; matrix products, arithmetic and copies ran while one was open for 29% -> 31% of each run, Pallas kernels for 31% -> 30%
where the time goes in v10:
time: 194 us; the launch traced here: 193 us
  Pallas kernels  58 us (30%)
  starting transfers between devices  37.1 us (19%)
  local copies, waits for them, and re-layouts  35.2 us (18%)
  other arithmetic  34.8 us (18%)
  waiting for transfers between devices  20.1 us (10%)
  matrix products  7.29 us (4%)
    pallas_call x3, Pallas kernels, cross_project(): pl.pallas_call(cross_project_kernel, grid=(steps,), in_specs=[pl.BlockSpe...  58 us
    all_to_all x3, starting transfers between devices, local(): lax.all_to_all(send, 'sta', split_axis=2, concat_axis=3, tiled=True)  30.7 us
    another operation x1, other arithmetic  19 us
    ppermute x6, waiting for transfers between devices, reduce_direct(): lax.ppermute(send, 'tm', perm=[(i, i ^ mask) for i in range(parts)])  11.9 us
    unnamed x18, local copies, waits for them, and re-layouts  7.35 us
    ppermute x2, waiting for transfers between devices, reduce_lags(): got = lax.ppermute(send, 'tm', perm=[(0, 2), (2, 0), (1, 3), (3, 1)])  7.14 us
    ppermute x6, starting transfers between devices, reduce_direct(): lax.ppermute(send, 'tm', perm=[(i, i ^ mask) for i in range(parts)])  5.11 us
    dynamic_slice x3, local copies, waits for them, and re-layouts, reduce_direct(): lax.dynamic_index_in_dim(blocks, index ^ mask, axis=0, keepdims=False)  4.69 us
  transfers between devices with their start and end apart: 13, of which 5 were waited for; matrix products, arithmetic and copies ran while one was open for 31% of the time, Pallas kernels for 30%

profile of v10, /device:TPU:1, one launch (start us, length us, event | category | flops | bytes accessed | tf_op | source)
XLA Modules:
  0.0 192.9 jit_solution(1489741233900735773)
XLA Ops:
  1.6 2.8 %gather_fusion = bf16[24,2,2,128]{3,2,1,0:T(2,128)(2,1)S(1)} fusion(bf16[2,4096,2,128]{3,2,1,0:T(2,128)(2,1)} %param.2, s32[1024]{0:T(1024)S(1)} %pad_clamp_fusion), kind=kCustom, calls=%fused_computation | custom fusion | bytes 49248 | tf_op jit(solution)/shard_map/jit(_take)/gather | solution.py:177
  4.4 2.1 %copy_bitcast_fusion.3 = bf16[2,2,32,32,128]{4,1,0,3,2:T(2,128)(2,1)S(1)} fusion(bf16[2,32,128,2,128]{4,3,2,1,0:T(2,128)(2,1)} %bitcast.111), kind=kLoop, calls=%fused_computation.39 | loop fusion | bytes 2097152 | tf_op jit(solution)/shard_map/transpose | solution.py:147
  7.0 3.6 %pad_maximum_fusion.1 = bf16[2,2,32,56,128]{4,1,0,3,2:T(2,128)(2,1)} fusion(bf16[2,2,32,24,128]{4,1,0,3,2:T(2,128)(2,1)S(1)} %broadcast_in_dim.14, bf16[2,2,32,32,128]{4,1,0,3,2:T(2,128)(2,1)S(1)} %copy_bitcast_fusion.3), kind=kLoop, calls=%fused_computation.25 | loop fusion | flops 917504 | bytes 3670016 | tf_op jit(solution)/shard_map/concatenate | solution.py:152
  10.6 11.3 %all-to-all-start = ((bf16[2,2,1792,128]{3,1,0,2:T(2,128)(2,1)}), bf16[2,2,1792,128]{3,1,0,2:T(2,128)(2,1)}, u32[]{:S(2)}, u32[]{:S(2)}) async-start(bf16[2,2,1792,128]{3,1,0,2:T(2,128)(2,1)} %bitcast.7), calls=%async_computation | async-start | bytes 3670016 | tf_op jit(solution)/shard_map/all_to_all | solution.py:180
  21.9 19.0 %multiply_convert_fusion.1 = (bf16[256,4096]{1,0:T(8,128)(2,1)S(1)}, bf16[256,4096]{1,0:T(8,128)(2,1)}) fusion(s32[256]{0:T(256)S(1)} %iota_add_fusion), kind=kLoop, calls=%fused_computation.9 | loop fusion | flops 19922944 | bytes 4195328 | tf_op jit(solution)/shard_map/convert.3
  40.8 4.1 %pad_maximum_fusion.tre_ref.tim_ref = bf16[256,8192]{1,0:T(8,128)(2,1)} fusion(bf16[256,4096]{1,0:T(8,128)(2,1)} %get-tuple-element.29, bf16[256,4096]{1,0:T(8,128)(2,1)S(1)} %get-tuple-element.28), kind=kLoop, calls=%fused_computation.7 | loop fusion | flops 8388608 | bytes 8388608 | tf_op jit(solution)/shard_map/concatenate | solution.py:29
  44.9 3.7 %fusion.76 = (bf16[2,32,48,2,128]{4,3,2,1,0:T(2,128)(2,1)S(1)}, bf16[2,32,48,2,128]{4,3,2,1,0:T(2,128)(2,1)}) fusion(bf16[2,32,128,2,128]{4,3,2,1,0:T(2,128)(2,1)S(1)} %bitcast.112), kind=kLoop, calls=%fused_computation.119 | loop fusion | bytes 6291456 | tf_op jit(solution)/shard_map/slice | solution.py:147
  48.6 2.8 %copy.32 = bf16[2,32,48,2,128]{4,3,0,2,1:T(2,128)(2,1)} copy(bf16[2,32,48,2,128]{4,3,2,1,0:T(2,128)(2,1)S(1)} %get-tuple-element.17) | data formatting | bytes 3145728
  51.5 1.7 copy.19
  53.7 9.4 %all-to-all-start.1 = ((bf16[2,2,1536,128]{3,1,0,2:T(2,128)(2,1)}), bf16[2,2,1536,128]{3,1,0,2:T(2,128)(2,1)S(1)}, u32[]{:S(2)}, u32[]{:S(2)}) async-start(bf16[2,2,1536,128]{3,1,0,2:T(2,128)(2,1)} %bitcast.2), calls=%async_computation.1 | async-start | bytes 3145728 | tf_op jit(solution)/shard_map/all_to_all | solution.py:187
  63.5 1.7 fusion.9
  68.9 15.1 %shard_map.28 = f32[256,768]{1,0:T(8,128)} custom-call(bf16[2,2,56,4096]{3,2,1,0:T(8,128)(2,1)} %copy-done, bf16[2,2,24,4096]{3,2,1,0:T(8,128)(2,1)} %slice.87.y_ref, bf16[256,8192]{1,0:T(8,128)(2,1)} %pad_maximum_fusion.tre_ref.tim_ref, bf16[256,8192]{1,0:T(8,128)(2,1)} %pad_maximum_fusion.tre_ref.tim_ref), custom_call_target="tpu_custom_call" | custom-call | tf_op jit(solution)/shard_map/pallas_call | solution.py:88
  84.0 2.2 %constant_dynamic-slice_fusion.3 = (f32[1,64,768]{2,1,0:T(8,128)S(1)}, f32[1,64,768]{2,1,0:T(8,128)}, f32[1,64,768]{2,1,0:T(8,128)}, f32[1,64,768]{2,1,0:T(8,128)S(1)}) fusion(f32[4,64,768]{2,1,0:T(8,128)} %bitcast.113, s32[]{:T(128)S(6)} %select_n.105, s32[]{:T(128)S(6)} %select_n.108, s32[]{:T(128)S(6)} %select_n.107, s32[]{:T(128)S(6)} %select_n.106), kind=kLoop, calls=%fused_computation.104 | loop fusion | bytes 1572880 | tf_op jit(solution)/shard_map/jit(dynamic_index_in_dim)/dynamic_slice | solution.py:161
  86.2 1.9 copy.24
  88.1 2.1 %collective-permute-start.2 = (f32[64,768]{0,1:T(8,128)}, f32[64,768]{0,1:T(8,128)}, u32[]{:S(2)}, u32[]{:S(2)}) collective-permute-start(f32[64,768]{0,1:T(8,128)} %bitcast.119), channel_id=1, source_target_pairs={{0,3},{1,2},{2,1},{3,0},{4,7},{5,6},{6,5},{7,4},{8,11},{9,10},{10,... | collective-permute-start | bytes 589832 | tf_op jit(solution)/shard_map/ppermute | solution.py:164
  90.2 1.9 copy.23
  93.7 2.9 %copy.34 = bf16[2,32,48,2,128]{4,3,0,2,1:T(2,128)(2,1)} copy(bf16[2,32,48,2,128]{4,3,2,1,0:T(2,128)(2,1)S(1)} %copy-done.1) | data formatting | bytes 3145728
  96.8 3.3 %collective-permute-done.2 = f32[64,768]{0,1:T(8,128)} collective-permute-done((f32[64,768]{0,1:T(8,128)}, f32[64,768]{0,1:T(8,128)}, u32[]{:S(2)}, u32[]{:S(2)}) %collective-permute-start.2) | collective-permute-done | bytes 196640 | tf_op jit(solution)/shard_map/ppermute | solution.py:164
  100.1 8.6 %collective-permute-done.1 = f32[64,768]{0,1:T(8,128)} collective-permute-done((f32[64,768]{0,1:T(8,128)}, f32[64,768]{0,1:T(8,128)}, u32[]{:S(2)}, u32[]{:S(2)}) %collective-permute-start.1) | collective-permute-done | bytes 196640 | tf_op jit(solution)/shard_map/ppermute | solution.py:164
  108.6 1.3 fusion.23
  111.7 10.1 %all-to-all-start.2 = ((bf16[2,2,1536,128]{3,1,0,2:T(2,128)(2,1)}), bf16[2,2,1536,128]{3,1,0,2:T(2,128)(2,1)S(1)}, u32[]{:S(2)}, u32[]{:S(2)}) async-start(bf16[2,2,1536,128]{3,1,0,2:T(2,128)(2,1)} %bitcast.19), calls=%async_computation.2 | async-start | bytes 3145728 | tf_op jit(solution)/shard_map/all_to_all | solution.py:187
  122.6 1.5 fusion.19
  124.9 1.7 divide_convert_fusion.2.x_ref
  126.6 21.4 %shard_map.29 = f32[256,1152]{1,0:T(8,128)} custom-call(bf16[2,2,48,4096]{3,2,1,0:T(8,128)(2,1)} %divide_convert_fusion.2.x_ref, bf16[2,2,24,4096]{3,2,1,0:T(8,128)(2,1)} %slice.87.y_ref, bf16[256,8192]{1,0:T(8,128)(2,1)} %pad_maximum_fusion.tre_ref.tim_ref, bf16[256,8192]{1,0:T(8,128)(2,1)} %pad_maximum_fusion.tre_ref.tim_ref), custom_call_target="tpu_custom_call" | custom-call | tf_op jit(solution)/shard_map/pallas_call | solution.py:88
  148.0 1.9 %dynamic-slice_bitcast_fusion.4 = (f32[64,1152]{1,0:T(8,128)S(1)}, f32[64,1152]{1,0:T(8,128)}, f32[64,1152]{1,0:T(8,128)S(1)}) fusion(f32[4,64,1152]{2,1,0:T(8,128)} %bitcast.109, s32[]{:T(128)S(6)} %select_n.106, s32[]{:T(128)S(6)} %select_n.108, s32[]{:T(128)S(6)} %select_n.107), kind=kLoop, calls=%fused_computation.56 | loop fusion | bytes 1769484 | tf_op jit(solution)/shard_map/jit(dynamic_index_in_dim)/squeeze | solution.py:163
  149.9 2.2 %collective-permute-start.4 = (f32[64,1152]{1,0:T(8,128)S(1)}, f32[64,1152]{1,0:T(8,128)}, u32[]{:S(2)}, u32[]{:S(2)}) collective-permute-start(f32[64,1152]{1,0:T(8,128)S(1)} %get-tuple-element.21), channel_id=1, source_target_pairs={{0,2},{1,3},{2,0},{3,1},{4,6},{5,7},{6,4},{7,5},{8,10},{9,11},{10,... | collective-permute-start | bytes 884744 | tf_op jit(solution)/shard_map/ppermute | solution.py:164
  152.7 1.5 fusion.14
  155.1 1.6 divide_convert_fusion.1.x_ref
  156.7 21.4 %shard_map.30 = f32[256,1152]{1,0:T(8,128)} custom-call(bf16[2,2,48,4096]{3,2,1,0:T(8,128)(2,1)} %divide_convert_fusion.1.x_ref, bf16[2,2,24,4096]{3,2,1,0:T(8,128)(2,1)} %slice.87.y_ref, bf16[256,8192]{1,0:T(8,128)(2,1)} %pad_maximum_fusion.tre_ref.tim_ref, bf16[256,8192]{1,0:T(8,128)(2,1)} %pad_maximum_fusion.tre_ref.tim_ref), custom_call_target="tpu_custom_call" | custom-call | tf_op jit(solution)/shard_map/pallas_call | solution.py:88
  178.1 1.5 fusion.77
  183.8 3.7 %collective-permute-done.9 = f32[64,576]{1,0:T(8,128)S(1)} collective-permute-done((f32[64,576]{1,0:T(8,128)S(1)}, f32[64,576]{1,0:T(8,128)S(1)}, u32[]{:S(2)}, u32[]{:S(2)}) %collective-permute-start.9) | collective-permute-done | bytes 147488 | tf_op jit(solution)/shard_map/ppermute | solution.py:120
  187.5 3.5 %collective-permute-done.7 = f32[64,576]{1,0:T(8,128)S(1)} collective-permute-done((f32[64,576]{1,0:T(8,128)S(1)}, f32[64,576]{1,0:T(8,128)S(1)}, u32[]{:S(2)}, u32[]{:S(2)}) %collective-permute-start.7) | collective-permute-done | bytes 147488 | tf_op jit(solution)/shard_map/ppermute | solution.py:120
  (72 shorter events, 19.2 us)
Async XLA Ops:
  10.6 40.9 %all-to-all-start = ((bf16[2,2,1792,128]{3,1,0,2:T(2,128)(2,1)}), bf16[2,2,1792,128]{3,1,0,2:T(2,128)(2,1)}, u32[]{:S(2)}, u32[]{:S(2)}) async-start(bf16[2,2,1792,128]{3,1,0,2:T(2,128)(2,1)} %bitcast.7), calls=%async_computation | async-start | bytes 3670016 | tf_op jit(solution)/shard_map/all_to_all | solution.py:180
  40.8 4.1 %copy-start.2 = (bf16[2,4096,2,128]{3,2,1,0:T(2,128)(2,1)S(1)}, bf16[2,4096,2,128]{3,2,1,0:T(2,128)(2,1)}, u32[]{:S(2)}) copy-start(bf16[2,4096,2,128]{3,2,1,0:T(2,128)(2,1)} %param.2) | copy-start | bytes 12582916
  51.5 13.7 %copy-start.6 = (pred[4096]{0:T(1024)(128)(4,1)}, pred[4096]{0:T(1024)(128)(4,1)S(1)}, u32[]{:S(2)}) copy-start(pred[4096]{0:T(1024)(128)(4,1)S(1)} %fusion.59) | copy-start | bytes 12292
  51.5 13.7 %copy-start.4 = (s32[4096]{0:T(1024)}, s32[4096]{0:T(1024)S(1)}, u32[]{:S(2)}) copy-start(s32[4096]{0:T(1024)S(1)} %get-tuple-element.31) | copy-start | bytes 49156
  53.7 57.4 %all-to-all-start.1 = ((bf16[2,2,1536,128]{3,1,0,2:T(2,128)(2,1)}), bf16[2,2,1536,128]{3,1,0,2:T(2,128)(2,1)S(1)}, u32[]{:S(2)}, u32[]{:S(2)}) async-start(bf16[2,2,1536,128]{3,1,0,2:T(2,128)(2,1)} %bitcast.2), calls=%async_computation.1 | async-start | bytes 3145728 | tf_op jit(solution)/shard_map/all_to_all | solution.py:187
  66.6 1.3 copy-start
  84.0 9.7 %copy-start.1 = (bf16[2,32,48,2,128]{4,3,2,1,0:T(2,128)(2,1)S(1)}, bf16[2,32,48,2,128]{4,3,2,1,0:T(2,128)(2,1)}, u32[]{:S(2)}) copy-start(bf16[2,32,48,2,128]{4,3,2,1,0:T(2,128)(2,1)} %get-tuple-element.18) | copy-start | bytes 4718596
  88.1 12.0 %collective-permute-start.2 = (f32[64,768]{0,1:T(8,128)}, f32[64,768]{0,1:T(8,128)}, u32[]{:S(2)}, u32[]{:S(2)}) collective-permute-start(f32[64,768]{0,1:T(8,128)} %bitcast.119), channel_id=1, source_target_pairs={{0,3},{1,2},{2,1},{3,0},{4,7},{5,6},{6,5},{7,4},{8,11},{9,10},{10,... | collective-permute-start | bytes 589832 | tf_op jit(solution)/shard_map/ppermute | solution.py:164
  92.1 16.6 %collective-permute-start.1 = (f32[64,768]{0,1:T(8,128)}, f32[64,768]{0,1:T(8,128)}, u32[]{:S(2)}, u32[]{:S(2)}) collective-permute-start(f32[64,768]{0,1:T(8,128)} %bitcast.120), channel_id=1, source_target_pairs={{0,2},{1,3},{2,0},{3,1},{4,6},{5,7},{6,4},{7,5},{8,10},{9,11},{10,... | collective-permute-start | bytes 589832 | tf_op jit(solution)/shard_map/ppermute | solution.py:164
  93.7 14.9 %collective-permute-start = (f32[64,768]{0,1:T(8,128)}, f32[64,768]{0,1:T(8,128)}, u32[]{:S(2)}, u32[]{:S(2)}) collective-permute-start(f32[64,768]{0,1:T(8,128)} %bitcast.121), channel_id=1, source_target_pairs={{0,1},{1,0},{2,3},{3,2},{4,5},{5,4},{6,7},{7,6},{8,9},{9,8},{10,11... | collective-permute-start | bytes 589832 | tf_op jit(solution)/shard_map/ppermute | solution.py:164
  111.7 40.4 %all-to-all-start.2 = ((bf16[2,2,1536,128]{3,1,0,2:T(2,128)(2,1)}), bf16[2,2,1536,128]{3,1,0,2:T(2,128)(2,1)S(1)}, u32[]{:S(2)}, u32[]{:S(2)}) async-start(bf16[2,2,1536,128]{3,1,0,2:T(2,128)(2,1)} %bitcast.19), calls=%async_computation.2 | async-start | bytes 3145728 | tf_op jit(solution)/shard_map/all_to_all | solution.py:187
  121.8 0.7 copy-start.5
  121.9 0.7 copy-start.7
  149.9 30.3 %collective-permute-start.5 = (f32[64,1152]{1,0:T(8,128)}, f32[64,1152]{1,0:T(8,128)}, u32[]{:S(2)}, u32[]{:S(2)}) collective-permute-start(f32[64,1152]{1,0:T(8,128)} %get-tuple-element.20), channel_id=1, source_target_pairs={{0,3},{1,2},{2,1},{3,0},{4,7},{5,6},{6,5},{7,4},{8,11},{9,10},{10,... | collective-permute-start | bytes 884744 | tf_op jit(solution)/shard_map/ppermute | solution.py:164
  149.9 30.3 %collective-permute-start.4 = (f32[64,1152]{1,0:T(8,128)S(1)}, f32[64,1152]{1,0:T(8,128)}, u32[]{:S(2)}, u32[]{:S(2)}) collective-permute-start(f32[64,1152]{1,0:T(8,128)S(1)} %get-tuple-element.21), channel_id=1, source_target_pairs={{0,2},{1,3},{2,0},{3,1},{4,6},{5,7},{6,4},{7,5},{8,10},{9,11},{10,... | collective-permute-start | bytes 884744 | tf_op jit(solution)/shard_map/ppermute | solution.py:164
  152.2 28.0 %collective-permute-start.3 = (f32[64,1152]{1,0:T(8,128)S(1)}, f32[64,1152]{1,0:T(8,128)}, u32[]{:S(2)}, u32[]{:S(2)}) collective-permute-start(f32[64,1152]{1,0:T(8,128)S(1)} %get-tuple-element.19), channel_id=1, source_target_pairs={{0,1},{1,0},{2,3},{3,2},{4,5},{5,4},{6,7},{7,6},{8,9},{9,8},{10,11... | collective-permute-start | bytes 884744 | tf_op jit(solution)/shard_map/ppermute | solution.py:164
  179.6 2.4 %collective-permute-start.8 = (f32[2,64,576]{2,1,0:T(8,128)S(1)}, f32[2,64,576]{2,1,0:T(8,128)S(1)}, u32[]{:S(2)}, u32[]{:S(2)}) collective-permute-start(f32[2,64,576]{2,1,0:T(8,128)S(1)} %dynamic-slice_bitcast_fusion), channel_id=1, source_target_pairs={{0,1},{1,0},{2,3},{3,2},{4,5},{5,4},{6,7},{7,6},{8,9},{9,8},{10,11... | collective-permute-start | bytes 884744 | tf_op jit(solution)/shard_map/ppermute | solution.py:116
  181.9 1.7 collective-permute-start.6
  182.1 9.4 %copy-start.3 = (f32[64,3,8,32]{3,2,1,0:T(8,128)S(1)}, f32[64,3,8,32]{3,2,1,0:T(8,128)}, u32[]{:S(2)}) copy-start(f32[64,3,8,32]{3,2,1,0:T(8,128)} %copy.30) | copy-start | bytes 589828
  182.1 5.4 %collective-permute-start.9 = (f32[64,576]{1,0:T(8,128)S(1)}, f32[64,576]{1,0:T(8,128)S(1)}, u32[]{:S(2)}, u32[]{:S(2)}) collective-permute-start(f32[64,576]{1,0:T(8,128)S(1)} %dynamic-slice_bitcast_fusion.5), channel_id=1, source_target_pairs={{0,2},{2,0},{1,3},{3,1},{4,6},{6,4},{5,7},{7,5},{8,10},{10,8},{9,1... | collective-permute-start | bytes 442376 | tf_op jit(solution)/shard_map/ppermute | solution.py:120
  183.7 7.3 %collective-permute-start.7 = (f32[64,576]{1,0:T(8,128)S(1)}, f32[64,576]{1,0:T(8,128)S(1)}, u32[]{:S(2)}, u32[]{:S(2)}) collective-permute-start(f32[64,576]{1,0:T(8,128)S(1)} %dynamic-slice_bitcast_fusion.6), channel_id=1, source_target_pairs={{0,2},{2,0},{1,3},{3,1},{4,6},{6,4},{5,7},{7,5},{8,10},{10,8},{9,1... | collective-permute-start | bytes 442376 | tf_op jit(solution)/shard_map/ppermute | solution.py:120

commit v11 on v9

--- a/solution.py
+++ b/solution.py
@@ -14,7 +14,7 @@
 NSRC = 8
 ROUNDS = 3
 
-CHUNK = 512
+CHUNK = 1024
 ROWS = 16
 
 EPSILON = 1e-05
@@ -70,7 +70,7 @@
             cim_ref[dest, :] = imag.astype(jnp.bfloat16)
         return carry
 
-    lax.fori_loop(0, stations // ROWS, body, 0)
+    lax.fori_loop(0, stations // ROWS, body, 0, unroll=True)
     dims = (((1,), (1,)), ((), ()))
     span = NSRC * stations
     for rnd in range(count_src // NSRC):
@@ -153,6 +153,20 @@
     return chunks.reshape(hours_dev, 2, -1, bins_dev)
 
 
+def reduce_direct(projected):
+    index = lax.axis_index("tm")
+    lags, width = projected.shape
+    parts = lax.axis_size("tm")
+    blocks = projected.reshape(parts, lags // parts, width)
+    total = lax.dynamic_index_in_dim(blocks, index, axis=0, keepdims=False)
+    for mask in range(1, parts):
+        send = lax.dynamic_index_in_dim(blocks, index ^ mask, axis=0, keepdims=False)
+        total = total + lax.ppermute(
+            send, "tm", perm=[(i, i ^ mask) for i in range(parts)]
+        )
+    return total
+
+
 def local(spectra, src_ids):
     hours_dev, stations, _, _ = spectra.shape
     shards = lax.axis_size("sta")
@@ -172,7 +186,7 @@
     row_count = transform.shape[0] // lax.axis_size("tm")
     sources = white_a[:, :, half:half + count_all]
     out_a = cross_project(white_a, sources, transform, half)
-    part_a = reduce_lags(out_a)
+    part_a = reduce_direct(out_a)
     white_b = whiten(joined_b)
     out_b = cross_project(white_b, sources, transform, half)
     cols = out_b.shape[1] // 2

time: 163 us -> 147 us (0.902)
  Pallas kernels: 49.8 us -> 35.6 us
  waiting for transfers between devices: 24.8 us -> 21.1 us
    pallas_call x2, Pallas kernels: 49.8 us -> 35.6 us  [cross_project(): pl.pallas_call(cross_project_kernel, grid=(steps,), in_specs=[pl.BlockSpe...]
    ppermute x0 -> x3, starting transfers between devices: none -> 3.08 us  [reduce_direct(): lax.ppermute(send, 'tm', perm=[(i, i ^ mask) for i in range(parts)])]
    ppermute x3 -> x2, waiting for transfers between devices: 2.58 us -> 0.01 us  [reduce_lags(): got = lax.ppermute(send, 'tm', perm=[(0, 1), (1, 0), (2, 3), (3, 2)])]
    ppermute x3 -> x2, starting transfers between devices: 2.39 us -> 0.51 us  [reduce_lags(): got = lax.ppermute(send, 'tm', perm=[(0, 1), (1, 0), (2, 3), (3, 2)])]
    ppermute x3 -> x2, waiting for transfers between devices: 8.65 us -> 7.53 us  [reduce_lags(): got = lax.ppermute(send, 'tm', perm=[(0, 2), (2, 0), (1, 3), (3, 1)])]
    unnamed x5 -> x13, local copies, waits for them, and re-layouts: 5.86 us -> 6.07 us
  transfers between devices with their start and end apart: 8 -> 9, of which waited for: 5 -> 3; matrix products, arithmetic and copies ran while one was open for 29% -> 33% of each run, Pallas kernels for 31% -> 24%
where the time goes in v11:
time: 147 us; the launch traced here: 146 us
  Pallas kernels  35.6 us (24%)
  other arithmetic  34.3 us (23%)
  local copies, waits for them, and re-layouts  25.5 us (17%)
  starting transfers between devices  22 us (15%)
  waiting for transfers between devices  21.1 us (14%)
  matrix products  7.09 us (5%)
    pallas_call x2, Pallas kernels, cross_project(): pl.pallas_call(cross_project_kernel, grid=(steps,), in_specs=[pl.BlockSpe...  35.6 us
    another operation x1, other arithmetic  18.2 us
    all_to_all x1, waiting for transfers between devices, local(): lax.all_to_all(send_a, 'sta', split_axis=2, concat_axis=3, tiled=True)  13.6 us
    all_to_all x1, starting transfers between devices, local(): lax.all_to_all(send_a, 'sta', split_axis=2, concat_axis=3, tiled=True)  11.4 us
    ppermute x2, waiting for transfers between devices, reduce_lags(): got = lax.ppermute(send, 'tm', perm=[(0, 2), (2, 0), (1, 3), (3, 1)])  7.53 us
    unnamed x13, local copies, waits for them, and re-layouts  6.07 us
    all_to_all x1, starting transfers between devices, local(): lax.all_to_all(send_b, 'sta', split_axis=2, concat_axis=3, tiled=True)  5.41 us
    concatenate x1, other arithmetic, to_send(): chunks = jnp.concatenate([chunks, copies], axis=3)  5.32 us
  transfers between devices with their start and end apart: 9, of which 3 were waited for; matrix products, arithmetic and copies ran while one was open for 33% of the time, Pallas kernels for 24%

profile of v11, /device:TPU:1, one launch (start us, length us, event | category | flops | bytes accessed | tf_op | source)
XLA Modules:
  0.0 146.0 jit_solution(5316173565543495329)
XLA Ops:
  1.6 2.8 %gather_fusion = bf16[24,2,2,128]{3,2,1,0:T(2,128)(2,1)S(1)} fusion(bf16[2,4096,2,128]{3,2,1,0:T(2,128)(2,1)} %param.2, s32[1024]{0:T(1024)S(1)} %pad_clamp_fusion), kind=kCustom, calls=%fused_computation | custom fusion | bytes 49248 | tf_op jit(solution)/shard_map/jit(_take)/gather | solution.py:177
  4.4 3.3 %copy_bitcast_fusion.2 = bf16[2,2,32,64,128]{4,1,0,3,2:T(2,128)(2,1)S(1)} fusion(bf16[2,32,128,2,128]{4,3,2,1,0:T(2,128)(2,1)} %bitcast.84), kind=kLoop, calls=%fused_computation.31 | loop fusion | bytes 4194304 | tf_op jit(solution)/shard_map/transpose | solution.py:147
  8.2 5.3 %pad_maximum_fusion.1 = bf16[2,2,32,88,128]{4,1,0,3,2:T(2,128)(2,1)} fusion(bf16[2,2,32,24,128]{4,1,0,3,2:T(2,128)(2,1)S(1)} %broadcast_in_dim.22, bf16[2,2,32,64,128]{4,1,0,3,2:T(2,128)(2,1)S(1)} %copy_bitcast_fusion.2), kind=kLoop, calls=%fused_computation.24 | loop fusion | flops 1441792 | bytes 5767168 | tf_op jit(solution)/shard_map/concatenate | solution.py:152
  13.5 11.4 %all-to-all-start = ((bf16[2,2,2816,128]{3,1,0,2:T(2,128)(2,1)}), bf16[2,2,2816,128]{3,1,0,2:T(2,128)(2,1)S(1)}, u32[]{:S(2)}, u32[]{:S(2)}) async-start(bf16[2,2,2816,128]{3,1,0,2:T(2,128)(2,1)} %bitcast.79), calls=%async_computation | async-start | bytes 5767168 | tf_op jit(solution)/shard_map/all_to_all | solution.py:179
  24.9 18.2 %multiply_convert_fusion.1 = (bf16[256,4096]{1,0:T(8,128)(2,1)S(1)}, bf16[256,4096]{1,0:T(8,128)(2,1)S(1)}) fusion(s32[256]{0:T(256)S(1)} %iota_add_fusion), kind=kLoop, calls=%fused_computation.13 | loop fusion | flops 19922944 | bytes 4195328 | tf_op jit(solution)/shard_map/convert.3
  43.1 2.6 %pad_maximum_fusion.tre_ref.tim_ref = bf16[256,8192]{1,0:T(8,128)(2,1)} fusion(bf16[256,4096]{1,0:T(8,128)(2,1)S(1)} %get-tuple-element.19, bf16[256,4096]{1,0:T(8,128)(2,1)S(1)} %get-tuple-element.18), kind=kLoop, calls=%fused_computation.9 | loop fusion | flops 8388608 | bytes 8388608 | tf_op jit(solution)/shard_map/concatenate | solution.py:29
  45.7 1.1 copy-done.1
  46.8 1.8 %slice.60 = bf16[2,32,64,2,128]{4,3,2,1,0:T(2,128)(2,1)S(1)} slice(bf16[2,32,128,2,128]{4,3,2,1,0:T(2,128)(2,1)S(1)} %bitcast.85), slice={[0:2], [0:32], [64:128], [0:2], [0:128]} | slice | bytes 4194304 | tf_op jit(solution)/shard_map/slice | solution.py:147
  48.6 3.1 %copy.17 = bf16[2,32,64,2,128]{4,3,0,2,1:T(2,128)(2,1)} copy(bf16[2,32,64,2,128]{4,3,2,1,0:T(2,128)(2,1)S(1)} %slice.60) | data formatting | bytes 4194304
  51.8 13.6 %all-to-all-done = bf16[2,2,2816,128]{3,1,0,2:T(2,128)(2,1)S(1)} async-done(((bf16[2,2,2816,128]{3,1,0,2:T(2,128)(2,1)}), bf16[2,2,2816,128]{3,1,0,2:T(2,128)(2,1)S(1)}, u32[]{:S(2)}, u32[]{:S(2)}) %all-to-all-start) | async-done | bytes 2883616 | tf_op jit(solution)/shard_map/all_to_all | solution.py:179
  66.5 5.4 %all-to-all-start.1 = ((bf16[2,2,2048,128]{3,1,0,2:T(2,128)(2,1)}), bf16[2,2,2048,128]{3,1,0,2:T(2,128)(2,1)}, u32[]{:S(2)}, u32[]{:S(2)}) async-start(bf16[2,2,2048,128]{3,1,0,2:T(2,128)(2,1)} %bitcast.81), calls=%async_computation.1 | async-start | bytes 4194304 | tf_op jit(solution)/shard_map/all_to_all | solution.py:184
  72.7 2.8 %fusion.9 = f32[2,88,64]{1,2,0:T(8,128)S(1)} fusion(f32[2,2,88,4096]{3,2,1,0:T(8,128)S(1)} %convert_element_type.34, s32[4096]{0:T(1024)S(1)} %get-tuple-element.20, s32[4096]{0:T(1024)S(1)} %get-tuple-element.21, pred[4096]{0:T(1024)(128)(4,1)S(1)} %fusion.40), kind=kOutput, calls=%fused_computation.22 | convolution fusion | flops 556335104 | bytes 5849088 | tf_op jit(solution)/shard_map/hrf,fb->hrb/dot_general | solution.py:132
  75.6 1.3 fusion.23
  76.9 1.4 divide_convert_fusion.x_ref
  78.3 1.6 %copy-done = bf16[2,2,88,4096]{3,2,1,0:T(8,128)(2,1)} copy-done((bf16[2,2,88,4096]{3,2,1,0:T(8,128)(2,1)}, bf16[2,2,88,4096]{3,2,1,0:T(8,128)(2,1)S(1)}, u32[]{:S(2)}) %copy-start) | copy-done | bytes 2883608
  79.9 0.9 slice.64.y_ref
  80.9 17.8 %shard_map.28 = f32[256,1536]{1,0:T(8,128)} custom-call(bf16[2,2,88,4096]{3,2,1,0:T(8,128)(2,1)} %copy-done, bf16[2,2,24,4096]{3,2,1,0:T(8,128)(2,1)} %slice.64.y_ref, bf16[256,8192]{1,0:T(8,128)(2,1)} %pad_maximum_fusion.tre_ref.tim_ref, bf16[256,8192]{1,0:T(8,128)(2,1)} %pad_maximum_fusion.tre_ref.tim_ref), custom_call_target="tpu_custom_call" | custom-call | tf_op jit(solution)/shard_map/pallas_call | solution.py:88
  98.7 1.3 dynamic-slice_bitcast_fusion.4
  100.0 2.4 %collective-permute-start.2 = (f32[64,1536]{1,0:T(8,128)S(1)}, f32[64,1536]{1,0:T(8,128)S(1)}, u32[]{:S(2)}, u32[]{:S(2)}) collective-permute-start(f32[64,1536]{1,0:T(8,128)S(1)} %get-tuple-element.14), channel_id=1, source_target_pairs={{0,3},{1,2},{2,1},{3,0},{4,7},{5,6},{6,5},{7,4},{8,11},{9,10},{10,... | collective-permute-start | bytes 1179656 | tf_op jit(solution)/shard_map/ppermute | solution.py:164
  103.1 1.9 %copy.14 = bf16[2,2,2048,128]{3,2,1,0:T(8,128)(2,1)S(1)} copy(bf16[2,2,2048,128]{3,1,0,2:T(2,128)(2,1)} %all-to-all-done.1) | data formatting | bytes 4194304 | tf_op jit(solution)/shard_map/all_to_all | solution.py:184
  105.7 1.9 %fusion.14 = f32[2,64,64]{2,1,0:T(8,128)S(1)} fusion(f32[2,2,64,4096]{3,2,1,0:T(8,128)S(1)} %copy_bitcast_fusion, s32[4096]{0:T(1024)S(1)} %get-tuple-element.20, s32[4096]{0:T(1024)S(1)} %copy-done.3, pred[4096]{0:T(1024)(128)(4,1)S(1)} %copy-done.5), kind=kOutput, calls=%fused_computation.29 | convolution fusion | flops 404750336 | bytes 4263936 | tf_op jit(solution)/shard_map/hrf,fb->hrb/dot_general | solution.py:132
  107.6 1.0 fusion.25
  108.6 1.9 %divide_convert_fusion.1.x_ref = bf16[2,2,64,4096]{3,2,1,0:T(8,128)(2,1)} fusion(f32[2,64,4096]{2,1,0:T(8,128)S(1)} %fusion.25, bf16[2,2,32,64,128]{4,3,2,1,0:T(8,128)(2,1)S(1)} %bitcast.78), kind=kLoop, calls=%fused_computation.11 | loop fusion | flops 3145728 | bytes 6291456 | tf_op jit(solution)/shard_map/convert_element_type | solution.py:140
  110.5 17.8 %shard_map.29 = f32[256,1536]{1,0:T(8,128)} custom-call(bf16[2,2,64,4096]{3,2,1,0:T(8,128)(2,1)} %divide_convert_fusion.1.x_ref, bf16[2,2,24,4096]{3,2,1,0:T(8,128)(2,1)} %slice.64.y_ref, bf16[256,8192]{1,0:T(8,128)(2,1)} %pad_maximum_fusion.tre_ref.tim_ref, bf16[256,8192]{1,0:T(8,128)(2,1)} %pad_maximum_fusion.tre_ref.tim_ref), custom_call_target="tpu_custom_call" | custom-call | tf_op jit(solution)/shard_map/pallas_call | solution.py:88
  128.2 1.5 %fusion.52 = (f32[256,768]{1,0:T(8,128)S(1)}, f32[256,768]{1,0:T(8,128)S(1)}) fusion(f32[256,1536]{1,0:T(8,128)} %shard_map.29), kind=kLoop, calls=%fused_computation.90 | loop fusion | bytes 3145728 | tf_op jit(solution)/shard_map/slice | solution.py:194
  131.8 1.2 fusion.18
  133.2 1.0 bitcast_add_fusion
  134.2 0.8 collective-permute-start.6
  135.1 1.0 bitcast_add_fusion.1
  137.0 3.3 %collective-permute-done.6 = f32[64,768]{1,0:T(8,128)S(1)} collective-permute-done((f32[64,768]{1,0:T(8,128)S(1)}, f32[64,768]{1,0:T(8,128)S(1)}, u32[]{:S(2)}, u32[]{:S(2)}) %collective-permute-start.6) | collective-permute-done | bytes 196640 | tf_op jit(solution)/shard_map/ppermute | solution.py:120
  140.3 4.2 %collective-permute-done.4 = f32[64,768]{1,0:T(8,128)S(1)} collective-permute-done((f32[64,768]{1,0:T(8,128)S(1)}, f32[64,768]{1,0:T(8,128)S(1)}, u32[]{:S(2)}, u32[]{:S(2)}) %collective-permute-start.4) | collective-permute-done | bytes 196640 | tf_op jit(solution)/shard_map/ppermute | solution.py:120
  145.0 0.9 copy.16
  (45 shorter events, 9.0 us)
Async XLA Ops:
  13.5 51.8 %all-to-all-start = ((bf16[2,2,2816,128]{3,1,0,2:T(2,128)(2,1)}), bf16[2,2,2816,128]{3,1,0,2:T(2,128)(2,1)S(1)}, u32[]{:S(2)}, u32[]{:S(2)}) async-start(bf16[2,2,2816,128]{3,1,0,2:T(2,128)(2,1)} %bitcast.79), calls=%async_computation | async-start | bytes 5767168 | tf_op jit(solution)/shard_map/all_to_all | solution.py:179
  43.1 3.7 %copy-start.1 = (bf16[2,4096,2,128]{3,2,1,0:T(2,128)(2,1)S(1)}, bf16[2,4096,2,128]{3,2,1,0:T(2,128)(2,1)}, u32[]{:S(2)}) copy-start(bf16[2,4096,2,128]{3,2,1,0:T(2,128)(2,1)} %param.2) | copy-start | bytes 12582916
  51.8 23.8 %copy-start.2 = (s32[4096]{0:T(1024)}, s32[4096]{0:T(1024)S(1)}, u32[]{:S(2)}) copy-start(s32[4096]{0:T(1024)S(1)} %get-tuple-element.21) | copy-start | bytes 49156
  66.5 36.5 %all-to-all-start.1 = ((bf16[2,2,2048,128]{3,1,0,2:T(2,128)(2,1)}), bf16[2,2,2048,128]{3,1,0,2:T(2,128)(2,1)}, u32[]{:S(2)}, u32[]{:S(2)}) async-start(bf16[2,2,2048,128]{3,1,0,2:T(2,128)(2,1)} %bitcast.81), calls=%async_computation.1 | async-start | bytes 4194304 | tf_op jit(solution)/shard_map/all_to_all | solution.py:184
  72.0 3.6 %copy-start.4 = (pred[4096]{0:T(1024)(128)(4,1)}, pred[4096]{0:T(1024)(128)(4,1)S(1)}, u32[]{:S(2)}) copy-start(pred[4096]{0:T(1024)(128)(4,1)S(1)} %fusion.40) | copy-start | bytes 12292
  78.3 1.6 %copy-start = (bf16[2,2,88,4096]{3,2,1,0:T(8,128)(2,1)}, bf16[2,2,88,4096]{3,2,1,0:T(8,128)(2,1)S(1)}, u32[]{:S(2)}) copy-start(bf16[2,2,88,4096]{3,2,1,0:T(8,128)(2,1)S(1)} %divide_convert_fusion.x_ref) | copy-start | bytes 8650756
  100.0 31.8 %collective-permute-start.2 = (f32[64,1536]{1,0:T(8,128)S(1)}, f32[64,1536]{1,0:T(8,128)S(1)}, u32[]{:S(2)}, u32[]{:S(2)}) collective-permute-start(f32[64,1536]{1,0:T(8,128)S(1)} %get-tuple-element.14), channel_id=1, source_target_pairs={{0,3},{1,2},{2,1},{3,0},{4,7},{5,6},{6,5},{7,4},{8,11},{9,10},{10,... | collective-permute-start | bytes 1179656 | tf_op jit(solution)/shard_map/ppermute | solution.py:164
  102.3 29.4 %collective-permute-start.1 = (f32[64,1536]{1,0:T(8,128)S(1)}, f32[64,1536]{1,0:T(8,128)S(1)}, u32[]{:S(2)}, u32[]{:S(2)}) collective-permute-start(f32[64,1536]{1,0:T(8,128)S(1)} %get-tuple-element.15), channel_id=1, source_target_pairs={{0,2},{1,3},{2,0},{3,1},{4,6},{5,7},{6,4},{7,5},{8,10},{9,11},{10,... | collective-permute-start | bytes 1179656 | tf_op jit(solution)/shard_map/ppermute | solution.py:164
  103.1 28.7 %collective-permute-start = (f32[64,1536]{1,0:T(8,128)S(1)}, f32[64,1536]{1,0:T(8,128)}, u32[]{:S(2)}, u32[]{:S(2)}) collective-permute-start(f32[64,1536]{1,0:T(8,128)S(1)} %get-tuple-element.13), channel_id=1, source_target_pairs={{0,1},{1,0},{2,3},{3,2},{4,5},{5,4},{6,7},{7,6},{8,9},{9,8},{10,11... | collective-permute-start | bytes 1179656 | tf_op jit(solution)/shard_map/ppermute | solution.py:164
  104.9 0.7 copy-start.3
  105.0 0.7 copy-start.5
  130.5 2.7 %collective-permute-start.5 = (f32[2,64,768]{2,1,0:T(8,128)}, f32[2,64,768]{2,1,0:T(8,128)}, u32[]{:S(2)}, u32[]{:S(2)}) collective-permute-start(f32[2,64,768]{2,1,0:T(8,128)} %dynamic-slice_bitcast_fusion), channel_id=1, source_target_pairs={{0,1},{1,0},{2,3},{3,2},{4,5},{5,4},{6,7},{7,6},{8,9},{9,8},{10,11... | collective-permute-start | bytes 1179656 | tf_op jit(solution)/shard_map/ppermute | solution.py:116
  131.8 3.3 %collective-permute-start.3 = (f32[2,64,768]{2,1,0:T(8,128)}, f32[2,64,768]{2,1,0:T(8,128)}, u32[]{:S(2)}, u32[]{:S(2)}) collective-permute-start(f32[2,64,768]{2,1,0:T(8,128)} %dynamic-slice_bitcast_fusion.1), channel_id=1, source_target_pairs={{0,1},{1,0},{2,3},{3,2},{4,5},{5,4},{6,7},{7,6},{8,9},{9,8},{10,11... | collective-permute-start | bytes 1179656 | tf_op jit(solution)/shard_map/ppermute | solution.py:116
  134.2 6.0 %collective-permute-start.6 = (f32[64,768]{1,0:T(8,128)S(1)}, f32[64,768]{1,0:T(8,128)S(1)}, u32[]{:S(2)}, u32[]{:S(2)}) collective-permute-start(f32[64,768]{1,0:T(8,128)S(1)} %dynamic-slice_bitcast_fusion.5), channel_id=1, source_target_pairs={{0,2},{2,0},{1,3},{3,1},{4,6},{6,4},{5,7},{7,5},{8,10},{10,8},{9,1... | collective-permute-start | bytes 589832 | tf_op jit(solution)/shard_map/ppermute | solution.py:120
  136.1 8.4 %collective-permute-start.4 = (f32[64,768]{1,0:T(8,128)S(1)}, f32[64,768]{1,0:T(8,128)S(1)}, u32[]{:S(2)}, u32[]{:S(2)}) collective-permute-start(f32[64,768]{1,0:T(8,128)S(1)} %dynamic-slice_bitcast_fusion.6), channel_id=1, source_target_pairs={{0,2},{2,0},{1,3},{3,1},{4,6},{6,4},{5,7},{7,5},{8,10},{10,8},{9,1... | collective-permute-start | bytes 589832 | tf_op jit(solution)/shard_map/ppermute | solution.py:120
